TPU v7x, 256 devices: a whole 4x4x8 slice. The times are simulated.
256 devices in a mesh: row: 8 (over y, core), col: 32 (over z, x).
Axes of the slice: x: 4, y: 4, z: 8, core: 2. Of those that a mesh axis runs over, the one named last changes fastest.
Arguments:
- blocks: float32 [128, 32, 256, 256], P('row', 'col'), may hold values from -6 to 6
- panel_rows: int32 [2, 64], P(None, 'row'), may hold values from -1 to 767, as said below
- target_slots: int32 [2, 128, 32], P(None, 'row', 'col'), may hold values from -1 to 7, as said below
- diag_inverse: float32 [2, 256, 256], replicated, may hold values from -1 to 1, as said below
- cross_block: float32 [256, 256], replicated, may hold values from -6 to 6
Outputs:
- factored: float32 [128, 32, 256, 256], P('row', 'col')
Inputs may be any that keep to these rules, and one draw needn't show every extreme that they name: `panel_rows`: slot q * 2 + m of row device r stands for the m-th structure row of block column class r + q times the number of row devices; both lists are -1 where that class is 0 or 1, and list 0 is -1 also where block column 0 lacks the row; otherwise list 0 equals list 1. `target_slots`: A filled slot of class c names in entry 0 a slot of its own row device and in entry 1 a slot of row device c modulo the number of row devices, within (c // number of row devices) * 2 and the 1 after it; both are filled or both -1, always -1 in classes 0 and 1; the target's block row number is at least its block column number. `diag_inverse`: each matrix is lower triangular.
All inputs are finite; a program needn't handle non-finite values.
Results may differ from a plain program's by a relative error of at most 0.0003.
Values sent between devices are 32-bit elements; how exact they have to be, the bound alone decides.
No kernel may reach another device: no remote copies, remote signals or barrier semaphores. Data moves between devices by JAX's collectives and lax.ppermute only.
A program may use at most 128 MiB of HBM per device.

v0:
```python
import jax
import jax.numpy as jnp
from jax import lax
from jax.sharding import PartitionSpec as P

PER_CLASS = 2


HIGHEST_PRECISION = lax.Precision.HIGHEST


def broadcast(array, axis, root):
    mine = lax.axis_index(axis) == root
    return lax.psum(jnp.where(mine, array, jnp.zeros_like(array)), axis)


def apply_inverse(panel_blocks, inverse):
    return jnp.einsum("sab,cb->sac", panel_blocks, inverse, precision=HIGHEST_PRECISION)


def per_device(blocks, panel_rows, target_slots, diag_inverse, cross_block):
    column = lax.axis_index("col")
    row_count = lax.axis_size("row")
    stored = blocks[:, 0]
    slot_count = panel_rows.shape[1]
    head_part = stored[:slot_count]
    first_live = (panel_rows[0] >= 0)[:, None, None]
    second_live = (panel_rows[1] >= 0)[:, None, None]
    cross_factor = jnp.dot(cross_block, diag_inverse[0].T, precision=HIGHEST_PRECISION)
    blank_part = jnp.zeros_like(head_part)
    class_start = column // row_count * PER_CLASS
    owner_row = column % row_count
    first_factor = lax.cond(
        column == 0,
        lambda: jnp.where(first_live, apply_inverse(head_part, diag_inverse[0]), 0.0),
        lambda: blank_part,
    )
    first_rows = broadcast(first_factor, "col", 0)
    first_cols = broadcast(
        lax.dynamic_slice_in_dim(first_rows, class_start, PER_CLASS, 0), "row", owner_row
    )
    second_factor = lax.cond(
        column == 1,
        lambda: jnp.where(
            second_live,
            apply_inverse(head_part - apply_inverse(first_rows, cross_factor), diag_inverse[1]),
            0.0,
        ),
        lambda: blank_part,
    )
    second_rows = broadcast(second_factor, "col", 1)
    second_cols = broadcast(
        lax.dynamic_slice_in_dim(second_rows, class_start, PER_CLASS, 0), "row", owner_row
    )
    row_index = target_slots[0, :, 0]
    col_index = target_slots[1, :, 0]
    present = row_index >= 0
    left_slot = jnp.where(present, row_index, 0)
    right_slot = jnp.where(present, col_index - class_start, 0)
    left_blocks = jnp.concatenate([first_rows[left_slot], second_rows[left_slot]], axis=2)
    right_blocks = jnp.concatenate([first_cols[right_slot], second_cols[right_slot]], axis=2)
    schur_term = jnp.einsum("sak,sbk->sab", left_blocks, right_blocks, precision=HIGHEST_PRECISION)
    trailing = stored - jnp.where(present[:, None, None], schur_term, 0.0)
    own_panel = jnp.where(column == 0, first_factor, second_factor)
    keep_mask = (column == 0) & first_live | (column == 1) & second_live
    head_blocks = jnp.where(keep_mask, own_panel, trailing[:slot_count])
    factored = jnp.concatenate([head_blocks, trailing[slot_count:]], axis=0)
    return factored[:, None]


def solution(mesh):
    return jax.shard_map(
        per_device,
        mesh=mesh,
        in_specs=(P("row", "col", None, None), P(None, "row"), P(None, "row", "col"), P(), P()),
        out_specs=P("row", "col", None, None),
        check_vma=False,
    )
```

profile of v0, /device:TPU:1, one launch (start us, length us, event | category | flops | bytes accessed | tf_op | source)
XLA Modules:
  0.0 430.2 jit_solution(9175127619029981087)
XLA Ops:
  6.5 0.0 copy-start
  6.5 0.0 all-reduce.5.cloned.1.call-start
  6.5 0.0 copy-start.9
  6.5 0.0 copy-start.8
  6.5 3.1 slice_bitcast_fusion
  9.7 0.0 copy-done.9
  9.7 0.0 copy-done.8
  9.7 3.4 conditional.2
  9.7 3.4 convolution_select_fusion
  13.1 0.0 copy-start.3
  13.2 1.8 broadcast_select_fusion.1
  15.0 0.3 copy-done.3
  15.2 0.0 all-reduce.5.cloned.1.call-update
  15.2 0.0 all-reduce.7.cloned.1.call-start
  15.3 0.0 copy-done
  15.3 0.4 fusion.22
  15.7 150.0 %all-reduce.5.cloned.1.call-done = f32[8,256,256]{2,1,0:T(8,128)} async-done(((f32[8,256,256]{2,1,0:T(8,128)}), f32[8,256,256]{2,1,0:T(8,128)}) %all-reduce.5.cloned.1.call-update) | async-done | bytes 2097168 | tf_op jit(solution)/shard_map/psum | solution.py:14
  165.7 0.2 conditional.3
  165.7 0.2 broadcast.124
  165.9 0.0 copy-start.5
  165.9 1.3 copy-done.5
  167.2 1.5 broadcast_select_fusion
  168.8 0.0 copy-start.2
  168.8 0.0 all-reduce.7.cloned.1.call-update
  168.8 0.0 copy-start.10
  168.8 0.2 all-reduce.9.cloned.1.call-start
  169.1 1.3 copy-done.2
  170.4 0.8 dynamic-slice_select_fusion.1
  171.2 150.5 %all-reduce.7.cloned.1.call-done = f32[8,256,256]{2,1,0:T(8,128)} async-done(((f32[8,256,256]{2,1,0:T(8,128)}), f32[8,256,256]{2,1,0:T(8,128)}) %all-reduce.7.cloned.1.call-update) | async-done | bytes 2097168 | tf_op jit(solution)/shard_map/psum | solution.py:14
  321.7 1.9 dynamic-slice_select_fusion
  323.6 0.0 all-reduce.9.cloned.1.call-update
  323.6 0.0 copy-done.10
  323.6 2.8 gather_fusion
  326.5 4.3 %gather_fusion.1 = f32[16,256,256]{2,1,0:T(8,128)} fusion(f32[8,256,256]{2,1,0:T(8,128)} %all-reduce.7.cloned.1.call-done, s32[1024]{0:T(1024)S(1)} %get-tuple-element.51), kind=kCustom, calls=%fused_computation.1 | custom fusion | bytes 8388672 | tf_op jit(solution)/shard_map/gather | solution.py:60
  330.8 60.6 %all-reduce.9.cloned.1.call-done = (f32[2,256,256]{2,1,0:T(8,128)}, f32[2,256,256]{2,1,0:T(8,128)}) async-done(((f32[2,256,256]{2,1,0:T(8,128)}, f32[2,256,256]{2,1,0:T(8,128)}), (f32[2,256,256]{2,1,0:T(8,128)}, f32[2,256,256]{2,1,0:T(8,128)})) %all-reduce.9.cloned.1.call-update) | async-done | bytes 1048592 | tf_op jit(solution)/shard_map/psum | solution.py:14
  391.4 0.0 copy-start.1
  391.4 3.9 gather_fusion.3
  395.3 0.0 copy-done.1
  395.4 2.8 gather_fusion.2
  398.1 0.0 copy-start.4
  398.1 0.0 copy-start.6
  398.1 22.5 %bitcast_subtract_fusion = f32[16,256,256]{2,1,0:T(8,128)S(1)} fusion(f32[16,1,256,256]{3,2,1,0:T(8,128)} %param.9, pred[16]{0:T(512)(128)(4,1)S(1)} %compare_bitcast_fusion.1, f32[16,256,256]{2,1,0:T(8,128)} %gather_fusion.3, f32[16,256,256]{2,1,0:T(8,128)} %gather_fusion.2, f32[16,256,256]{2,1,0:T(8,128)} %gather_fusion.1, f32[16,256,256]{2,1,0:T(8,128)} %gather_fusion), kind=kOutput, calls=%fused_computation.23 | convolution fusion | flops 6448742400 | bytes 25165840 | tf_op jit(solution)/shard_map/sak,sbk->sab/dot_general | solution.py:62
  420.6 0.0 copy-done.4
  420.6 0.0 copy-done.6
  420.6 0.6 slice_select_fusion
  421.2 2.4 maximum_bitcast_fusion
  (5 shorter events, 0.0 us)
Async XLA Ops:
  6.5 8.8 %copy-start = (f32[256,256]{1,0:T(8,128)S(1)}, f32[256,256]{1,0:T(8,128)}, u32[]{:S(2)}) copy-start(f32[256,256]{1,0:T(8,128)} %param.13) | copy-start | bytes 786436
  6.5 159.2 %all-reduce.5.cloned.1.call-start = ((), (), s32[]{:S(2)}) async-start(), calls=%async_computation | async-start | bytes 4194304 | tf_op jit(solution)/shard_map/psum | solution.py:14
  6.5 3.1 copy-start.9
  6.5 3.1 copy-start.8
  13.1 2.1 copy-start.3
  15.2 306.5 %all-reduce.7.cloned.1.call-start = ((), (), s32[]{:S(2)}) async-start(), calls=%async_computation.1 | async-start | bytes 4194304 | tf_op jit(solution)/shard_map/psum | solution.py:14
  165.9 1.3 copy-start.5
  168.8 1.6 copy-start.2
  168.8 154.8 %copy-start.10 = (s32[2,16,1]{1,2,0:T(1,128)S(1)}, s32[2,16,1]{1,2,0:T(1,128)}, u32[]{:S(2)}) copy-start(s32[2,16,1]{1,2,0:T(1,128)} %param.11) | copy-start | bytes 388
  168.8 222.6 %all-reduce.9.cloned.1.call-start = ((), (), s32[]{:S(2)}) async-start(), calls=%async_computation.2 | async-start | bytes 2097152 | tf_op jit(solution)/shard_map/psum | solution.py:14
  391.4 3.9 copy-start.1
  398.1 22.5 %copy-start.4 = (f32[8,256,256]{2,1,0:T(8,128)S(1)}, f32[8,256,256]{2,1,0:T(8,128)}, u32[]{:S(2)}) copy-start(f32[8,256,256]{2,1,0:T(8,128)} %copy-done.3) | copy-start | bytes 6291460
  398.1 22.5 %copy-start.6 = (f32[8,256,256]{2,1,0:T(8,128)S(1)}, f32[8,256,256]{2,1,0:T(8,128)}, u32[]{:S(2)}) copy-start(f32[8,256,256]{2,1,0:T(8,128)} %copy-done.5) | copy-start | bytes 6291460
Sparse Core Ops, SparseCore 0:
  15.4 150.3 all-reduce.4
  169.7 151.9 all-reduce.6
  324.1 67.2 all-reduce.8
where the time goes:
time: 432 us; the launch traced here: 430 us
  waiting for transfers between devices  361 us (84%)
  matrix products  26.3 us (6%)
  local copies, waits for them, and re-layouts  20 us (5%)
  between operations  13.3 us (3%)
  other arithmetic  9.07 us (2%)
    psum x3, waiting for transfers between devices, broadcast(): return lax.psum(jnp.where(mine, array, jnp.zeros_like(array)), axis)  361 us
    dot_general x1, matrix products, per_device(): jnp.einsum('sak,sbk->sab', left_blocks, right_blocks, precision=HIGHEST_P...  22.5 us
  transfers between devices with their start and end apart: 3, of which 3 were waited for; matrix products, arithmetic and copies ran while one was open for 2% of the time, Pallas kernels for 0%

commit v1 on v0

v1 whole, which is shorter than its diff:
```python
import jax
import jax.numpy as jnp
from jax import lax
from jax.sharding import PartitionSpec as P

PER_CLASS = 2


HIGHEST_PRECISION = lax.Precision.HIGHEST


def broadcast(array, axis, root):
    mine = lax.axis_index(axis) == root
    return lax.psum(jnp.where(mine, array, jnp.zeros_like(array)), axis)


def apply_inverse(panel_rows_block, inverse):
    return jnp.einsum("ab,cb->ac", panel_rows_block, inverse, precision=HIGHEST_PRECISION)


def per_device(blocks, panel_rows, target_slots, diag_inverse, cross_block):
    column = lax.axis_index("col")
    row_count = lax.axis_size("row")
    col_count = lax.axis_size("col")
    stored = blocks[:, 0]
    slot_count = panel_rows.shape[1]
    block = stored.shape[-1]
    head_part = stored[:slot_count]
    chunk = slot_count * block // col_count
    pieces = head_part.reshape(col_count, chunk, block)
    received = lax.all_to_all(pieces, "col", 0, 0, tiled=True)
    zero_rows = received[0]
    one_rows = received[1]
    piece_slot = column * chunk // block
    first_live = lax.dynamic_index_in_dim(panel_rows[0], piece_slot, keepdims=False) >= 0
    second_live = lax.dynamic_index_in_dim(panel_rows[1], piece_slot, keepdims=False) >= 0
    cross_factor = jnp.dot(cross_block, diag_inverse[0].T, precision=HIGHEST_PRECISION)
    first_piece = jnp.where(first_live, apply_inverse(zero_rows, diag_inverse[0]), 0.0)
    updated_piece = one_rows - apply_inverse(first_piece, cross_factor)
    second_piece = jnp.where(second_live, apply_inverse(updated_piece, diag_inverse[1]), 0.0)
    both_pieces = jnp.stack([first_piece, second_piece])
    both_rows = lax.all_gather(both_pieces, "col", axis=1, tiled=True)
    both_rows = both_rows.reshape(2, slot_count, block, block)
    first_rows = both_rows[0]
    second_rows = both_rows[1]
    class_start = column // row_count * PER_CLASS
    owner_row = column % row_count
    both_cols = broadcast(
        lax.dynamic_slice_in_dim(both_rows, class_start, PER_CLASS, 1), "row", owner_row
    )
    first_cols = both_cols[0]
    second_cols = both_cols[1]
    row_index = target_slots[0, :, 0]
    col_index = target_slots[1, :, 0]
    present = row_index >= 0
    left_slot = jnp.where(present, row_index, 0)
    right_slot = jnp.where(present, col_index - class_start, 0)
    left_blocks = jnp.concatenate([first_rows[left_slot], second_rows[left_slot]], axis=2)
    right_blocks = jnp.concatenate([first_cols[right_slot], second_cols[right_slot]], axis=2)
    schur_term = jnp.einsum("sak,sbk->sab", left_blocks, right_blocks, precision=HIGHEST_PRECISION)
    trailing = stored - jnp.where(present[:, None, None], schur_term, 0.0)
    head_live = panel_rows >= 0
    keep_mask = ((column == 0) & head_live[0] | (column == 1) & head_live[1])[:, None, None]
    own_panel = jnp.where(column == 0, first_rows, second_rows)
    head_blocks = jnp.where(keep_mask, own_panel, trailing[:slot_count])
    factored = jnp.concatenate([head_blocks, trailing[slot_count:]], axis=0)
    return factored[:, None]


def solution(mesh):
    return jax.shard_map(
        per_device,
        mesh=mesh,
        in_specs=(P("row", "col", None, None), P(None, "row"), P(None, "row", "col"), P(), P()),
        out_specs=P("row", "col", None, None),
        check_vma=False,
    )
```

time: 432 us -> 261 us (0.60)
  waiting for transfers between devices: 361 us -> 181 us
  starting transfers between devices: 0.27 us -> 12.1 us
    psum x3 -> x1, waiting for transfers between devices: 361 us -> 54.8 us  [broadcast(): return lax.psum(jnp.where(mine, array, jnp.zeros_like(array)), axis)]
    all_gather x0 -> x1, waiting for transfers between devices: none -> 78.6 us  [per_device(): both_rows = lax.all_gather(both_pieces, 'col', axis=1, tiled=True)]
    all_to_all x0 -> x1, waiting for transfers between devices: none -> 47.3 us  [per_device(): received = lax.all_to_all(pieces, 'col', 0, 0, tiled=True)]
    all_to_all x0 -> x1, starting transfers between devices: none -> 12 us  [per_device(): received = lax.all_to_all(pieces, 'col', 0, 0, tiled=True)]
  transfers between devices with their start and end apart: 3 -> 3, of which waited for: 3 -> 3; matrix products, arithmetic and copies ran while one was open for 2% -> 5% of each run, Pallas kernels for 0% -> 0%
where the time goes in v1:
time: 261 us; the launch traced here: 259 us
  waiting for transfers between devices  181 us (69%)
  matrix products  25.2 us (10%)
  local copies, waits for them, and re-layouts  21 us (8%)
  between operations  13.6 us (5%)
  starting transfers between devices  12.1 us (5%)
  other arithmetic  6.69 us (3%)
    all_gather x1, waiting for transfers between devices, per_device(): both_rows = lax.all_gather(both_pieces, 'col', axis=1, tiled=True)  78.6 us
    psum x1, waiting for transfers between devices, broadcast(): return lax.psum(jnp.where(mine, array, jnp.zeros_like(array)), axis)  54.8 us
    all_to_all x1, waiting for transfers between devices, per_device(): received = lax.all_to_all(pieces, 'col', 0, 0, tiled=True)  47.3 us
    dot_general x1, matrix products, per_device(): jnp.einsum('sak,sbk->sab', left_blocks, right_blocks, precision=HIGHEST_P...  22.4 us
    all_to_all x1, starting transfers between devices, per_device(): received = lax.all_to_all(pieces, 'col', 0, 0, tiled=True)  12 us
  transfers between devices with their start and end apart: 3, of which 3 were waited for; matrix products, arithmetic and copies ran while one was open for 5% of the time, Pallas kernels for 0%

profile of v1, /device:TPU:1, one launch (start us, length us, event | category | flops | bytes accessed | tf_op | source)
XLA Modules:
  0.0 259.2 jit_solution(12338296099703063530)
XLA Ops:
  6.5 0.0 copy-start
  6.5 0.0 copy-start.4
  6.5 0.0 copy-start.2
  6.5 3.1 %slice.58 = f32[8,1,256,256]{3,2,1,0:T(8,128)} slice(f32[16,1,256,256]{3,2,1,0:T(8,128)} %param.5), slice={[0:8], [0:1], [0:256], [0:256]} | slice | bytes 4194304 | tf_op jit(solution)/shard_map/slice | solution.py:28
  9.7 0.0 copy-start.3
  9.7 12.0 %all-to-all-start = ((f32[32,64,256]{2,1,0:T(8,128)}), f32[32,64,256]{2,1,0:T(8,128)S(1)}, u32[]{:S(2)}, u32[]{:S(2)}) async-start(f32[32,64,256]{2,1,0:T(8,128)} %bitcast.2), calls=%async_computation | async-start | bytes 4194304 | tf_op jit(solution)/shard_map/all_to_all | solution.py:31
  21.7 0.0 all-gather.2.cloned.1.call-start
  21.7 0.0 copy-done.4
  21.8 0.7 fusion.24
  22.4 0.0 copy-done
  22.4 0.0 copy-done.2
  22.4 0.4 fusion.13
  22.9 47.3 %all-to-all-done = f32[32,64,256]{2,1,0:T(8,128)S(1)} async-done(((f32[32,64,256]{2,1,0:T(8,128)}), f32[32,64,256]{2,1,0:T(8,128)S(1)}, u32[]{:S(2)}, u32[]{:S(2)}) %all-to-all-start) | async-done | bytes 2097184 | tf_op jit(solution)/shard_map/all_to_all | solution.py:31
  70.1 0.9 convolution_select_fusion.1
  71.1 0.4 convolution_subtract_fusion
  71.4 1.1 fusion.7
  72.5 0.7 pad_maximum_fusion
  73.2 0.0 all-gather.2.cloned.1.call-update
  73.2 0.0 all-reduce.2.cloned.1.call-start
  73.3 0.0 copy-done.3
  73.3 78.6 %all-gather.2.cloned.1.call-done = f32[2,2048,256]{2,1,0:T(8,128)} async-done(((f32[2,64,256]{2,1,0:T(8,128)}), f32[2,2048,256]{2,1,0:T(8,128)}) %all-gather.2.cloned.1.call-update) | async-done | bytes 4194320 | tf_op jit(solution)/shard_map/all_gather | solution.py:42
  152.0 2.3 dynamic-slice_select_fusion
  154.2 0.0 all-reduce.2.cloned.1.call-update
  154.3 3.8 %fusion.22 = (f32[1,2048,256]{2,1,0:T(8,128)S(1)}, f32[1,2048,256]{2,1,0:T(8,128)}) fusion(f32[2,2048,256]{2,1,0:T(8,128)} %all-gather.2.cloned.1.call-done), kind=kLoop, calls=%fused_computation.45 | loop fusion | bytes 8388608 | tf_op jit(solution)/shard_map/slice | solution.py:44
  158.1 2.8 %gather_fusion = f32[16,256,256]{2,1,0:T(8,128)} fusion(f32[8,256,256]{2,1,0:T(8,128)S(1)} %bitcast.55, s32[1024]{0:T(1024)S(1)} %get-tuple-element.18), kind=kCustom, calls=%fused_computation | custom fusion | bytes 8388672 | tf_op jit(solution)/shard_map/gather | solution.py:58
  160.9 4.4 %gather_fusion.1 = f32[16,256,256]{2,1,0:T(8,128)} fusion(f32[8,256,256]{2,1,0:T(8,128)} %bitcast.57, s32[1024]{0:T(1024)S(1)} %get-tuple-element.18), kind=kCustom, calls=%fused_computation.1 | custom fusion | bytes 8388672 | tf_op jit(solution)/shard_map/gather | solution.py:58
  165.3 54.8 %all-reduce.2.cloned.1.call-done = f32[2,2,256,256]{3,2,1,0:T(8,128)} async-done(((f32[2,2,256,256]{3,2,1,0:T(8,128)}), f32[2,2,256,256]{3,2,1,0:T(8,128)}) %all-reduce.2.cloned.1.call-update) | async-done | bytes 1048592 | tf_op jit(solution)/shard_map/psum | solution.py:14
  220.0 1.3 slice_bitcast_fusion.1
  221.3 2.8 %gather_fusion.2 = f32[16,256,256]{2,1,0:T(8,128)} fusion(f32[2,256,256]{2,1,0:T(8,128)S(1)} %get-tuple-element.9, s32[1024]{0:T(1024)S(1)} %get-tuple-element.17), kind=kCustom, calls=%fused_computation.2 | custom fusion | bytes 8388672 | tf_op jit(solution)/shard_map/gather | solution.py:59
  224.1 2.8 %gather_fusion.3 = f32[16,256,256]{2,1,0:T(8,128)} fusion(f32[2,256,256]{2,1,0:T(8,128)S(1)} %get-tuple-element.10, s32[1024]{0:T(1024)S(1)} %get-tuple-element.17), kind=kCustom, calls=%fused_computation.3 | custom fusion | bytes 8388672 | tf_op jit(solution)/shard_map/gather | solution.py:59
  226.9 0.0 copy-start.1
  226.9 22.4 %bitcast_subtract_fusion = f32[16,256,256]{2,1,0:T(8,128)S(1)} fusion(f32[16,1,256,256]{3,2,1,0:T(8,128)} %param.5, pred[16]{0:T(512)(128)(4,1)S(1)} %compare_bitcast_fusion, f32[16,256,256]{2,1,0:T(8,128)} %gather_fusion.3, f32[16,256,256]{2,1,0:T(8,128)} %gather_fusion.2, f32[16,256,256]{2,1,0:T(8,128)} %gather_fusion.1, f32[16,256,256]{2,1,0:T(8,128)} %gather_fusion), kind=kOutput, calls=%fused_computation.12 | convolution fusion | flops 6448742400 | bytes 25165840 | tf_op jit(solution)/shard_map/sak,sbk->sab/dot_general | solution.py:60
  249.4 0.0 copy-done.1
  249.4 0.6 slice_select_fusion
  250.0 2.4 maximum_bitcast_fusion
  (6 shorter events, 0.0 us)
Async XLA Ops:
  6.5 15.9 %copy-start = (f32[256,256]{1,0:T(8,128)S(1)}, f32[256,256]{1,0:T(8,128)}, u32[]{:S(2)}) copy-start(f32[256,256]{1,0:T(8,128)} %param.9) | copy-start | bytes 786436
  6.5 15.2 %copy-start.4 = (s32[2,8]{1,0:T(2,128)S(1)}, s32[2,8]{1,0:T(2,128)}, u32[]{:S(2)}) copy-start(s32[2,8]{1,0:T(2,128)} %param.6) | copy-start | bytes 196
  6.5 15.9 %copy-start.2 = (f32[2,256,256]{2,1,0:T(8,128)S(1)}, f32[2,256,256]{2,1,0:T(8,128)}, u32[]{:S(2)}) copy-start(f32[2,256,256]{2,1,0:T(8,128)} %param.8) | copy-start | bytes 1572868
  9.7 63.6 %copy-start.3 = (s32[2,16,1]{1,2,0:T(1,128)S(1)}, s32[2,16,1]{1,2,0:T(1,128)}, u32[]{:S(2)}) copy-start(s32[2,16,1]{1,2,0:T(1,128)} %param.7) | copy-start | bytes 388
  9.7 60.5 %all-to-all-start = ((f32[32,64,256]{2,1,0:T(8,128)}), f32[32,64,256]{2,1,0:T(8,128)S(1)}, u32[]{:S(2)}, u32[]{:S(2)}) async-start(f32[32,64,256]{2,1,0:T(8,128)} %bitcast.2), calls=%async_computation | async-start | bytes 4194304 | tf_op jit(solution)/shard_map/all_to_all | solution.py:31
  21.7 130.3 %all-gather.2.cloned.1.call-start = ((), (), s32[]{:S(2)}) async-start(), calls=%async_computation.1 | async-start | bytes 4325376 | tf_op jit(solution)/shard_map/all_gather | solution.py:42
  73.2 146.8 %all-reduce.2.cloned.1.call-start = ((), (), s32[]{:S(2)}) async-start(), calls=%async_computation.2 | async-start | bytes 2097152 | tf_op jit(solution)/shard_map/psum | solution.py:14
  226.9 22.5 %copy-start.1 = (f32[1,2048,256]{2,1,0:T(8,128)S(1)}, f32[1,2048,256]{2,1,0:T(8,128)}, u32[]{:S(2)}) copy-start(f32[1,2048,256]{2,1,0:T(8,128)} %get-tuple-element.8) | copy-start | bytes 6291460
Sparse Core Ops, SparseCore 0:
  73.3 78.6 all-gather.1
  154.4 65.5 all-reduce.1

commit v2 on v1

--- a/solution.py
+++ b/solution.py
@@ -1,17 +1,17 @@
 import jax
 import jax.numpy as jnp
+import numpy as np
 from jax import lax
+from jax.sharding import Mesh
 from jax.sharding import PartitionSpec as P
 
 PER_CLASS = 2
+X_SIZE = 4
 
 
 HIGHEST_PRECISION = lax.Precision.HIGHEST
-
-
-def broadcast(array, axis, root):
-    mine = lax.axis_index(axis) == root
-    return lax.psum(jnp.where(mine, array, jnp.zeros_like(array)), axis)
+COL_AXES = ("zh", "zl", "x")
+CLASS_AXES = ("zl", "x")
 
 
 def apply_inverse(panel_rows_block, inverse):
@@ -19,16 +19,16 @@
 
 
 def per_device(blocks, panel_rows, target_slots, diag_inverse, cross_block):
-    column = lax.axis_index("col")
     row_count = lax.axis_size("row")
-    col_count = lax.axis_size("col")
+    col_count = lax.axis_size(COL_AXES)
+    column = lax.axis_index(COL_AXES)
     stored = blocks[:, 0]
     slot_count = panel_rows.shape[1]
     block = stored.shape[-1]
     head_part = stored[:slot_count]
     chunk = slot_count * block // col_count
     pieces = head_part.reshape(col_count, chunk, block)
-    received = lax.all_to_all(pieces, "col", 0, 0, tiled=True)
+    received = lax.all_to_all(pieces, COL_AXES, 0, 0, tiled=True)
     zero_rows = received[0]
     one_rows = received[1]
     piece_slot = column * chunk // block
@@ -39,17 +39,21 @@
     updated_piece = one_rows - apply_inverse(first_piece, cross_factor)
     second_piece = jnp.where(second_live, apply_inverse(updated_piece, diag_inverse[1]), 0.0)
     both_pieces = jnp.stack([first_piece, second_piece])
-    both_rows = lax.all_gather(both_pieces, "col", axis=1, tiled=True)
+    class_size = lax.axis_size(CLASS_AXES)
+    swap = [(a * class_size + b, b * class_size + a) for a in range(row_count) for b in range(class_size)]
+    swapped = lax.ppermute(both_pieces, ("row",) + CLASS_AXES, swap)
+    class_pieces = lax.all_gather(swapped, "row", axis=0, tiled=False)
+    per_slot = block // chunk
+    class_pieces = class_pieces.reshape(PER_CLASS, per_slot, 2, chunk, block)
+    both_cols = class_pieces.transpose(2, 0, 1, 3, 4).reshape(2, PER_CLASS, block, block)
+    both_rows = lax.all_gather(both_pieces, "x", axis=1, tiled=True)
+    both_rows = lax.all_gather(both_rows, ("zh", "zl"), axis=1, tiled=True)
     both_rows = both_rows.reshape(2, slot_count, block, block)
     first_rows = both_rows[0]
     second_rows = both_rows[1]
-    class_start = column // row_count * PER_CLASS
-    owner_row = column % row_count
-    both_cols = broadcast(
-        lax.dynamic_slice_in_dim(both_rows, class_start, PER_CLASS, 1), "row", owner_row
-    )
     first_cols = both_cols[0]
     second_cols = both_cols[1]
+    class_start = column // row_count * PER_CLASS
     row_index = target_slots[0, :, 0]
     col_index = target_slots[1, :, 0]
     present = row_index >= 0
@@ -68,10 +72,22 @@
 
 
 def solution(mesh):
+    row_count = mesh.shape["row"]
+    col_count = mesh.shape["col"]
+    devices = np.asarray(mesh.devices).reshape(
+        row_count, col_count // row_count, row_count // X_SIZE, X_SIZE
+    )
+    split_mesh = Mesh(devices, ("row",) + COL_AXES)
     return jax.shard_map(
         per_device,
-        mesh=mesh,
-        in_specs=(P("row", "col", None, None), P(None, "row"), P(None, "row", "col"), P(), P()),
-        out_specs=P("row", "col", None, None),
+        mesh=split_mesh,
+        in_specs=(
+            P("row", COL_AXES, None, None),
+            P(None, "row"),
+            P(None, "row", COL_AXES),
+            P(),
+            P(),
+        ),
+        out_specs=P("row", COL_AXES, None, None),
         check_vma=False,
     )

time: 261 us -> 210 us (0.80)
  waiting for transfers between devices: 181 us -> 114 us
  blocking collectives: 0 us -> 14.5 us
  starting transfers between devices: 12.1 us -> 17.1 us
  other arithmetic: 6.69 us -> 3.7 us
    psum x1 -> x0, waiting for transfers between devices: 54.8 us -> none  [broadcast(): return lax.psum(jnp.where(mine, array, jnp.zeros_like(array)), axis)]
    all_gather x1 -> x2, waiting for transfers between devices: 78.6 us -> 64 us  [the longest x1 49.2 us: per_device(): both_rows = lax.all_gather(both_rows, ('zh', 'zl'), axis=1, tiled=True)]
    all_gather x0 -> x1, blocking collectives: none -> 14.5 us  [per_device(): both_rows = lax.all_gather(both_pieces, 'x', axis=1, tiled=True)]
    ppermute x0 -> x1, starting transfers between devices: none -> 5.02 us  [per_device(): swapped = lax.ppermute(both_pieces, ('row',) + CLASS_AXES, swap)]
    ppermute x0 -> x1, waiting for transfers between devices: none -> 2.64 us  [per_device(): swapped = lax.ppermute(both_pieces, ('row',) + CLASS_AXES, swap)]
  transfers between devices with their start and end apart: 3 -> 4, of which waited for: 3 -> 4; matrix products, arithmetic and copies ran while one was open for 5% -> 4% of each run, Pallas kernels for 0% -> 0%
where the time goes in v2:
time: 210 us
  waiting for transfers between devices  114 us (54%)
  matrix products  25.2 us (12%)
  local copies, waits for them, and re-layouts  21.7 us (10%)
  starting transfers between devices  17.1 us (8%)
  blocking collectives  14.5 us (7%)
  between operations  13.6 us (6%)
  other arithmetic  3.7 us (2%)
    all_gather x1, waiting for transfers between devices, per_device(): both_rows = lax.all_gather(both_rows, ('zh', 'zl'), axis=1, tiled=True)  49.2 us
    all_to_all x1, waiting for transfers between devices, per_device(): received = lax.all_to_all(pieces, COL_AXES, 0, 0, tiled=True)  47.3 us
    dot_general x1, matrix products, per_device(): jnp.einsum('sak,sbk->sab', left_blocks, right_blocks, precision=HIGHEST_P...  22.4 us
    all_gather x1, waiting for transfers between devices, per_device(): class_pieces = lax.all_gather(swapped, 'row', axis=0, tiled=False)  14.8 us
    all_gather x1, blocking collectives, per_device(): both_rows = lax.all_gather(both_pieces, 'x', axis=1, tiled=True)  14.5 us
    all_to_all x1, starting transfers between devices, per_device(): received = lax.all_to_all(pieces, COL_AXES, 0, 0, tiled=True)  12 us
    ppermute x1, starting transfers between devices, per_device(): swapped = lax.ppermute(both_pieces, ('row',) + CLASS_AXES, swap)  5.02 us
    gather x1, local copies, waits for them, and re-layouts, per_device(): second_rows[left_slot]  4.4 us
  transfers between devices with their start and end apart: 4, of which 4 were waited for; matrix products, arithmetic and copies ran while one was open for 4% of the time, Pallas kernels for 0%

profile of v2, /device:TPU:1, one launch (start us, length us, event | category | flops | bytes accessed | tf_op | source)
XLA Modules:
  0.0 209.8 jit_solution(8617858853089298550)
XLA Ops:
  6.5 0.0 copy-start
  6.5 0.0 copy-start.5
  6.5 0.0 copy-start.2
  6.5 3.1 %slice.60 = f32[8,1,256,256]{3,2,1,0:T(8,128)} slice(f32[16,1,256,256]{3,2,1,0:T(8,128)} %param.5), slice={[0:8], [0:1], [0:256], [0:256]} | slice | bytes 4194304 | tf_op jit(solution)/shard_map/slice | solution.py:28
  9.7 0.0 copy-start.4
  9.7 12.0 %all-to-all-start = ((f32[32,64,256]{2,1,0:T(8,128)}), f32[32,64,256]{2,1,0:T(8,128)S(1)}, u32[]{:S(2)}, u32[]{:S(2)}) async-start(f32[32,64,256]{2,1,0:T(8,128)} %bitcast.2), calls=%async_computation | async-start | bytes 4194304 | tf_op jit(solution)/shard_map/all_to_all | solution.py:31
  21.7 0.0 all-gather.6.cloned.1.call-start
  21.7 0.0 copy-done.5
  21.8 0.6 fusion.25
  22.4 0.0 copy-done
  22.4 0.0 copy-done.2
  22.4 0.4 fusion.13
  22.8 47.3 %all-to-all-done = f32[32,64,256]{2,1,0:T(8,128)S(1)} async-done(((f32[32,64,256]{2,1,0:T(8,128)}), f32[32,64,256]{2,1,0:T(8,128)S(1)}, u32[]{:S(2)}, u32[]{:S(2)}) %all-to-all-start) | async-done | bytes 2097184 | tf_op jit(solution)/shard_map/all_to_all | solution.py:31
  70.1 1.0 convolution_select_fusion.1
  71.1 0.4 convolution_subtract_fusion
  71.5 1.0 fusion.7
  72.5 5.0 %collective-permute-start = (f32[2,64,256]{2,1,0:T(8,128)S(1)}, f32[2,64,256]{2,1,0:T(8,128)S(1)}, u32[]{:S(2)}, u32[]{:S(2)}) collective-permute-start(f32[2,64,256]{2,1,0:T(8,128)S(1)} %pad_maximum_fusion), channel_id=1, source_target_pairs={{0,0},{1,32},{2,64},{3,96},{4,128},{5,160},{6,192},{7,224},{32,1},... | collective-permute-start | bytes 393224 | tf_op jit(solution)/shard_map/ppermute | solution.py:44
  77.6 2.6 %collective-permute-done = f32[2,64,256]{2,1,0:T(8,128)S(1)} collective-permute-done((f32[2,64,256]{2,1,0:T(8,128)S(1)}, f32[2,64,256]{2,1,0:T(8,128)S(1)}, u32[]{:S(2)}, u32[]{:S(2)}) %collective-permute-start) | collective-permute-done | bytes 131104 | tf_op jit(solution)/shard_map/ppermute | solution.py:44
  80.2 0.0 copy-start.3
  80.2 0.7 copy-done.3
  80.9 0.0 all-gather.6.cloned.1.call-update
  80.9 0.0 all-gather.4.cloned.1.call-start
  80.9 14.5 %all_gather.12 = f32[2,256,256]{2,1,0:T(8,128)} all-gather(f32[2,64,256]{2,1,0:T(8,128)S(1)} %pad_maximum_fusion), channel_id=1, replica_groups=mesh['row'=8,'zh'=4,'zl'=2,'x'=4] {'x'}, dimensions={1}, use_global_device_ids=true | all-gather | bytes 655360 | tf_op jit(solution)/shard_map/all_gather | solution.py:49
  95.4 0.0 all-gather.4.cloned.1.call-update
  95.5 0.0 copy-done.4
  95.6 14.8 %all-gather.6.cloned.1.call-done = f32[16,64,256]{2,1,0:T(8,128)} async-done(((f32[2,64,256]{2,1,0:T(8,128)}), f32[16,64,256]{2,1,0:T(8,128)}) %all-gather.6.cloned.1.call-update) | async-done | bytes 1048592 | tf_op jit(solution)/shard_map/all_gather | solution.py:45
  110.3 1.3 fusion.23
  111.6 2.8 %gather_fusion.2 = f32[16,256,256]{2,1,0:T(8,128)} fusion(f32[2,256,256]{2,1,0:T(8,128)S(1)} %bitcast.56, s32[1024]{0:T(1024)S(1)} %get-tuple-element.17), kind=kCustom, calls=%fused_computation.2 | custom fusion | bytes 8388672 | tf_op jit(solution)/shard_map/gather | solution.py:63
  114.4 2.8 %gather_fusion.3 = f32[16,256,256]{2,1,0:T(8,128)} fusion(f32[2,256,256]{2,1,0:T(8,128)S(1)} %bitcast.55, s32[1024]{0:T(1024)S(1)} %get-tuple-element.17), kind=kCustom, calls=%fused_computation.3 | custom fusion | bytes 8388672 | tf_op jit(solution)/shard_map/gather | solution.py:63
  117.2 49.2 %all-gather.4.cloned.1.call-done = f32[2,2048,256]{2,1,0:T(8,128)} async-done(((f32[2,256,256]{2,1,0:T(8,128)}), f32[2,2048,256]{2,1,0:T(8,128)}) %all-gather.4.cloned.1.call-update) | async-done | bytes 4194320 | tf_op jit(solution)/shard_map/all_gather | solution.py:50
  166.4 3.8 %fusion.22 = (f32[1,2048,256]{2,1,0:T(8,128)S(1)}, f32[1,2048,256]{2,1,0:T(8,128)}) fusion(f32[2,2048,256]{2,1,0:T(8,128)} %all-gather.4.cloned.1.call-done), kind=kLoop, calls=%fused_computation.42 | loop fusion | bytes 8388608 | tf_op jit(solution)/shard_map/slice | solution.py:52
  170.3 2.8 %gather_fusion = f32[16,256,256]{2,1,0:T(8,128)} fusion(f32[8,256,256]{2,1,0:T(8,128)S(1)} %bitcast.57, s32[1024]{0:T(1024)S(1)} %get-tuple-element.18), kind=kCustom, calls=%fused_computation | custom fusion | bytes 8388672 | tf_op jit(solution)/shard_map/gather | solution.py:62
  173.0 4.4 %gather_fusion.1 = f32[16,256,256]{2,1,0:T(8,128)} fusion(f32[8,256,256]{2,1,0:T(8,128)} %bitcast.59, s32[1024]{0:T(1024)S(1)} %get-tuple-element.18), kind=kCustom, calls=%fused_computation.1 | custom fusion | bytes 8388672 | tf_op jit(solution)/shard_map/gather | solution.py:62
  177.4 0.0 copy-start.1
  177.4 22.4 %bitcast_subtract_fusion = f32[16,256,256]{2,1,0:T(8,128)S(1)} fusion(f32[16,1,256,256]{3,2,1,0:T(8,128)} %param.5, pred[16]{0:T(512)(128)(4,1)S(1)} %compare_bitcast_fusion, f32[16,256,256]{2,1,0:T(8,128)} %gather_fusion.3, f32[16,256,256]{2,1,0:T(8,128)} %gather_fusion.2, f32[16,256,256]{2,1,0:T(8,128)} %gather_fusion.1, f32[16,256,256]{2,1,0:T(8,128)} %gather_fusion), kind=kOutput, calls=%fused_computation.12 | convolution fusion | flops 6448742400 | bytes 25165840 | tf_op jit(solution)/shard_map/sak,sbk->sab/dot_general | solution.py:64
  199.9 0.0 copy-done.1
  199.9 0.6 slice_select_fusion
  200.5 2.4 %maximum_bitcast_fusion = f32[16,1,256,256]{3,2,1,0:T(8,128)} fusion(f32[8,256,256]{2,1,0:T(8,128)S(1)} %get-tuple-element.6, f32[8,256,256]{2,1,0:T(8,128)S(1)} %get-tuple-element.5), kind=kLoop, calls=%fused_computation.11 | loop fusion | flops 1048576 | bytes 8388608 | tf_op jit(solution)/shard_map/broadcast_in_dim | solution.py:71
  (7 shorter events, 0.0 us)
Async XLA Ops:
  6.5 15.9 %copy-start = (f32[256,256]{1,0:T(8,128)S(1)}, f32[256,256]{1,0:T(8,128)}, u32[]{:S(2)}) copy-start(f32[256,256]{1,0:T(8,128)} %param.9) | copy-start | bytes 786436
  6.5 15.2 %copy-start.5 = (s32[2,8]{1,0:T(2,128)S(1)}, s32[2,8]{1,0:T(2,128)}, u32[]{:S(2)}) copy-start(s32[2,8]{1,0:T(2,128)} %param.6) | copy-start | bytes 196
  6.5 15.9 %copy-start.2 = (f32[2,256,256]{2,1,0:T(8,128)S(1)}, f32[2,256,256]{2,1,0:T(8,128)}, u32[]{:S(2)}) copy-start(f32[2,256,256]{2,1,0:T(8,128)} %param.8) | copy-start | bytes 1572868
  9.7 85.8 %copy-start.4 = (s32[2,16,1]{1,2,0:T(1,128)S(1)}, s32[2,16,1]{1,2,0:T(1,128)}, u32[]{:S(2)}) copy-start(s32[2,16,1]{1,2,0:T(1,128)} %param.7) | copy-start | bytes 388
  9.7 60.5 %all-to-all-start = ((f32[32,64,256]{2,1,0:T(8,128)}), f32[32,64,256]{2,1,0:T(8,128)S(1)}, u32[]{:S(2)}, u32[]{:S(2)}) async-start(f32[32,64,256]{2,1,0:T(8,128)} %bitcast.2), calls=%async_computation | async-start | bytes 4194304 | tf_op jit(solution)/shard_map/all_to_all | solution.py:31
  21.7 88.7 %all-gather.6.cloned.1.call-start = ((), (), s32[]{:S(2)}) async-start(), calls=%async_computation.2 | async-start | bytes 1179648 | tf_op jit(solution)/shard_map/all_gather | solution.py:45
  72.5 7.7 %collective-permute-start = (f32[2,64,256]{2,1,0:T(8,128)S(1)}, f32[2,64,256]{2,1,0:T(8,128)S(1)}, u32[]{:S(2)}, u32[]{:S(2)}) collective-permute-start(f32[2,64,256]{2,1,0:T(8,128)S(1)} %pad_maximum_fusion), channel_id=1, source_target_pairs={{0,0},{1,32},{2,64},{3,96},{4,128},{5,160},{6,192},{7,224},{32,1},... | collective-permute-start | bytes 393224 | tf_op jit(solution)/shard_map/ppermute | solution.py:44
  80.2 0.7 copy-start.3
  80.9 85.5 %all-gather.4.cloned.1.call-start = ((), (), s32[]{:S(2)}) async-start(), calls=%async_computation.1 | async-start | bytes 4718592 | tf_op jit(solution)/shard_map/all_gather | solution.py:50
  177.4 22.5 %copy-start.1 = (f32[1,2048,256]{2,1,0:T(8,128)S(1)}, f32[1,2048,256]{2,1,0:T(8,128)}, u32[]{:S(2)}) copy-start(f32[1,2048,256]{2,1,0:T(8,128)} %get-tuple-element.8) | copy-start | bytes 6291460
Sparse Core Ops, SparseCore 0:
  81.0 29.2 all-gather.5
  112.1 54.2 all-gather.3

commit v3 on v2

--- a/solution.py
+++ b/solution.py
@@ -10,6 +10,7 @@
 
 
 HIGHEST_PRECISION = lax.Precision.HIGHEST
+PRODUCT_PRECISION = lax.Precision.HIGH
 COL_AXES = ("zh", "zl", "x")
 CLASS_AXES = ("zl", "x")
 
@@ -51,17 +52,15 @@
     both_rows = both_rows.reshape(2, slot_count, block, block)
     first_rows = both_rows[0]
     second_rows = both_rows[1]
-    first_cols = both_cols[0]
-    second_cols = both_cols[1]
     class_start = column // row_count * PER_CLASS
     row_index = target_slots[0, :, 0]
     col_index = target_slots[1, :, 0]
     present = row_index >= 0
     left_slot = jnp.where(present, row_index, 0)
     right_slot = jnp.where(present, col_index - class_start, 0)
-    left_blocks = jnp.concatenate([first_rows[left_slot], second_rows[left_slot]], axis=2)
-    right_blocks = jnp.concatenate([first_cols[right_slot], second_cols[right_slot]], axis=2)
-    schur_term = jnp.einsum("sak,sbk->sab", left_blocks, right_blocks, precision=HIGHEST_PRECISION)
+    products = jnp.einsum("fakm,fbjm->abkj", both_rows, both_cols, precision=PRODUCT_PRECISION)
+    products = products.reshape(slot_count * PER_CLASS, block, block)
+    schur_term = products[left_slot * PER_CLASS + right_slot]
     trailing = stored - jnp.where(present[:, None, None], schur_term, 0.0)
     head_live = panel_rows >= 0
     keep_mask = ((column == 0) & head_live[0] | (column == 1) & head_live[1])[:, None, None]

time: 210 us -> 199 us (0.948)
  matrix products: 25.2 us -> 10 us
  local copies, waits for them, and re-layouts: 21.7 us -> 15.9 us
  waiting for transfers between devices: 114 us -> 119 us
  other arithmetic: 3.7 us -> 8.09 us
    dot_general x1, matrix products: 22.4 us -> 7.27 us  [per_device(): jnp.einsum('fakm,fbjm->abkj', both_rows, both_cols, precision=PRODUCT_PRE...]
    gather x4 -> x1, local copies, waits for them, and re-layouts: 12.8 us -> 5.01 us  [per_device(): schur_term = products[left_slot * PER_CLASS + right_slot]]
    all_gather x1, waiting for transfers between devices: 49.2 us -> 54.8 us  [per_device(): both_rows = lax.all_gather(both_rows, ('zh', 'zl'), axis=1, tiled=True)]
    transpose x0 -> x1, local copies, waits for them, and re-layouts: none -> 5.41 us  [per_device(): jnp.einsum('fakm,fbjm->abkj', both_rows, both_cols, precision=PRODUCT_PRE...]
    slice x2 -> x0, local copies, waits for them, and re-layouts: 5.13 us -> none  [the longest x1 3.83 us: per_device(): first_rows = both_rows[0]]
    sub x0 -> x1, other arithmetic: none -> 4.23 us  [per_device(): trailing = stored - jnp.where(present[:, None, None], schur_term, 0.0)]
  transfers between devices with their start and end apart: 4 -> 4, of which waited for: 4 -> 4; matrix products, arithmetic and copies ran while one was open for 4% -> 1% of each run, Pallas kernels for 0% -> 0%
where the time goes in v3:
time: 199 us
  waiting for transfers between devices  119 us (60%)
  starting transfers between devices  17.1 us (9%)
  local copies, waits for them, and re-layouts  15.9 us (8%)
  blocking collectives  14.5 us (7%)
  between operations  13.6 us (7%)
  matrix products  10 us (5%)
  other arithmetic  8.09 us (4%)
    all_gather x1, waiting for transfers between devices, per_device(): both_rows = lax.all_gather(both_rows, ('zh', 'zl'), axis=1, tiled=True)  54.8 us
    all_to_all x1, waiting for transfers between devices, per_device(): received = lax.all_to_all(pieces, COL_AXES, 0, 0, tiled=True)  47.3 us
    all_gather x1, waiting for transfers between devices, per_device(): class_pieces = lax.all_gather(swapped, 'row', axis=0, tiled=False)  14.8 us
    all_gather x1, blocking collectives, per_device(): both_rows = lax.all_gather(both_pieces, 'x', axis=1, tiled=True)  14.5 us
    all_to_all x1, starting transfers between devices, per_device(): received = lax.all_to_all(pieces, COL_AXES, 0, 0, tiled=True)  12 us
    dot_general x1, matrix products, per_device(): jnp.einsum('fakm,fbjm->abkj', both_rows, both_cols, precision=PRODUCT_PRE...  7.27 us
    transpose x1, local copies, waits for them, and re-layouts, per_device(): jnp.einsum('fakm,fbjm->abkj', both_rows, both_cols, precision=PRODUCT_PRE...  5.41 us
    ppermute x1, starting transfers between devices, per_device(): swapped = lax.ppermute(both_pieces, ('row',) + CLASS_AXES, swap)  5.02 us
  transfers between devices with their start and end apart: 4, of which 4 were waited for; matrix products, arithmetic and copies ran while one was open for 1% of the time, Pallas kernels for 0%

profile of v3, /device:TPU:1, one launch (start us, length us, event | category | flops | bytes accessed | tf_op | source)
XLA Modules:
  0.0 198.7 jit_solution(16694996694409143675)
XLA Ops:
  6.5 0.0 copy-start
  6.5 0.0 copy-start.5
  6.5 0.0 copy-start.2
  6.5 3.1 %slice.52 = f32[8,1,256,256]{3,2,1,0:T(8,128)} slice(f32[16,1,256,256]{3,2,1,0:T(8,128)} %param.5), slice={[0:8], [0:1], [0:256], [0:256]} | slice | bytes 4194304 | tf_op jit(solution)/shard_map/slice | solution.py:29
  9.7 0.0 copy-start.4
  9.7 12.0 %all-to-all-start = ((f32[32,64,256]{2,1,0:T(8,128)}), f32[32,64,256]{2,1,0:T(8,128)S(1)}, u32[]{:S(2)}, u32[]{:S(2)}) async-start(f32[32,64,256]{2,1,0:T(8,128)} %bitcast.2), calls=%async_computation | async-start | bytes 4194304 | tf_op jit(solution)/shard_map/all_to_all | solution.py:32
  21.7 0.0 all-gather.6.cloned.1.call-start
  21.7 0.0 copy-done.5
  21.8 0.7 fusion.18
  22.4 0.0 copy-done
  22.4 0.0 copy-done.2
  22.4 0.4 fusion.8
  22.9 47.3 %all-to-all-done = f32[32,64,256]{2,1,0:T(8,128)S(1)} async-done(((f32[32,64,256]{2,1,0:T(8,128)}), f32[32,64,256]{2,1,0:T(8,128)S(1)}, u32[]{:S(2)}, u32[]{:S(2)}) %all-to-all-start) | async-done | bytes 2097184 | tf_op jit(solution)/shard_map/all_to_all | solution.py:32
  70.1 0.9 convolution_select_fusion.1
  71.1 0.4 convolution_subtract_fusion
  71.4 1.1 fusion.6
  72.5 5.0 %collective-permute-start = (f32[2,64,256]{2,1,0:T(8,128)S(1)}, f32[2,64,256]{2,1,0:T(8,128)S(1)}, u32[]{:S(2)}, u32[]{:S(2)}) collective-permute-start(f32[2,64,256]{2,1,0:T(8,128)S(1)} %pad_maximum_fusion), channel_id=1, source_target_pairs={{0,0},{1,32},{2,64},{3,96},{4,128},{5,160},{6,192},{7,224},{32,1},... | collective-permute-start | bytes 393224 | tf_op jit(solution)/shard_map/ppermute | solution.py:45
  77.5 2.6 %collective-permute-done = f32[2,64,256]{2,1,0:T(8,128)S(1)} collective-permute-done((f32[2,64,256]{2,1,0:T(8,128)S(1)}, f32[2,64,256]{2,1,0:T(8,128)S(1)}, u32[]{:S(2)}, u32[]{:S(2)}) %collective-permute-start) | collective-permute-done | bytes 131104 | tf_op jit(solution)/shard_map/ppermute | solution.py:45
  80.2 0.0 copy-start.3
  80.2 0.7 copy-done.3
  80.8 0.0 all-gather.6.cloned.1.call-update
  80.9 0.0 all-gather.4.cloned.1.call-start
  80.9 14.5 %all_gather.12 = f32[2,256,256]{2,1,0:T(8,128)} all-gather(f32[2,64,256]{2,1,0:T(8,128)S(1)} %pad_maximum_fusion), channel_id=1, replica_groups=mesh['row'=8,'zh'=4,'zl'=2,'x'=4] {'x'}, dimensions={1}, use_global_device_ids=true | all-gather | bytes 655360 | tf_op jit(solution)/shard_map/all_gather | solution.py:50
  95.4 0.0 all-gather.4.cloned.1.call-update
  95.5 0.0 copy-done.4
  95.5 14.8 %all-gather.6.cloned.1.call-done = f32[16,64,256]{2,1,0:T(8,128)} async-done(((f32[2,64,256]{2,1,0:T(8,128)}), f32[16,64,256]{2,1,0:T(8,128)}) %all-gather.6.cloned.1.call-update) | async-done | bytes 1048592 | tf_op jit(solution)/shard_map/all_gather | solution.py:46
  110.3 1.3 copy.12
  111.6 54.8 %all-gather.4.cloned.1.call-done = f32[2,2048,256]{2,1,0:T(8,128)} async-done(((f32[2,256,256]{2,1,0:T(8,128)}), f32[2,2048,256]{2,1,0:T(8,128)}) %all-gather.4.cloned.1.call-update) | async-done | bytes 4194320 | tf_op jit(solution)/shard_map/all_gather | solution.py:51
  166.4 7.3 %fusion.3 = f32[8,2,256,256]{2,3,0,1:T(8,128)} fusion(f32[2,2,256,256,1]{3,2,0,4,1:T(8,128)S(1)} %bitcast.70, f32[2,8,256,256]{3,2,1,0:T(8,128)} %bitcast.67), kind=kOutput, calls=%fused_computation.6 | convolution fusion | flops 3221225472 | bytes 9437184 | tf_op jit(solution)/shard_map/fakm,fbjm->abkj/dot_general | solution.py:61
  173.7 5.4 %copy.14 = f32[8,2,256,256]{3,2,1,0:T(8,128)} copy(f32[8,2,256,256]{2,3,0,1:T(8,128)} %fusion.3) | data formatting | bytes 8388608 | tf_op jit(solution)/shard_map/fakm,fbjm->abkj/transpose | solution.py:61
  179.1 5.0 %gather_fusion = f32[16,256,256]{2,1,0:T(8,128)} fusion(f32[16,256,256]{2,1,0:T(8,128)} %bitcast.68, s32[1024]{0:T(1024)S(1)} %pad_clamp_fusion), kind=kCustom, calls=%fused_computation | custom fusion | bytes 8388672 | tf_op jit(solution)/shard_map/gather | solution.py:63
  184.1 0.0 copy-start.1
  184.1 4.2 %bitcast_subtract_fusion = f32[16,256,256]{2,1,0:T(8,128)S(1)} fusion(f32[16,1,256,256]{3,2,1,0:T(8,128)} %param.5, f32[16,256,256]{2,1,0:T(8,128)} %gather_fusion, pred[16]{0:T(512)(128)(4,1)S(1)} %compare_bitcast_fusion), kind=kLoop, calls=%fused_computation.4 | loop fusion | flops 2097152 | bytes 12582928 | tf_op jit(solution)/shard_map/sub | solution.py:64
  188.3 0.4 copy-done.1
  188.7 0.3 slice_select_fusion.1
  189.0 0.4 slice_select_fusion
  189.4 2.4 %maximum_bitcast_fusion = f32[16,1,256,256]{3,2,1,0:T(8,128)} fusion(f32[8,256,256]{2,1,0:T(8,128)S(1)} %get-tuple-element.6, f32[8,256,256]{2,1,0:T(8,128)S(1)} %get-tuple-element.5), kind=kLoop, calls=%fused_computation.1 | loop fusion | flops 1048576 | bytes 8388608 | tf_op jit(solution)/shard_map/broadcast_in_dim | solution.py:70
  (7 shorter events, 0.1 us)
Async XLA Ops:
  6.5 15.9 %copy-start = (f32[256,256]{1,0:T(8,128)S(1)}, f32[256,256]{1,0:T(8,128)}, u32[]{:S(2)}) copy-start(f32[256,256]{1,0:T(8,128)} %param.9) | copy-start | bytes 786436
  6.5 15.2 %copy-start.5 = (s32[2,8]{1,0:T(2,128)S(1)}, s32[2,8]{1,0:T(2,128)}, u32[]{:S(2)}) copy-start(s32[2,8]{1,0:T(2,128)} %param.6) | copy-start | bytes 196
  6.5 15.9 %copy-start.2 = (f32[2,256,256]{2,1,0:T(8,128)S(1)}, f32[2,256,256]{2,1,0:T(8,128)}, u32[]{:S(2)}) copy-start(f32[2,256,256]{2,1,0:T(8,128)} %param.8) | copy-start | bytes 1572868
  9.7 85.8 %copy-start.4 = (s32[2,16,1]{1,2,0:T(1,128)S(1)}, s32[2,16,1]{1,2,0:T(1,128)}, u32[]{:S(2)}) copy-start(s32[2,16,1]{1,2,0:T(1,128)} %param.7) | copy-start | bytes 388
  9.7 60.5 %all-to-all-start = ((f32[32,64,256]{2,1,0:T(8,128)}), f32[32,64,256]{2,1,0:T(8,128)S(1)}, u32[]{:S(2)}, u32[]{:S(2)}) async-start(f32[32,64,256]{2,1,0:T(8,128)} %bitcast.2), calls=%async_computation | async-start | bytes 4194304 | tf_op jit(solution)/shard_map/all_to_all | solution.py:32
  21.7 88.6 %all-gather.6.cloned.1.call-start = ((), (), s32[]{:S(2)}) async-start(), calls=%async_computation.2 | async-start | bytes 1179648 | tf_op jit(solution)/shard_map/all_gather | solution.py:46
  72.5 7.7 %collective-permute-start = (f32[2,64,256]{2,1,0:T(8,128)S(1)}, f32[2,64,256]{2,1,0:T(8,128)S(1)}, u32[]{:S(2)}, u32[]{:S(2)}) collective-permute-start(f32[2,64,256]{2,1,0:T(8,128)S(1)} %pad_maximum_fusion), channel_id=1, source_target_pairs={{0,0},{1,32},{2,64},{3,96},{4,128},{5,160},{6,192},{7,224},{32,1},... | collective-permute-start | bytes 393224 | tf_op jit(solution)/shard_map/ppermute | solution.py:45
  80.2 0.7 copy-start.3
  80.9 85.5 %all-gather.4.cloned.1.call-start = ((), (), s32[]{:S(2)}) async-start(), calls=%async_computation.1 | async-start | bytes 4718592 | tf_op jit(solution)/shard_map/all_gather | solution.py:51
  184.1 4.6 %copy-start.1 = (f32[2,2048,256]{2,1,0:T(8,128)S(1)}, f32[2,2048,256]{2,1,0:T(8,128)}, u32[]{:S(2)}) copy-start(f32[2,2048,256]{2,1,0:T(8,128)} %all-gather.4.cloned.1.call-done) | copy-start | bytes 12582916
Sparse Core Ops, SparseCore 0:
  81.0 29.2 all-gather.5
  112.1 54.2 all-gather.3

commit v4 on v3

--- a/solution.py
+++ b/solution.py
@@ -43,7 +43,8 @@
     class_size = lax.axis_size(CLASS_AXES)
     swap = [(a * class_size + b, b * class_size + a) for a in range(row_count) for b in range(class_size)]
     swapped = lax.ppermute(both_pieces, ("row",) + CLASS_AXES, swap)
-    class_pieces = lax.all_gather(swapped, "row", axis=0, tiled=False)
+    spread = jnp.broadcast_to(swapped[None], (row_count,) + swapped.shape)
+    class_pieces = lax.all_to_all(spread, "row", 0, 0, tiled=True)
     per_slot = block // chunk
     class_pieces = class_pieces.reshape(PER_CLASS, per_slot, 2, chunk, block)
     both_cols = class_pieces.transpose(2, 0, 1, 3, 4).reshape(2, PER_CLASS, block, block)

time: 199 us -> 173 us (0.87)
  waiting for transfers between devices: 119 us -> 83.3 us
  starting transfers between devices: 17.1 us -> 28.7 us
    all_gather x1, waiting for transfers between devices: 54.8 us -> 18.3 us  [per_device(): both_rows = lax.all_gather(both_rows, ('zh', 'zl'), axis=1, tiled=True)]
    all_to_all x0 -> x1, waiting for transfers between devices: none -> 15 us  [per_device(): class_pieces = lax.all_to_all(spread, 'row', 0, 0, tiled=True)]
    all_gather x1 -> x0, waiting for transfers between devices: 14.8 us -> none  [per_device(): class_pieces = lax.all_gather(swapped, 'row', axis=0, tiled=False)]
    all_to_all x0 -> x1, starting transfers between devices: none -> 10.8 us  [per_device(): class_pieces = lax.all_to_all(spread, 'row', 0, 0, tiled=True)]
where the time goes in v4:
time: 173 us
  waiting for transfers between devices  83.3 us (48%)
  starting transfers between devices  28.7 us (17%)
  local copies, waits for them, and re-layouts  15.1 us (9%)
  blocking collectives  13.8 us (8%)
  between operations  13.6 us (8%)
  matrix products  10 us (6%)
  other arithmetic  8.07 us (5%)
    all_to_all x1, waiting for transfers between devices, per_device(): received = lax.all_to_all(pieces, COL_AXES, 0, 0, tiled=True)  47.3 us
    all_gather x1, waiting for transfers between devices, per_device(): both_rows = lax.all_gather(both_rows, ('zh', 'zl'), axis=1, tiled=True)  18.3 us
    all_to_all x1, waiting for transfers between devices, per_device(): class_pieces = lax.all_to_all(spread, 'row', 0, 0, tiled=True)  15 us
    all_gather x1, blocking collectives, per_device(): both_rows = lax.all_gather(both_pieces, 'x', axis=1, tiled=True)  13.8 us
    all_to_all x1, starting transfers between devices, per_device(): received = lax.all_to_all(pieces, COL_AXES, 0, 0, tiled=True)  11.9 us
    all_to_all x1, starting transfers between devices, per_device(): class_pieces = lax.all_to_all(spread, 'row', 0, 0, tiled=True)  10.8 us
    dot_general x1, matrix products, per_device(): jnp.einsum('fakm,fbjm->abkj', both_rows, both_cols, precision=PRODUCT_PRE...  7.27 us
    ppermute x1, starting transfers between devices, per_device(): swapped = lax.ppermute(both_pieces, ('row',) + CLASS_AXES, swap)  5.96 us
  transfers between devices with their start and end apart: 4, of which 4 were waited for; matrix products, arithmetic and copies ran while one was open for 1% of the time, Pallas kernels for 0%

profile of v4, /device:TPU:1, one launch (start us, length us, event | category | flops | bytes accessed | tf_op | source)
XLA Modules:
  0.0 172.6 jit_solution(12573956232011336802)
XLA Ops:
  6.5 0.0 copy-start
  6.5 0.0 copy-start.4
  6.5 0.0 copy-start.2
  6.5 3.1 %slice.52 = f32[8,1,256,256]{3,2,1,0:T(8,128)} slice(f32[16,1,256,256]{3,2,1,0:T(8,128)} %param.5), slice={[0:8], [0:1], [0:256], [0:256]} | slice | bytes 4194304 | tf_op jit(solution)/shard_map/slice | solution.py:29
  9.7 11.9 %all-to-all-start = ((f32[32,64,256]{2,1,0:T(8,128)}), f32[32,64,256]{2,1,0:T(8,128)S(1)}, u32[]{:S(2)}, u32[]{:S(2)}) async-start(f32[32,64,256]{2,1,0:T(8,128)} %bitcast.2), calls=%async_computation | async-start | bytes 4194304 | tf_op jit(solution)/shard_map/all_to_all | solution.py:32
  21.5 0.0 copy-start.3
  21.5 0.0 all-gather.2.cloned.1.call-start
  21.6 0.0 copy-done.4
  21.6 0.7 fusion.18
  22.3 0.0 copy-done
  22.3 0.0 copy-done.2
  22.3 0.4 fusion.8
  22.7 47.3 %all-to-all-done = f32[32,64,256]{2,1,0:T(8,128)S(1)} async-done(((f32[32,64,256]{2,1,0:T(8,128)}), f32[32,64,256]{2,1,0:T(8,128)S(1)}, u32[]{:S(2)}, u32[]{:S(2)}) %all-to-all-start) | async-done | bytes 2097184 | tf_op jit(solution)/shard_map/all_to_all | solution.py:32
  70.0 1.0 convolution_select_fusion.1
  71.0 0.4 convolution_subtract_fusion
  71.4 1.0 fusion.6
  72.4 13.8 %all_gather.6 = f32[2,256,256]{2,1,0:T(8,128)} all-gather(f32[2,64,256]{2,1,0:T(8,128)S(1)} %pad_maximum_fusion), channel_id=1, replica_groups=mesh['row'=8,'zh'=4,'zl'=2,'x'=4] {'x'}, dimensions={1}, use_global_device_ids=true | all-gather | bytes 655360 | tf_op jit(solution)/shard_map/all_gather | solution.py:51
  86.2 0.0 all-gather.2.cloned.1.call-update
  86.2 6.0 %collective-permute-start = (f32[2,64,256]{2,1,0:T(8,128)S(1)}, f32[2,64,256]{2,1,0:T(8,128)S(1)}, u32[]{:S(2)}, u32[]{:S(2)}) collective-permute-start(f32[2,64,256]{2,1,0:T(8,128)S(1)} %pad_maximum_fusion), channel_id=1, source_target_pairs={{0,0},{1,32},{2,64},{3,96},{4,128},{5,160},{6,192},{7,224},{32,1},... | collective-permute-start | bytes 393224 | tf_op jit(solution)/shard_map/ppermute | solution.py:45
  92.2 2.6 %collective-permute-done = f32[2,64,256]{2,1,0:T(8,128)S(1)} collective-permute-done((f32[2,64,256]{2,1,0:T(8,128)S(1)}, f32[2,64,256]{2,1,0:T(8,128)S(1)}, u32[]{:S(2)}, u32[]{:S(2)}) %collective-permute-start) | collective-permute-done | bytes 131104 | tf_op jit(solution)/shard_map/ppermute | solution.py:45
  94.8 1.1 broadcast_in_dim.43
  95.9 10.8 %all-to-all-start.1 = ((f32[8,2,64,256]{3,2,1,0:T(8,128)}), f32[8,2,64,256]{3,2,1,0:T(8,128)S(1)}, u32[]{:S(2)}, u32[]{:S(2)}) async-start(f32[8,2,64,256]{3,2,1,0:T(8,128)} %broadcast_in_dim.43), calls=%async_computation.1 | async-start | bytes 2097152 | tf_op jit(solution)/shard_map/all_to_all | solution.py:47
  106.7 0.0 copy-done.3
  106.8 15.0 %all-to-all-done.1 = f32[8,2,64,256]{3,2,1,0:T(8,128)S(1)} async-done(((f32[8,2,64,256]{3,2,1,0:T(8,128)}), f32[8,2,64,256]{3,2,1,0:T(8,128)S(1)}, u32[]{:S(2)}, u32[]{:S(2)}) %all-to-all-start.1) | async-done | bytes 1048608 | tf_op jit(solution)/shard_map/all_to_all | solution.py:47
  121.8 0.1 copy.7
  121.9 18.3 %all-gather.2.cloned.1.call-done = f32[2,2048,256]{2,1,0:T(8,128)} async-done(((f32[2,256,256]{2,1,0:T(8,128)}), f32[2,2048,256]{2,1,0:T(8,128)}) %all-gather.2.cloned.1.call-update) | async-done | bytes 4194320 | tf_op jit(solution)/shard_map/all_gather | solution.py:52
  140.3 7.3 %fusion.3 = f32[8,2,256,256]{2,3,0,1:T(8,128)} fusion(f32[2,2,256,256,1]{3,2,0,4,1:T(8,128)S(1)} %bitcast.70, f32[2,8,256,256]{3,2,1,0:T(8,128)} %bitcast.67), kind=kOutput, calls=%fused_computation.6 | convolution fusion | flops 3221225472 | bytes 9437184 | tf_op jit(solution)/shard_map/fakm,fbjm->abkj/dot_general | solution.py:62
  147.5 5.4 %copy.9 = f32[8,2,256,256]{3,2,1,0:T(8,128)} copy(f32[8,2,256,256]{2,3,0,1:T(8,128)} %fusion.3) | data formatting | bytes 8388608 | tf_op jit(solution)/shard_map/fakm,fbjm->abkj/transpose | solution.py:62
  152.9 5.0 %gather_fusion = f32[16,256,256]{2,1,0:T(8,128)} fusion(f32[16,256,256]{2,1,0:T(8,128)} %bitcast.68, s32[1024]{0:T(1024)S(1)} %pad_clamp_fusion), kind=kCustom, calls=%fused_computation | custom fusion | bytes 8388672 | tf_op jit(solution)/shard_map/gather | solution.py:64
  158.0 0.0 copy-start.1
  158.0 4.2 %bitcast_subtract_fusion = f32[16,256,256]{2,1,0:T(8,128)S(1)} fusion(f32[16,1,256,256]{3,2,1,0:T(8,128)} %param.5, f32[16,256,256]{2,1,0:T(8,128)} %gather_fusion, pred[16]{0:T(512)(128)(4,1)S(1)} %compare_bitcast_fusion), kind=kLoop, calls=%fused_computation.4 | loop fusion | flops 2097152 | bytes 12582928 | tf_op jit(solution)/shard_map/sub | solution.py:65
  162.2 0.4 copy-done.1
  162.6 0.3 slice_select_fusion.1
  162.9 0.4 slice_select_fusion
  163.3 2.4 %maximum_bitcast_fusion = f32[16,1,256,256]{3,2,1,0:T(8,128)} fusion(f32[8,256,256]{2,1,0:T(8,128)S(1)} %get-tuple-element.6, f32[8,256,256]{2,1,0:T(8,128)S(1)} %get-tuple-element.5), kind=kLoop, calls=%fused_computation.1 | loop fusion | flops 1048576 | bytes 8388608 | tf_op jit(solution)/shard_map/broadcast_in_dim | solution.py:71
  (7 shorter events, 0.1 us)
Async XLA Ops:
  6.5 15.8 %copy-start = (f32[256,256]{1,0:T(8,128)S(1)}, f32[256,256]{1,0:T(8,128)}, u32[]{:S(2)}) copy-start(f32[256,256]{1,0:T(8,128)} %param.9) | copy-start | bytes 786436
  6.5 15.1 %copy-start.4 = (s32[2,8]{1,0:T(2,128)S(1)}, s32[2,8]{1,0:T(2,128)}, u32[]{:S(2)}) copy-start(s32[2,8]{1,0:T(2,128)} %param.6) | copy-start | bytes 196
  6.5 15.8 %copy-start.2 = (f32[2,256,256]{2,1,0:T(8,128)S(1)}, f32[2,256,256]{2,1,0:T(8,128)}, u32[]{:S(2)}) copy-start(f32[2,256,256]{2,1,0:T(8,128)} %param.8) | copy-start | bytes 1572868
  9.7 60.4 %all-to-all-start = ((f32[32,64,256]{2,1,0:T(8,128)}), f32[32,64,256]{2,1,0:T(8,128)S(1)}, u32[]{:S(2)}, u32[]{:S(2)}) async-start(f32[32,64,256]{2,1,0:T(8,128)} %bitcast.2), calls=%async_computation | async-start | bytes 4194304 | tf_op jit(solution)/shard_map/all_to_all | solution.py:32
  21.5 85.2 %copy-start.3 = (s32[2,16,1]{1,2,0:T(1,128)S(1)}, s32[2,16,1]{1,2,0:T(1,128)}, u32[]{:S(2)}) copy-start(s32[2,16,1]{1,2,0:T(1,128)} %param.7) | copy-start | bytes 388
  21.5 118.7 %all-gather.2.cloned.1.call-start = ((), (), s32[]{:S(2)}) async-start(), calls=%async_computation.2 | async-start | bytes 4718592 | tf_op jit(solution)/shard_map/all_gather | solution.py:52
  86.2 8.6 %collective-permute-start = (f32[2,64,256]{2,1,0:T(8,128)S(1)}, f32[2,64,256]{2,1,0:T(8,128)S(1)}, u32[]{:S(2)}, u32[]{:S(2)}) collective-permute-start(f32[2,64,256]{2,1,0:T(8,128)S(1)} %pad_maximum_fusion), channel_id=1, source_target_pairs={{0,0},{1,32},{2,64},{3,96},{4,128},{5,160},{6,192},{7,224},{32,1},... | collective-permute-start | bytes 393224 | tf_op jit(solution)/shard_map/ppermute | solution.py:45
  95.9 25.9 %all-to-all-start.1 = ((f32[8,2,64,256]{3,2,1,0:T(8,128)}), f32[8,2,64,256]{3,2,1,0:T(8,128)S(1)}, u32[]{:S(2)}, u32[]{:S(2)}) async-start(f32[8,2,64,256]{3,2,1,0:T(8,128)} %broadcast_in_dim.43), calls=%async_computation.1 | async-start | bytes 2097152 | tf_op jit(solution)/shard_map/all_to_all | solution.py:47
  158.0 4.6 %copy-start.1 = (f32[2,2048,256]{2,1,0:T(8,128)S(1)}, f32[2,2048,256]{2,1,0:T(8,128)}, u32[]{:S(2)}) copy-start(f32[2,2048,256]{2,1,0:T(8,128)} %all-gather.2.cloned.1.call-done) | copy-start | bytes 12582916
Sparse Core Ops, SparseCore 0:
  86.3 53.9 all-gather.1

commit v5 on v4

--- a/solution.py
+++ b/solution.py
@@ -59,9 +59,8 @@
     present = row_index >= 0
     left_slot = jnp.where(present, row_index, 0)
     right_slot = jnp.where(present, col_index - class_start, 0)
-    products = jnp.einsum("fakm,fbjm->abkj", both_rows, both_cols, precision=PRODUCT_PRECISION)
-    products = products.reshape(slot_count * PER_CLASS, block, block)
-    schur_term = products[left_slot * PER_CLASS + right_slot]
+    products = jnp.einsum("fakm,fbjm->akbj", both_rows, both_cols, precision=PRODUCT_PRECISION)
+    schur_term = products[left_slot, :, right_slot, :]
     trailing = stored - jnp.where(present[:, None, None], schur_term, 0.0)
     head_live = panel_rows >= 0
     keep_mask = ((column == 0) & head_live[0] | (column == 1) & head_live[1])[:, None, None]

time: 173 us -> 167 us (0.965)
  local copies, waits for them, and re-layouts: 15.1 us -> 9.68 us
    transpose x1 -> x0, local copies, waits for them, and re-layouts: 5.39 us -> none  [per_device(): jnp.einsum('fakm,fbjm->abkj', both_rows, both_cols, precision=PRODUCT_PRE...]
where the time goes in v5:
time: 167 us
  waiting for transfers between devices  83.3 us (50%)
  starting transfers between devices  28.7 us (17%)
  blocking collectives  13.8 us (8%)
  between operations  13.5 us (8%)
  matrix products  9.97 us (6%)
  local copies, waits for them, and re-layouts  9.68 us (6%)
  other arithmetic  8.07 us (5%)
    all_to_all x1, waiting for transfers between devices, per_device(): received = lax.all_to_all(pieces, COL_AXES, 0, 0, tiled=True)  47.3 us
    all_gather x1, waiting for transfers between devices, per_device(): both_rows = lax.all_gather(both_rows, ('zh', 'zl'), axis=1, tiled=True)  18.3 us
    all_to_all x1, waiting for transfers between devices, per_device(): class_pieces = lax.all_to_all(spread, 'row', 0, 0, tiled=True)  15 us
    all_gather x1, blocking collectives, per_device(): both_rows = lax.all_gather(both_pieces, 'x', axis=1, tiled=True)  13.8 us
    all_to_all x1, starting transfers between devices, per_device(): received = lax.all_to_all(pieces, COL_AXES, 0, 0, tiled=True)  11.9 us
    all_to_all x1, starting transfers between devices, per_device(): class_pieces = lax.all_to_all(spread, 'row', 0, 0, tiled=True)  10.8 us
    dot_general x1, matrix products, per_device(): jnp.einsum('fakm,fbjm->akbj', both_rows, both_cols, precision=PRODUCT_PRE...  7.19 us
    ppermute x1, starting transfers between devices, per_device(): swapped = lax.ppermute(both_pieces, ('row',) + CLASS_AXES, swap)  5.96 us
  transfers between devices with their start and end apart: 4, of which 4 were waited for; matrix products, arithmetic and copies ran while one was open for 1% of the time, Pallas kernels for 0%

profile of v5, /device:TPU:1, one launch (start us, length us, event | category | flops | bytes accessed | tf_op | source)
XLA Modules:
  0.0 167.1 jit_solution(10187118807811461021)
XLA Ops:
  6.5 0.0 copy-start
  6.5 0.0 copy-start.4
  6.5 0.0 copy-start.2
  6.5 3.1 %slice.52 = f32[8,1,256,256]{3,2,1,0:T(8,128)} slice(f32[16,1,256,256]{3,2,1,0:T(8,128)} %param.5), slice={[0:8], [0:1], [0:256], [0:256]} | slice | bytes 4194304 | tf_op jit(solution)/shard_map/slice | solution.py:29
  9.7 11.9 %all-to-all-start = ((f32[32,64,256]{2,1,0:T(8,128)}), f32[32,64,256]{2,1,0:T(8,128)S(1)}, u32[]{:S(2)}, u32[]{:S(2)}) async-start(f32[32,64,256]{2,1,0:T(8,128)} %bitcast.2), calls=%async_computation | async-start | bytes 4194304 | tf_op jit(solution)/shard_map/all_to_all | solution.py:32
  21.5 0.0 copy-start.3
  21.5 0.0 all-gather.2.cloned.1.call-start
  21.6 0.0 copy-done.4
  21.6 0.7 fusion.18
  22.3 0.0 copy-done
  22.3 0.0 copy-done.2
  22.3 0.4 fusion.7
  22.7 47.3 %all-to-all-done = f32[32,64,256]{2,1,0:T(8,128)S(1)} async-done(((f32[32,64,256]{2,1,0:T(8,128)}), f32[32,64,256]{2,1,0:T(8,128)S(1)}, u32[]{:S(2)}, u32[]{:S(2)}) %all-to-all-start) | async-done | bytes 2097184 | tf_op jit(solution)/shard_map/all_to_all | solution.py:32
  70.0 1.0 convolution_select_fusion.1
  71.0 0.4 convolution_subtract_fusion
  71.4 1.0 fusion.5
  72.4 13.8 %all_gather.6 = f32[2,256,256]{2,1,0:T(8,128)} all-gather(f32[2,64,256]{2,1,0:T(8,128)S(1)} %pad_maximum_fusion), channel_id=1, replica_groups=mesh['row'=8,'zh'=4,'zl'=2,'x'=4] {'x'}, dimensions={1}, use_global_device_ids=true | all-gather | bytes 655360 | tf_op jit(solution)/shard_map/all_gather | solution.py:51
  86.2 0.0 all-gather.2.cloned.1.call-update
  86.2 6.0 %collective-permute-start = (f32[2,64,256]{2,1,0:T(8,128)S(1)}, f32[2,64,256]{2,1,0:T(8,128)S(1)}, u32[]{:S(2)}, u32[]{:S(2)}) collective-permute-start(f32[2,64,256]{2,1,0:T(8,128)S(1)} %pad_maximum_fusion), channel_id=1, source_target_pairs={{0,0},{1,32},{2,64},{3,96},{4,128},{5,160},{6,192},{7,224},{32,1},... | collective-permute-start | bytes 393224 | tf_op jit(solution)/shard_map/ppermute | solution.py:45
  92.2 2.6 %collective-permute-done = f32[2,64,256]{2,1,0:T(8,128)S(1)} collective-permute-done((f32[2,64,256]{2,1,0:T(8,128)S(1)}, f32[2,64,256]{2,1,0:T(8,128)S(1)}, u32[]{:S(2)}, u32[]{:S(2)}) %collective-permute-start) | collective-permute-done | bytes 131104 | tf_op jit(solution)/shard_map/ppermute | solution.py:45
  94.8 1.1 broadcast_in_dim.44
  95.9 10.8 %all-to-all-start.1 = ((f32[8,2,64,256]{3,2,1,0:T(8,128)}), f32[8,2,64,256]{3,2,1,0:T(8,128)S(1)}, u32[]{:S(2)}, u32[]{:S(2)}) async-start(f32[8,2,64,256]{3,2,1,0:T(8,128)} %broadcast_in_dim.44), calls=%async_computation.1 | async-start | bytes 2097152 | tf_op jit(solution)/shard_map/all_to_all | solution.py:47
  106.7 0.0 copy-done.3
  106.8 15.0 %all-to-all-done.1 = f32[8,2,64,256]{3,2,1,0:T(8,128)S(1)} async-done(((f32[8,2,64,256]{3,2,1,0:T(8,128)}), f32[8,2,64,256]{3,2,1,0:T(8,128)S(1)}, u32[]{:S(2)}, u32[]{:S(2)}) %all-to-all-start.1) | async-done | bytes 1048608 | tf_op jit(solution)/shard_map/all_to_all | solution.py:47
  121.8 0.1 copy.8
  121.9 18.3 %all-gather.2.cloned.1.call-done = f32[2,2048,256]{2,1,0:T(8,128)} async-done(((f32[2,256,256]{2,1,0:T(8,128)}), f32[2,2048,256]{2,1,0:T(8,128)}) %all-gather.2.cloned.1.call-update) | async-done | bytes 4194320 | tf_op jit(solution)/shard_map/all_gather | solution.py:52
  140.3 7.2 %fusion.2 = f32[8,256,2,256]{3,1,2,0:T(8,128)} fusion(f32[2,2,256,256,1]{3,2,0,1,4:T(8,128)S(1)} %bitcast.66, f32[2,8,256,256,1]{3,2,1,0,4:T(8,128)} %bitcast.64), kind=kOutput, calls=%fused_computation.5 | convolution fusion | flops 3221225472 | bytes 9437184 | tf_op jit(solution)/shard_map/fakm,fbjm->akbj/dot_general | solution.py:62
  147.5 5.0 %gather_fusion = f32[16,256,256]{2,1,0:T(8,128)} fusion(f32[8,256,2,256]{3,1,2,0:T(8,128)} %fusion.2, s32[16]{0:T(128)S(1)} %fusion.16), kind=kCustom, calls=%fused_computation | custom fusion | bytes 8388736 | tf_op jit(solution)/shard_map/gather | solution.py:63
  152.4 0.0 copy-start.1
  152.4 4.2 %bitcast_subtract_fusion = f32[16,256,256]{2,1,0:T(8,128)S(1)} fusion(f32[16,1,256,256]{3,2,1,0:T(8,128)} %param.5, f32[16,256,256]{2,1,0:T(8,128)} %gather_fusion, pred[16]{0:T(512)(128)(4,1)S(1)} %compare_bitcast_fusion), kind=kLoop, calls=%fused_computation.4 | loop fusion | flops 2097152 | bytes 12582928 | tf_op jit(solution)/shard_map/sub | solution.py:64
  156.7 0.4 copy-done.1
  157.1 0.3 slice_select_fusion.1
  157.4 0.4 slice_select_fusion
  157.8 2.4 %maximum_bitcast_fusion = f32[16,1,256,256]{3,2,1,0:T(8,128)} fusion(f32[8,256,256]{2,1,0:T(8,128)S(1)} %get-tuple-element.6, f32[8,256,256]{2,1,0:T(8,128)S(1)} %get-tuple-element.5), kind=kLoop, calls=%fused_computation.1 | loop fusion | flops 1048576 | bytes 8388608 | tf_op jit(solution)/shard_map/broadcast_in_dim | solution.py:70
  (6 shorter events, 0.1 us)
Async XLA Ops:
  6.5 15.8 %copy-start = (f32[256,256]{1,0:T(8,128)S(1)}, f32[256,256]{1,0:T(8,128)}, u32[]{:S(2)}) copy-start(f32[256,256]{1,0:T(8,128)} %param.9) | copy-start | bytes 786436
  6.5 15.1 %copy-start.4 = (s32[2,8]{1,0:T(2,128)S(1)}, s32[2,8]{1,0:T(2,128)}, u32[]{:S(2)}) copy-start(s32[2,8]{1,0:T(2,128)} %param.6) | copy-start | bytes 196
  6.5 15.8 %copy-start.2 = (f32[2,256,256]{2,1,0:T(8,128)S(1)}, f32[2,256,256]{2,1,0:T(8,128)}, u32[]{:S(2)}) copy-start(f32[2,256,256]{2,1,0:T(8,128)} %param.8) | copy-start | bytes 1572868
  9.7 60.4 %all-to-all-start = ((f32[32,64,256]{2,1,0:T(8,128)}), f32[32,64,256]{2,1,0:T(8,128)S(1)}, u32[]{:S(2)}, u32[]{:S(2)}) async-start(f32[32,64,256]{2,1,0:T(8,128)} %bitcast.2), calls=%async_computation | async-start | bytes 4194304 | tf_op jit(solution)/shard_map/all_to_all | solution.py:32
  21.5 85.2 %copy-start.3 = (s32[2,16,1]{1,2,0:T(1,128)S(1)}, s32[2,16,1]{1,2,0:T(1,128)}, u32[]{:S(2)}) copy-start(s32[2,16,1]{1,2,0:T(1,128)} %param.7) | copy-start | bytes 388
  21.5 118.7 %all-gather.2.cloned.1.call-start = ((), (), s32[]{:S(2)}) async-start(), calls=%async_computation.2 | async-start | bytes 4718592 | tf_op jit(solution)/shard_map/all_gather | solution.py:52
  86.2 8.6 %collective-permute-start = (f32[2,64,256]{2,1,0:T(8,128)S(1)}, f32[2,64,256]{2,1,0:T(8,128)S(1)}, u32[]{:S(2)}, u32[]{:S(2)}) collective-permute-start(f32[2,64,256]{2,1,0:T(8,128)S(1)} %pad_maximum_fusion), channel_id=1, source_target_pairs={{0,0},{1,32},{2,64},{3,96},{4,128},{5,160},{6,192},{7,224},{32,1},... | collective-permute-start | bytes 393224 | tf_op jit(solution)/shard_map/ppermute | solution.py:45
  95.9 25.9 %all-to-all-start.1 = ((f32[8,2,64,256]{3,2,1,0:T(8,128)}), f32[8,2,64,256]{3,2,1,0:T(8,128)S(1)}, u32[]{:S(2)}, u32[]{:S(2)}) async-start(f32[8,2,64,256]{3,2,1,0:T(8,128)} %broadcast_in_dim.44), calls=%async_computation.1 | async-start | bytes 2097152 | tf_op jit(solution)/shard_map/all_to_all | solution.py:47
  152.4 4.6 %copy-start.1 = (f32[2,2048,256]{2,1,0:T(8,128)S(1)}, f32[2,2048,256]{2,1,0:T(8,128)}, u32[]{:S(2)}) copy-start(f32[2,2048,256]{2,1,0:T(8,128)} %all-gather.2.cloned.1.call-done) | copy-start | bytes 12582916
Sparse Core Ops, SparseCore 0:
  86.3 53.9 all-gather.1

commit v6 on v5

--- a/solution.py
+++ b/solution.py
@@ -2,6 +2,8 @@
 import jax.numpy as jnp
 import numpy as np
 from jax import lax
+from jax.experimental import pallas as pl
+from jax.experimental.pallas import tpu as pltpu
 from jax.sharding import Mesh
 from jax.sharding import PartitionSpec as P
 
@@ -17,6 +19,32 @@
 
 def apply_inverse(panel_rows_block, inverse):
     return jnp.einsum("ab,cb->ac", panel_rows_block, inverse, precision=HIGHEST_PRECISION)
+
+
+def tail_kernel(table_ref, stored_ref, product_ref, panel_ref, out_ref):
+    slot = pl.program_id(0)
+    kept = stored_ref[...] - jnp.where(table_ref[2, slot] > 0, product_ref[...], 0.0)
+    out_ref[...] = jnp.where(table_ref[3, slot] > 0, panel_ref[...], kept)
+
+
+def finish_slots(table, stored, products, panels):
+    slots, block, _ = stored.shape
+    head = panels.shape[0] // 2
+    spec = pltpu.PrefetchScalarGridSpec(
+        num_scalar_prefetch=1,
+        grid=(slots,),
+        in_specs=[
+            pl.BlockSpec((1, block, block), lambda s, t: (s, 0, 0)),
+            pl.BlockSpec((1, block, block), lambda s, t: (t[0, s], 0, t[1, s])),
+            pl.BlockSpec(
+                (1, block, block), lambda s, t: (t[4, 0] * head + jnp.minimum(s, head - 1), 0, 0)
+            ),
+        ],
+        out_specs=pl.BlockSpec((1, block, block), lambda s, t: (s, 0, 0)),
+    )
+    return pl.pallas_call(
+        tail_kernel, grid_spec=spec, out_shape=jax.ShapeDtypeStruct(stored.shape, stored.dtype)
+    )(table, stored, products, panels)
 
 
 def per_device(blocks, panel_rows, target_slots, diag_inverse, cross_block):
@@ -51,22 +79,22 @@
     both_rows = lax.all_gather(both_pieces, "x", axis=1, tiled=True)
     both_rows = lax.all_gather(both_rows, ("zh", "zl"), axis=1, tiled=True)
     both_rows = both_rows.reshape(2, slot_count, block, block)
-    first_rows = both_rows[0]
-    second_rows = both_rows[1]
     class_start = column // row_count * PER_CLASS
     row_index = target_slots[0, :, 0]
     col_index = target_slots[1, :, 0]
     present = row_index >= 0
-    left_slot = jnp.where(present, row_index, 0)
-    right_slot = jnp.where(present, col_index - class_start, 0)
+    left_slot = jnp.clip(jnp.where(present, row_index, 0), 0, slot_count - 1)
+    right_slot = jnp.clip(jnp.where(present, col_index - class_start, 0), 0, PER_CLASS - 1)
     products = jnp.einsum("fakm,fbjm->akbj", both_rows, both_cols, precision=PRODUCT_PRECISION)
-    schur_term = products[left_slot, :, right_slot, :]
-    trailing = stored - jnp.where(present[:, None, None], schur_term, 0.0)
+    products = products.reshape(slot_count, block, PER_CLASS * block)
     head_live = panel_rows >= 0
-    keep_mask = ((column == 0) & head_live[0] | (column == 1) & head_live[1])[:, None, None]
-    own_panel = jnp.where(column == 0, first_rows, second_rows)
-    head_blocks = jnp.where(keep_mask, own_panel, trailing[:slot_count])
-    factored = jnp.concatenate([head_blocks, trailing[slot_count:]], axis=0)
+    keep_head = (column == 0) & head_live[0] | (column == 1) & head_live[1]
+    slots = stored.shape[0]
+    keep = jnp.zeros((slots,), jnp.bool_).at[:slot_count].set(keep_head)
+    panel_column = jnp.full((slots,), column == 1)
+    table = jnp.stack([left_slot, right_slot, present, keep, panel_column]).astype(jnp.int32)
+    panels = both_rows.reshape(2 * slot_count, block, block)
+    factored = finish_slots(table, stored, products, panels)
     return factored[:, None]
 
 

time: 167 us -> 167 us (level)
  Pallas kernels: 0 us -> 11.5 us
  other arithmetic: 8.07 us -> 0.7 us
  local copies, waits for them, and re-layouts: 9.68 us -> 4.92 us
    pallas_call x0 -> x1, Pallas kernels: none -> 11.5 us  [finish_slots(): pl.pallas_call(tail_kernel, grid_spec=spec, out_shape=jax.ShapeDtypeStruc...]
    gather x1 -> x0, local copies, waits for them, and re-layouts: 4.97 us -> none  [per_device(): schur_term = products[left_slot, :, right_slot, :]]
    sub x1 -> x0, other arithmetic: 4.23 us -> none  [per_device(): trailing = stored - jnp.where(present[:, None, None], schur_term, 0.0)]
    broadcast_in_dim x1 -> x0, other arithmetic: 2.44 us -> none  [per_device(): return factored[:, None]]
  transfers between devices with their start and end apart: 4 -> 4, of which waited for: 4 -> 4; matrix products, arithmetic and copies ran while one was open for 1% -> 2% of each run, Pallas kernels for 0% -> 0%
where the time goes in v6:
time: 167 us; the launch traced here: 166 us
  waiting for transfers between devices  82.7 us (50%)
  starting transfers between devices  28.7 us (17%)
  blocking collectives  13.8 us (8%)
  between operations  13.5 us (8%)
  Pallas kernels  11.5 us (7%)
  matrix products  10.1 us (6%)
  local copies, waits for them, and re-layouts  4.92 us (3%)
    all_to_all x1, waiting for transfers between devices, per_device(): received = lax.all_to_all(pieces, COL_AXES, 0, 0, tiled=True)  47.3 us
    all_gather x1, waiting for transfers between devices, per_device(): both_rows = lax.all_gather(both_rows, ('zh', 'zl'), axis=1, tiled=True)  18.3 us
    all_to_all x1, waiting for transfers between devices, per_device(): class_pieces = lax.all_to_all(spread, 'row', 0, 0, tiled=True)  14.4 us
    all_gather x1, blocking collectives, per_device(): both_rows = lax.all_gather(both_pieces, 'x', axis=1, tiled=True)  13.8 us
    all_to_all x1, starting transfers between devices, per_device(): received = lax.all_to_all(pieces, COL_AXES, 0, 0, tiled=True)  11.9 us
    pallas_call x1, Pallas kernels, finish_slots(): pl.pallas_call(tail_kernel, grid_spec=spec, out_shape=jax.ShapeDtypeStruc...  11.5 us
    all_to_all x1, starting transfers between devices, per_device(): class_pieces = lax.all_to_all(spread, 'row', 0, 0, tiled=True)  10.9 us
    dot_general x1, matrix products, per_device(): jnp.einsum('fakm,fbjm->akbj', both_rows, both_cols, precision=PRODUCT_PRE...  7.29 us
  transfers between devices with their start and end apart: 4, of which 4 were waited for; matrix products, arithmetic and copies ran while one was open for 2% of the time, Pallas kernels for 0%

profile of v6, /device:TPU:1, one launch (start us, length us, event | category | flops | bytes accessed | tf_op | source)
XLA Modules:
  0.0 165.9 jit_solution(8243003236715704631)
XLA Ops:
  6.5 0.0 copy-start
  6.5 0.0 copy-start.2
  6.5 0.0 copy-start.1
  6.5 3.1 %slice.51 = f32[8,1,256,256]{3,2,1,0:T(8,128)} slice(f32[16,1,256,256]{3,2,1,0:T(8,128)} %param.7), slice={[0:8], [0:1], [0:256], [0:256]} | slice | bytes 4194304 | tf_op jit(solution)/shard_map/slice | solution.py:57
  9.7 11.9 %all-to-all-start = ((f32[32,64,256]{2,1,0:T(8,128)}), f32[32,64,256]{2,1,0:T(8,128)S(1)}, u32[]{:S(2)}, u32[]{:S(2)}) async-start(f32[32,64,256]{2,1,0:T(8,128)} %bitcast.6), calls=%async_computation | async-start | bytes 4194304 | tf_op jit(solution)/shard_map/all_to_all | solution.py:60
  21.5 0.0 copy-start.3
  21.5 0.0 all-gather.2.cloned.1.call-start
  21.6 0.0 copy-done.2
  21.6 0.7 fusion.12
  22.3 0.0 copy-done
  22.3 0.0 copy-done.1
  22.3 0.4 fusion.2
  22.7 47.3 %all-to-all-done = f32[32,64,256]{2,1,0:T(8,128)S(1)} async-done(((f32[32,64,256]{2,1,0:T(8,128)}), f32[32,64,256]{2,1,0:T(8,128)S(1)}, u32[]{:S(2)}, u32[]{:S(2)}) %all-to-all-start) | async-done | bytes 2097184 | tf_op jit(solution)/shard_map/all_to_all | solution.py:60
  70.0 1.0 convolution_select_fusion.1
  71.0 0.4 convolution_subtract_fusion
  71.4 1.0 fusion
  72.4 13.8 %all_gather.6 = f32[2,256,256]{2,1,0:T(8,128)} all-gather(f32[2,64,256]{2,1,0:T(8,128)S(1)} %pad_maximum_fusion), channel_id=1, replica_groups=mesh['row'=8,'zh'=4,'zl'=2,'x'=4] {'x'}, dimensions={1}, use_global_device_ids=true | all-gather | bytes 655360 | tf_op jit(solution)/shard_map/all_gather | solution.py:79
  86.2 0.0 all-gather.2.cloned.1.call-update
  86.2 6.0 %collective-permute-start = (f32[2,64,256]{2,1,0:T(8,128)S(1)}, f32[2,64,256]{2,1,0:T(8,128)S(1)}, u32[]{:S(2)}, u32[]{:S(2)}) collective-permute-start(f32[2,64,256]{2,1,0:T(8,128)S(1)} %pad_maximum_fusion), channel_id=1, source_target_pairs={{0,0},{1,32},{2,64},{3,96},{4,128},{5,160},{6,192},{7,224},{32,1},... | collective-permute-start | bytes 393224 | tf_op jit(solution)/shard_map/ppermute | solution.py:73
  92.2 2.6 %collective-permute-done = f32[2,64,256]{2,1,0:T(8,128)S(1)} collective-permute-done((f32[2,64,256]{2,1,0:T(8,128)S(1)}, f32[2,64,256]{2,1,0:T(8,128)S(1)}, u32[]{:S(2)}, u32[]{:S(2)}) %collective-permute-start) | collective-permute-done | bytes 131104 | tf_op jit(solution)/shard_map/ppermute | solution.py:73
  94.8 1.1 broadcast_in_dim.19
  95.9 10.9 %all-to-all-start.1 = ((f32[8,2,64,256]{3,2,1,0:T(8,128)}), f32[8,2,64,256]{3,2,1,0:T(8,128)S(1)}, u32[]{:S(2)}, u32[]{:S(2)}) async-start(f32[8,2,64,256]{3,2,1,0:T(8,128)} %broadcast_in_dim.19), calls=%async_computation.1 | async-start | bytes 2097152 | tf_op jit(solution)/shard_map/all_to_all | solution.py:75
  106.8 0.0 copy-done.3
  106.8 0.6 stack.27.table_ref
  107.4 14.4 %all-to-all-done.1 = f32[8,2,64,256]{3,2,1,0:T(8,128)S(1)} async-done(((f32[8,2,64,256]{3,2,1,0:T(8,128)}), f32[8,2,64,256]{3,2,1,0:T(8,128)S(1)}, u32[]{:S(2)}, u32[]{:S(2)}) %all-to-all-start.1) | async-done | bytes 1048608 | tf_op jit(solution)/shard_map/all_to_all | solution.py:75
  121.8 0.1 copy.8
  121.9 18.3 %all-gather.2.cloned.1.call-done = f32[2,2048,256]{2,1,0:T(8,128)} async-done(((f32[2,256,256]{2,1,0:T(8,128)}), f32[2,2048,256]{2,1,0:T(8,128)}) %all-gather.2.cloned.1.call-update) | async-done | bytes 4194320 | tf_op jit(solution)/shard_map/all_gather | solution.py:80
  140.3 7.3 %convolution_bitcast_fusion.product_ref = f32[8,256,512]{2,1,0:T(8,128)} fusion(f32[2,8,256,256]{3,2,1,0:T(8,128)} %bitcast.57, f32[512,2,256,1]{2,0,3,1:T(8,128)S(1)} %bitcast.60), kind=kOutput, calls=%fused_computation | convolution fusion | flops 3221225472 | bytes 9437184 | tf_op jit(solution)/shard_map/fakm,fbjm->akbj/dot_general | solution.py:88
  147.6 11.5 %shard_map.55 = f32[16,256,256]{2,1,0:T(8,128)} custom-call(s32[5,16]{1,0:T(8,128)} %stack.27.table_ref, f32[16,256,256]{2,1,0:T(8,128)} %bitcast.59, f32[8,256,512]{2,1,0:T(8,128)} %convolution_bitcast_fusion.product_ref, f32[16,256,256]{2,1,0:T(8,128)} %bitcast.58), custom_call_target="tpu_custom_call" | custom-call | tf_op jit(solution)/shard_map/pallas_call | solution.py:45
  (8 shorter events, 0.1 us)
Async XLA Ops:
  6.5 15.8 %copy-start = (f32[256,256]{1,0:T(8,128)S(1)}, f32[256,256]{1,0:T(8,128)}, u32[]{:S(2)}) copy-start(f32[256,256]{1,0:T(8,128)} %param.11) | copy-start | bytes 786436
  6.5 15.1 %copy-start.2 = (s32[2,8]{1,0:T(2,128)S(1)}, s32[2,8]{1,0:T(2,128)}, u32[]{:S(2)}) copy-start(s32[2,8]{1,0:T(2,128)} %param.8) | copy-start | bytes 196
  6.5 15.8 %copy-start.1 = (f32[2,256,256]{2,1,0:T(8,128)S(1)}, f32[2,256,256]{2,1,0:T(8,128)}, u32[]{:S(2)}) copy-start(f32[2,256,256]{2,1,0:T(8,128)} %param.10) | copy-start | bytes 1572868
  9.7 60.4 %all-to-all-start = ((f32[32,64,256]{2,1,0:T(8,128)}), f32[32,64,256]{2,1,0:T(8,128)S(1)}, u32[]{:S(2)}, u32[]{:S(2)}) async-start(f32[32,64,256]{2,1,0:T(8,128)} %bitcast.6), calls=%async_computation | async-start | bytes 4194304 | tf_op jit(solution)/shard_map/all_to_all | solution.py:60
  21.5 85.2 %copy-start.3 = (s32[2,16,1]{1,2,0:T(1,128)S(1)}, s32[2,16,1]{1,2,0:T(1,128)}, u32[]{:S(2)}) copy-start(s32[2,16,1]{1,2,0:T(1,128)} %param.9) | copy-start | bytes 388
  21.5 118.7 %all-gather.2.cloned.1.call-start = ((), (), s32[]{:S(2)}) async-start(), calls=%async_computation.2 | async-start | bytes 4718592 | tf_op jit(solution)/shard_map/all_gather | solution.py:80
  86.2 8.6 %collective-permute-start = (f32[2,64,256]{2,1,0:T(8,128)S(1)}, f32[2,64,256]{2,1,0:T(8,128)S(1)}, u32[]{:S(2)}, u32[]{:S(2)}) collective-permute-start(f32[2,64,256]{2,1,0:T(8,128)S(1)} %pad_maximum_fusion), channel_id=1, source_target_pairs={{0,0},{1,32},{2,64},{3,96},{4,128},{5,160},{6,192},{7,224},{32,1},... | collective-permute-start | bytes 393224 | tf_op jit(solution)/shard_map/ppermute | solution.py:73
  95.9 26.0 %all-to-all-start.1 = ((f32[8,2,64,256]{3,2,1,0:T(8,128)}), f32[8,2,64,256]{3,2,1,0:T(8,128)S(1)}, u32[]{:S(2)}, u32[]{:S(2)}) async-start(f32[8,2,64,256]{3,2,1,0:T(8,128)} %broadcast_in_dim.19), calls=%async_computation.1 | async-start | bytes 2097152 | tf_op jit(solution)/shard_map/all_to_all | solution.py:75
Sparse Core Ops, SparseCore 0:
  86.3 53.9 all-gather.1

commit v7 on v6

--- a/solution.py
+++ b/solution.py
@@ -9,6 +9,7 @@
 
 PER_CLASS = 2
 X_SIZE = 4
+HALVES = 2
 
 
 HIGHEST_PRECISION = lax.Precision.HIGHEST
@@ -57,28 +58,34 @@
     head_part = stored[:slot_count]
     chunk = slot_count * block // col_count
     pieces = head_part.reshape(col_count, chunk, block)
-    received = lax.all_to_all(pieces, COL_AXES, 0, 0, tiled=True)
-    zero_rows = received[0]
-    one_rows = received[1]
     piece_slot = column * chunk // block
     first_live = lax.dynamic_index_in_dim(panel_rows[0], piece_slot, keepdims=False) >= 0
     second_live = lax.dynamic_index_in_dim(panel_rows[1], piece_slot, keepdims=False) >= 0
     cross_factor = jnp.dot(cross_block, diag_inverse[0].T, precision=HIGHEST_PRECISION)
-    first_piece = jnp.where(first_live, apply_inverse(zero_rows, diag_inverse[0]), 0.0)
-    updated_piece = one_rows - apply_inverse(first_piece, cross_factor)
-    second_piece = jnp.where(second_live, apply_inverse(updated_piece, diag_inverse[1]), 0.0)
-    both_pieces = jnp.stack([first_piece, second_piece])
     class_size = lax.axis_size(CLASS_AXES)
     swap = [(a * class_size + b, b * class_size + a) for a in range(row_count) for b in range(class_size)]
-    swapped = lax.ppermute(both_pieces, ("row",) + CLASS_AXES, swap)
-    spread = jnp.broadcast_to(swapped[None], (row_count,) + swapped.shape)
-    class_pieces = lax.all_to_all(spread, "row", 0, 0, tiled=True)
+    half = chunk // HALVES
+    row_parts = []
+    col_parts = []
+    for part in range(HALVES):
+        received = lax.all_to_all(pieces[:, part * half:(part + 1) * half], COL_AXES, 0, 0, tiled=True)
+        zero_rows = received[0]
+        one_rows = received[1]
+        first_piece = jnp.where(first_live, apply_inverse(zero_rows, diag_inverse[0]), 0.0)
+        updated_piece = one_rows - apply_inverse(first_piece, cross_factor)
+        second_piece = jnp.where(second_live, apply_inverse(updated_piece, diag_inverse[1]), 0.0)
+        both_pieces = jnp.stack([first_piece, second_piece])
+        swapped = lax.ppermute(both_pieces, ("row",) + CLASS_AXES, swap)
+        spread = jnp.broadcast_to(swapped[None], (row_count,) + swapped.shape)
+        col_parts.append(lax.all_to_all(spread, "row", 0, 0, tiled=True))
+        gathered = lax.all_gather(both_pieces, "x", axis=1, tiled=True)
+        row_parts.append(lax.all_gather(gathered, ("zh", "zl"), axis=1, tiled=True))
     per_slot = block // chunk
-    class_pieces = class_pieces.reshape(PER_CLASS, per_slot, 2, chunk, block)
+    both_rows = jnp.stack(
+        [part.reshape(2, slot_count, per_slot, half, block) for part in row_parts], axis=3
+    ).reshape(2, slot_count, block, block)
+    class_pieces = jnp.stack(col_parts, axis=2).reshape(PER_CLASS, per_slot, 2, chunk, block)
     both_cols = class_pieces.transpose(2, 0, 1, 3, 4).reshape(2, PER_CLASS, block, block)
-    both_rows = lax.all_gather(both_pieces, "x", axis=1, tiled=True)
-    both_rows = lax.all_gather(both_rows, ("zh", "zl"), axis=1, tiled=True)
-    both_rows = both_rows.reshape(2, slot_count, block, block)
     class_start = column // row_count * PER_CLASS
     row_index = target_slots[0, :, 0]
     col_index = target_slots[1, :, 0]

time: 167 us -> 195 us (1.17)
  blocking collectives: 13.8 us -> 55.7 us
  waiting for transfers between devices: 82.7 us -> 42.4 us
  starting transfers between devices: 28.7 us -> 47.6 us
  matrix products: 10.1 us -> 13 us
  other arithmetic: 0.7 us -> 3.34 us
  local copies, waits for them, and re-layouts: 4.92 us -> 7.32 us
    all_to_all x0 -> x1, blocking collectives: none -> 31.7 us  [per_device(): lax.all_to_all(pieces[:, part * half:(part + 1) * half], COL_AXES, 0, 0,...]
    all_to_all x2 -> x3, waiting for transfers between devices: 61.7 us -> 36.5 us  [the longest x1 24.1 us: per_device(): lax.all_to_all(pieces[:, part * half:(part + 1) * half], COL_AXES, 0, 0,...]
    all_gather x1 -> x2, waiting for transfers between devices: 18.3 us -> 0.04 us  [per_device(): row_parts.append(lax.all_gather(gathered, ('zh', 'zl'), axis=1, tiled=True))]
    ppermute x1 -> x2, starting transfers between devices: 5.96 us -> 17.8 us  [per_device(): swapped = lax.ppermute(both_pieces, ('row',) + CLASS_AXES, swap)]
    all_gather x1 -> x2, blocking collectives: 13.8 us -> 24 us  [per_device(): gathered = lax.all_gather(both_pieces, 'x', axis=1, tiled=True)]
    all_to_all x2 -> x3, starting transfers between devices: 22.7 us -> 29.7 us  [the longest x2 17.7 us: per_device(): col_parts.append(lax.all_to_all(spread, 'row', 0, 0, tiled=True))]
    dot_general x3 -> x6, matrix products: 2.36 us -> 6.59 us  [apply_inverse(): jnp.einsum('ab,cb->ac', panel_rows_block, inverse, precision=HIGHEST_PREC...]
    ppermute x1 -> x2, waiting for transfers between devices: 2.63 us -> 5.88 us  [per_device(): swapped = lax.ppermute(both_pieces, ('row',) + CLASS_AXES, swap)]
  transfers between devices with their start and end apart: 4 -> 7, of which waited for: 4 -> 5; matrix products, arithmetic and copies ran while one was open for 2% -> 4% of each run, Pallas kernels for 0% -> 0%
where the time goes in v7:
time: 195 us
  blocking collectives  55.7 us (29%)
  starting transfers between devices  47.6 us (24%)
  waiting for transfers between devices  42.4 us (22%)
  between operations  13.6 us (7%)
  matrix products  13 us (7%)
  Pallas kernels  11.5 us (6%)
  local copies, waits for them, and re-layouts  7.32 us (4%)
  other arithmetic  3.34 us (2%)
    all_to_all x1, blocking collectives, per_device(): lax.all_to_all(pieces[:, part * half:(part + 1) * half], COL_AXES, 0, 0,...  31.7 us
    all_to_all x1, waiting for transfers between devices, per_device(): lax.all_to_all(pieces[:, part * half:(part + 1) * half], COL_AXES, 0, 0,...  24.1 us
    all_gather x2, blocking collectives, per_device(): gathered = lax.all_gather(both_pieces, 'x', axis=1, tiled=True)  24 us
    ppermute x2, starting transfers between devices, per_device(): swapped = lax.ppermute(both_pieces, ('row',) + CLASS_AXES, swap)  17.8 us
    all_to_all x2, starting transfers between devices, per_device(): col_parts.append(lax.all_to_all(spread, 'row', 0, 0, tiled=True))  17.7 us
    all_to_all x2, waiting for transfers between devices, per_device(): col_parts.append(lax.all_to_all(spread, 'row', 0, 0, tiled=True))  12.4 us
    all_to_all x1, starting transfers between devices, per_device(): lax.all_to_all(pieces[:, part * half:(part + 1) * half], COL_AXES, 0, 0,...  12 us
    pallas_call x1, Pallas kernels, finish_slots(): pl.pallas_call(tail_kernel, grid_spec=spec, out_shape=jax.ShapeDtypeStruc...  11.5 us
  transfers between devices with their start and end apart: 7, of which 5 were waited for; matrix products, arithmetic and copies ran while one was open for 4% of the time, Pallas kernels for 0%

profile of v7, /device:TPU:1, one launch (start us, length us, event | category | flops | bytes accessed | tf_op | source)
XLA Modules:
  0.0 194.5 jit_solution(5140739295231607545)
XLA Ops:
  6.5 0.0 copy-start
  6.5 0.0 slice-start
  6.5 0.0 copy-start.3
  6.5 1.7 slice-done
  8.2 1.2 fusion.16
  9.4 12.0 %all-to-all-start = ((f32[32,32,256]{2,1,0:T(8,128)}), f32[32,32,256]{2,1,0:T(8,128)S(1)}, u32[]{:S(2)}, u32[]{:S(2)}) async-start(f32[32,32,256]{2,1,0:T(8,128)} %get-tuple-element.17), calls=%async_computation | async-start | bytes 2097152 | tf_op jit(solution)/shard_map/all_to_all | solution.py:71
  21.4 0.0 all-gather.3.cloned.1.call-start
  21.5 0.0 copy-done.3
  21.5 0.7 fusion.18
  22.2 0.0 copy-done
  22.2 1.4 fusion.5
  23.6 24.1 %all-to-all-done = f32[32,32,256]{2,1,0:T(8,128)S(1)} async-done(((f32[32,32,256]{2,1,0:T(8,128)}), f32[32,32,256]{2,1,0:T(8,128)S(1)}, u32[]{:S(2)}, u32[]{:S(2)}) %all-to-all-start) | async-done | bytes 1048608 | tf_op jit(solution)/shard_map/all_to_all | solution.py:71
  47.6 2.0 %convolution_select_fusion.3 = f32[32,256]{1,0:T(8,128)S(1)} fusion(f32[2,256,256]{2,1,0:T(8,128)} %param.10, f32[32,32,256]{2,1,0:T(8,128)S(1)} %all-to-all-done, pred[]{:T(512)} %bitcast.5), kind=kOutput, calls=%fused_computation.9 | convolution fusion | flops 25174016 | bytes 328192 | tf_op jit(solution)/shard_map/ab,cb->ac/dot_general | solution.py:22
  49.6 0.3 convolution_subtract_fusion.1
  50.0 0.0 copy-start.4
  50.0 1.9 fusion.1
  51.9 11.2 %all_gather.12 = f32[2,128,256]{2,1,0:T(8,128)} all-gather(f32[2,32,256]{2,1,0:T(8,128)S(1)} %pad_maximum_fusion.2), channel_id=1, replica_groups=mesh['row'=8,'zh'=4,'zl'=2,'x'=4] {'x'}, dimensions={1}, use_global_device_ids=true | all-gather | bytes 327680 | tf_op jit(solution)/shard_map/all_gather | solution.py:81
  63.1 0.0 all-gather.3.cloned.1.call-update
  63.1 0.0 all-gather.5.cloned.1.call-start
  63.2 31.7 %all_to_all.20 = f32[32,32,256]{2,1,0:T(8,128)S(1)} all-to-all(f32[32,32,256]{2,1,0:T(8,128)S(1)} %get-tuple-element.18), channel_id=1, replica_groups=mesh['row'=8,'zh'=4,'zl'=2,'x'=4] {'zh','zl','x'}, dimensions={0} | all-to-all | bytes 2097152 | tf_op jit(solution)/shard_map/all_to_all | solution.py:71
  94.9 0.0 copy-done.2
  94.9 1.0 convolution_select_fusion.1
  95.9 0.3 convolution_subtract_fusion
  96.3 1.0 fusion
  97.3 12.8 %all_gather.14 = f32[2,128,256]{2,1,0:T(8,128)} all-gather(f32[2,32,256]{2,1,0:T(8,128)S(1)} %pad_maximum_fusion.3), channel_id=1, replica_groups=mesh['row'=8,'zh'=4,'zl'=2,'x'=4] {'x'}, dimensions={1}, use_global_device_ids=true | all-gather | bytes 327680 | tf_op jit(solution)/shard_map/all_gather | solution.py:81
  110.1 0.0 all-gather.5.cloned.1.call-update
  110.1 15.9 %collective-permute-start = (f32[2,32,256]{2,1,0:T(8,128)S(1)}, f32[2,32,256]{2,1,0:T(8,128)S(1)}, u32[]{:S(2)}, u32[]{:S(2)}) collective-permute-start(f32[2,32,256]{2,1,0:T(8,128)S(1)} %pad_maximum_fusion.2), channel_id=1, source_target_pairs={{0,0},{1,32},{2,64},{3,96},{4,128},{5,160},{6,192},{7,224},{32,1},... | collective-permute-start | bytes 196616 | tf_op jit(solution)/shard_map/ppermute | solution.py:78
  126.1 1.9 %collective-permute-done = f32[2,32,256]{2,1,0:T(8,128)S(1)} collective-permute-done((f32[2,32,256]{2,1,0:T(8,128)S(1)}, f32[2,32,256]{2,1,0:T(8,128)S(1)}, u32[]{:S(2)}, u32[]{:S(2)}) %collective-permute-start) | collective-permute-done | bytes 65568 | tf_op jit(solution)/shard_map/ppermute | solution.py:78
  128.0 0.8 broadcast_in_dim.27
  128.8 11.0 %all-to-all-start.2 = ((f32[8,2,32,256]{3,2,1,0:T(8,128)}), f32[8,2,32,256]{3,2,1,0:T(8,128)S(1)}, u32[]{:S(2)}, u32[]{:S(2)}) async-start(f32[8,2,32,256]{3,2,1,0:T(8,128)} %broadcast_in_dim.27), calls=%async_computation.2 | async-start | bytes 1048576 | tf_op jit(solution)/shard_map/all_to_all | solution.py:80
  139.8 1.9 collective-permute-start.1
  141.8 3.9 %collective-permute-done.1 = f32[2,32,256]{2,1,0:T(8,128)S(1)} collective-permute-done((f32[2,32,256]{2,1,0:T(8,128)S(1)}, f32[2,32,256]{2,1,0:T(8,128)S(1)}, u32[]{:S(2)}, u32[]{:S(2)}) %collective-permute-start.1) | collective-permute-done | bytes 65568 | tf_op jit(solution)/shard_map/ppermute | solution.py:78
  145.7 3.6 %all-to-all-done.2 = f32[8,2,32,256]{3,2,1,0:T(8,128)S(1)} async-done(((f32[8,2,32,256]{3,2,1,0:T(8,128)}), f32[8,2,32,256]{3,2,1,0:T(8,128)S(1)}, u32[]{:S(2)}, u32[]{:S(2)}) %all-to-all-start.2) | async-done | bytes 524320 | tf_op jit(solution)/shard_map/all_to_all | solution.py:80
  149.3 0.8 broadcast_in_dim.28
  150.2 6.7 %all-to-all-start.3 = ((f32[8,2,32,256]{3,2,1,0:T(8,128)}), f32[8,2,32,256]{3,2,1,0:T(8,128)S(1)}, u32[]{:S(2)}, u32[]{:S(2)}) async-start(f32[8,2,32,256]{3,2,1,0:T(8,128)} %broadcast_in_dim.28), calls=%async_computation.3 | async-start | bytes 1048576 | tf_op jit(solution)/shard_map/all_to_all | solution.py:80
  156.9 0.0 copy-done.4
  156.9 0.6 stack.48.table_ref
  157.5 8.8 %all-to-all-done.3 = f32[8,2,32,256]{3,2,1,0:T(8,128)S(1)} async-done(((f32[8,2,32,256]{3,2,1,0:T(8,128)}), f32[8,2,32,256]{3,2,1,0:T(8,128)S(1)}, u32[]{:S(2)}, u32[]{:S(2)}) %all-to-all-start.3) | async-done | bytes 524320 | tf_op jit(solution)/shard_map/all_to_all | solution.py:80
  166.4 0.1 pad_maximum_fusion.1
  166.4 0.1 copy.21
  166.5 0.0 all-gather.3.cloned.1.call-done
  166.6 0.0 all-gather.5.cloned.1.call-done
  166.6 2.5 %pad_maximum_fusion = f32[2,8,4,2,32,256]{5,4,3,2,1,0:T(8,128)S(1)} fusion(f32[2,8,4,1,32,256]{5,4,3,2,1,0:T(8,128)} %bitcast.90, f32[2,8,4,1,32,256]{5,4,3,2,1,0:T(8,128)} %bitcast.89), kind=kLoop, calls=%fused_computation | loop fusion | flops 1048576 | bytes 8388608 | tf_op jit(solution)/shard_map/stack | solution.py:84
  169.2 0.0 copy-start.1
  169.2 0.6 copy.20
  169.8 1.5 copy-done.1
  171.2 5.0 %convolution_bitcast_fusion.product_ref = f32[8,256,512]{2,1,0:T(8,128)} fusion(f32[2,8,256,256]{3,2,0,1:T(8,128)S(1)} %bitcast.82, f32[512,2,256,1]{2,0,1,3:T(8,128)S(1)} %bitcast.85), kind=kOutput, calls=%fused_computation.1 | convolution fusion | flops 3221225472 | bytes 9437184 | tf_op jit(solution)/shard_map/fakm,fbjm->akbj/dot_general | solution.py:95
  176.2 11.5 %shard_map.55 = f32[16,256,256]{2,1,0:T(8,128)} custom-call(s32[5,16]{1,0:T(8,128)} %stack.48.table_ref, f32[16,256,256]{2,1,0:T(8,128)} %bitcast.83, f32[8,256,512]{2,1,0:T(8,128)} %convolution_bitcast_fusion.product_ref, f32[16,256,256]{2,1,0:T(8,128)} %bitcast.81), custom_call_target="tpu_custom_call" | custom-call | tf_op jit(solution)/shard_map/pallas_call | solution.py:46
  (10 shorter events, 0.1 us)
Async XLA Ops:
  6.5 15.6 %copy-start = (f32[256,256]{1,0:T(8,128)S(1)}, f32[256,256]{1,0:T(8,128)}, u32[]{:S(2)}) copy-start(f32[256,256]{1,0:T(8,128)} %param.11) | copy-start | bytes 786436
  6.5 1.7 slice-start
  6.5 14.9 %copy-start.3 = (s32[2,8]{1,0:T(2,128)S(1)}, s32[2,8]{1,0:T(2,128)}, u32[]{:S(2)}) copy-start(s32[2,8]{1,0:T(2,128)} %param.8) | copy-start | bytes 196
  9.4 85.5 %copy-start.2 = (f32[2,256,256]{2,1,0:T(8,128)S(1)}, f32[2,256,256]{2,1,0:T(8,128)}, u32[]{:S(2)}) copy-start(f32[2,256,256]{2,1,0:T(8,128)} %param.10) | copy-start | bytes 1572868
  9.4 38.2 %all-to-all-start = ((f32[32,32,256]{2,1,0:T(8,128)}), f32[32,32,256]{2,1,0:T(8,128)S(1)}, u32[]{:S(2)}, u32[]{:S(2)}) async-start(f32[32,32,256]{2,1,0:T(8,128)} %get-tuple-element.17), calls=%async_computation | async-start | bytes 2097152 | tf_op jit(solution)/shard_map/all_to_all | solution.py:71
  21.4 145.2 %all-gather.3.cloned.1.call-start = ((), (), s32[]{:S(2)}) async-start(), calls=%async_computation.4 | async-start | bytes 2359296 | tf_op jit(solution)/shard_map/all_gather | solution.py:82
  50.0 106.9 %copy-start.4 = (s32[2,16,1]{1,2,0:T(1,128)S(1)}, s32[2,16,1]{1,2,0:T(1,128)}, u32[]{:S(2)}) copy-start(s32[2,16,1]{1,2,0:T(1,128)} %param.9) | copy-start | bytes 388
  63.1 103.5 %all-gather.5.cloned.1.call-start = ((), (), s32[]{:S(2)}) async-start(), calls=%async_computation.5 | async-start | bytes 2359296 | tf_op jit(solution)/shard_map/all_gather | solution.py:82
  110.1 17.9 %collective-permute-start = (f32[2,32,256]{2,1,0:T(8,128)S(1)}, f32[2,32,256]{2,1,0:T(8,128)S(1)}, u32[]{:S(2)}, u32[]{:S(2)}) collective-permute-start(f32[2,32,256]{2,1,0:T(8,128)S(1)} %pad_maximum_fusion.2), channel_id=1, source_target_pairs={{0,0},{1,32},{2,64},{3,96},{4,128},{5,160},{6,192},{7,224},{32,1},... | collective-permute-start | bytes 196616 | tf_op jit(solution)/shard_map/ppermute | solution.py:78
  128.8 20.5 %all-to-all-start.2 = ((f32[8,2,32,256]{3,2,1,0:T(8,128)}), f32[8,2,32,256]{3,2,1,0:T(8,128)S(1)}, u32[]{:S(2)}, u32[]{:S(2)}) async-start(f32[8,2,32,256]{3,2,1,0:T(8,128)} %broadcast_in_dim.27), calls=%async_computation.2 | async-start | bytes 1048576 | tf_op jit(solution)/shard_map/all_to_all | solution.py:80
  139.8 5.9 %collective-permute-start.1 = (f32[2,32,256]{2,1,0:T(8,128)S(1)}, f32[2,32,256]{2,1,0:T(8,128)S(1)}, u32[]{:S(2)}, u32[]{:S(2)}) collective-permute-start(f32[2,32,256]{2,1,0:T(8,128)S(1)} %pad_maximum_fusion.3), channel_id=1, source_target_pairs={{0,0},{1,32},{2,64},{3,96},{4,128},{5,160},{6,192},{7,224},{32,1},... | collective-permute-start | bytes 196616 | tf_op jit(solution)/shard_map/ppermute | solution.py:78
  150.2 16.2 %all-to-all-start.3 = ((f32[8,2,32,256]{3,2,1,0:T(8,128)}), f32[8,2,32,256]{3,2,1,0:T(8,128)S(1)}, u32[]{:S(2)}, u32[]{:S(2)}) async-start(f32[8,2,32,256]{3,2,1,0:T(8,128)} %broadcast_in_dim.28), calls=%async_computation.3 | async-start | bytes 1048576 | tf_op jit(solution)/shard_map/all_to_all | solution.py:80
  169.2 2.0 %copy-start.1 = (f32[2,8,4,2,32,256]{5,4,3,2,1,0:T(8,128)}, f32[2,8,4,2,32,256]{5,4,3,2,1,0:T(8,128)S(1)}, u32[]{:S(2)}) copy-start(f32[2,8,4,2,32,256]{5,4,3,2,1,0:T(8,128)S(1)} %pad_maximum_fusion) | copy-start | bytes 12582916
Sparse Core Ops, SparseCore 0:
  63.3 52.7 all-gather.2
  117.9 39.9 all-gather.4

commit v8 on v6

--- a/solution.py
+++ b/solution.py
@@ -12,7 +12,7 @@
 
 
 HIGHEST_PRECISION = lax.Precision.HIGHEST
-PRODUCT_PRECISION = lax.Precision.HIGH
+TRANSPOSED_RIGHT = (((1,), (1,)), ((), ()))
 COL_AXES = ("zh", "zl", "x")
 CLASS_AXES = ("zl", "x")
 
@@ -21,30 +21,41 @@
     return jnp.einsum("ab,cb->ac", panel_rows_block, inverse, precision=HIGHEST_PRECISION)
 
 
-def tail_kernel(table_ref, stored_ref, product_ref, panel_ref, out_ref):
+def tail_kernel(table_ref, stored_ref, left_one, left_two, right_one, right_two, panel_ref, out_ref):
     slot = pl.program_id(0)
-    kept = stored_ref[...] - jnp.where(table_ref[2, slot] > 0, product_ref[...], 0.0)
-    out_ref[...] = jnp.where(table_ref[3, slot] > 0, panel_ref[...], kept)
+    schur = lax.dot_general(
+        left_one[0], right_one[0], TRANSPOSED_RIGHT, precision=HIGHEST_PRECISION,
+        preferred_element_type=jnp.float32,
+    )
+    schur += lax.dot_general(
+        left_two[0], right_two[0], TRANSPOSED_RIGHT, precision=HIGHEST_PRECISION,
+        preferred_element_type=jnp.float32,
+    )
+    kept = stored_ref[0] - jnp.where(table_ref[2, slot] > 0, schur, 0.0)
+    out_ref[0] = jnp.where(table_ref[3, slot] > 0, panel_ref[0], kept)
 
 
-def finish_slots(table, stored, products, panels):
+def finish_slots(table, stored, rows, cols):
     slots, block, _ = stored.shape
-    head = panels.shape[0] // 2
+    head = rows.shape[0] // 2
+    classes = cols.shape[0] // 2
+    tile = (1, block, block)
     spec = pltpu.PrefetchScalarGridSpec(
         num_scalar_prefetch=1,
         grid=(slots,),
         in_specs=[
-            pl.BlockSpec((1, block, block), lambda s, t: (s, 0, 0)),
-            pl.BlockSpec((1, block, block), lambda s, t: (t[0, s], 0, t[1, s])),
-            pl.BlockSpec(
-                (1, block, block), lambda s, t: (t[4, 0] * head + jnp.minimum(s, head - 1), 0, 0)
-            ),
+            pl.BlockSpec(tile, lambda s, t: (s, 0, 0)),
+            pl.BlockSpec(tile, lambda s, t: (t[0, s], 0, 0)),
+            pl.BlockSpec(tile, lambda s, t: (head + t[0, s], 0, 0)),
+            pl.BlockSpec(tile, lambda s, t: (t[1, s], 0, 0)),
+            pl.BlockSpec(tile, lambda s, t: (classes + t[1, s], 0, 0)),
+            pl.BlockSpec(tile, lambda s, t: (t[4, 0] * head + jnp.minimum(s, head - 1), 0, 0)),
         ],
-        out_specs=pl.BlockSpec((1, block, block), lambda s, t: (s, 0, 0)),
+        out_specs=pl.BlockSpec(tile, lambda s, t: (s, 0, 0)),
     )
     return pl.pallas_call(
         tail_kernel, grid_spec=spec, out_shape=jax.ShapeDtypeStruct(stored.shape, stored.dtype)
-    )(table, stored, products, panels)
+    )(table, stored, rows, rows, cols, cols, rows)
 
 
 def per_device(blocks, panel_rows, target_slots, diag_inverse, cross_block):
@@ -85,16 +96,15 @@
     present = row_index >= 0
     left_slot = jnp.clip(jnp.where(present, row_index, 0), 0, slot_count - 1)
     right_slot = jnp.clip(jnp.where(present, col_index - class_start, 0), 0, PER_CLASS - 1)
-    products = jnp.einsum("fakm,fbjm->akbj", both_rows, both_cols, precision=PRODUCT_PRECISION)
-    products = products.reshape(slot_count, block, PER_CLASS * block)
     head_live = panel_rows >= 0
     keep_head = (column == 0) & head_live[0] | (column == 1) & head_live[1]
     slots = stored.shape[0]
     keep = jnp.zeros((slots,), jnp.bool_).at[:slot_count].set(keep_head)
     panel_column = jnp.full((slots,), column == 1)
     table = jnp.stack([left_slot, right_slot, present, keep, panel_column]).astype(jnp.int32)
-    panels = both_rows.reshape(2 * slot_count, block, block)
-    factored = finish_slots(table, stored, products, panels)
+    rows = both_rows.reshape(2 * slot_count, block, block)
+    cols = both_cols.reshape(2 * PER_CLASS, block, block)
+    factored = finish_slots(table, stored, rows, cols)
     return factored[:, None]
 
 

time: 167 us -> 165 us (0.988)
  matrix products: 10.1 us -> 2.78 us
  Pallas kernels: 11.5 us -> 16.9 us
    dot_general x1 -> x0, matrix products: 7.29 us -> none  [per_device(): jnp.einsum('fakm,fbjm->akbj', both_rows, both_cols, precision=PRODUCT_PRE...]
    pallas_call x1, Pallas kernels: 11.5 us -> 16.9 us  [finish_slots(): pl.pallas_call(tail_kernel, grid_spec=spec, out_shape=jax.ShapeDtypeStruc...]
where the time goes in v8:
time: 165 us; the launch traced here: 164 us
  waiting for transfers between devices  81.7 us (50%)
  starting transfers between devices  28.9 us (18%)
  Pallas kernels  16.9 us (10%)
  blocking collectives  13.8 us (8%)
  between operations  13.5 us (8%)
  local copies, waits for them, and re-layouts  5.86 us (4%)
  matrix products  2.78 us (2%)
    all_to_all x1, waiting for transfers between devices, per_device(): received = lax.all_to_all(pieces, COL_AXES, 0, 0, tiled=True)  47.3 us
    all_gather x1, waiting for transfers between devices, per_device(): both_rows = lax.all_gather(both_rows, ('zh', 'zl'), axis=1, tiled=True)  17.4 us
    pallas_call x1, Pallas kernels, finish_slots(): pl.pallas_call(tail_kernel, grid_spec=spec, out_shape=jax.ShapeDtypeStruc...  16.9 us
    all_to_all x1, waiting for transfers between devices, per_device(): class_pieces = lax.all_to_all(spread, 'row', 0, 0, tiled=True)  14.4 us
    all_gather x1, blocking collectives, per_device(): both_rows = lax.all_gather(both_pieces, 'x', axis=1, tiled=True)  13.8 us
    all_to_all x1, starting transfers between devices, per_device(): received = lax.all_to_all(pieces, COL_AXES, 0, 0, tiled=True)  12 us
    all_to_all x1, starting transfers between devices, per_device(): class_pieces = lax.all_to_all(spread, 'row', 0, 0, tiled=True)  10.9 us
    ppermute x1, starting transfers between devices, per_device(): swapped = lax.ppermute(both_pieces, ('row',) + CLASS_AXES, swap)  5.96 us
  transfers between devices with their start and end apart: 4, of which 4 were waited for; matrix products, arithmetic and copies ran while one was open for 2% of the time, Pallas kernels for 0%

profile of v8, /device:TPU:1, one launch (start us, length us, event | category | flops | bytes accessed | tf_op | source)
XLA Modules:
  0.0 164.1 jit_solution(6334174074330205928)
XLA Ops:
  6.5 0.0 copy-start
  6.5 3.1 %slice.51 = f32[8,1,256,256]{3,2,1,0:T(8,128)} slice(f32[16,1,256,256]{3,2,1,0:T(8,128)} %param.7), slice={[0:8], [0:1], [0:256], [0:256]} | slice | bytes 4194304 | tf_op jit(solution)/shard_map/slice | solution.py:68
  9.6 0.0 copy-start.2
  9.6 0.0 copy-start.1
  9.6 12.0 %all-to-all-start = ((f32[32,64,256]{2,1,0:T(8,128)}), f32[32,64,256]{2,1,0:T(8,128)S(1)}, u32[]{:S(2)}, u32[]{:S(2)}) async-start(f32[32,64,256]{2,1,0:T(8,128)} %bitcast.6), calls=%async_computation | async-start | bytes 4194304 | tf_op jit(solution)/shard_map/all_to_all | solution.py:71
  21.6 0.0 all-gather.2.cloned.1.call-start
  21.7 0.0 copy-done.2
  21.7 0.7 fusion.12
  22.4 0.0 copy-done
  22.4 0.0 copy-done.1
  22.4 0.4 fusion.2
  22.8 47.3 %all-to-all-done = f32[32,64,256]{2,1,0:T(8,128)S(1)} async-done(((f32[32,64,256]{2,1,0:T(8,128)}), f32[32,64,256]{2,1,0:T(8,128)S(1)}, u32[]{:S(2)}, u32[]{:S(2)}) %all-to-all-start) | async-done | bytes 2097184 | tf_op jit(solution)/shard_map/all_to_all | solution.py:71
  70.1 1.0 convolution_select_fusion.1
  71.1 0.4 convolution_subtract_fusion
  71.5 1.0 fusion
  72.5 0.0 copy-start.3
  72.5 13.8 %all_gather.6 = f32[2,256,256]{2,1,0:T(8,128)} all-gather(f32[2,64,256]{2,1,0:T(8,128)S(1)} %pad_maximum_fusion), channel_id=1, replica_groups=mesh['row'=8,'zh'=4,'zl'=2,'x'=4] {'x'}, dimensions={1}, use_global_device_ids=true | all-gather | bytes 655360 | tf_op jit(solution)/shard_map/all_gather | solution.py:90
  86.3 0.0 all-gather.2.cloned.1.call-update
  86.3 6.0 %collective-permute-start = (f32[2,64,256]{2,1,0:T(8,128)S(1)}, f32[2,64,256]{2,1,0:T(8,128)S(1)}, u32[]{:S(2)}, u32[]{:S(2)}) collective-permute-start(f32[2,64,256]{2,1,0:T(8,128)S(1)} %pad_maximum_fusion), channel_id=1, source_target_pairs={{0,0},{1,32},{2,64},{3,96},{4,128},{5,160},{6,192},{7,224},{32,1},... | collective-permute-start | bytes 393224 | tf_op jit(solution)/shard_map/ppermute | solution.py:84
  92.3 2.6 %collective-permute-done = f32[2,64,256]{2,1,0:T(8,128)S(1)} collective-permute-done((f32[2,64,256]{2,1,0:T(8,128)S(1)}, f32[2,64,256]{2,1,0:T(8,128)S(1)}, u32[]{:S(2)}, u32[]{:S(2)}) %collective-permute-start) | collective-permute-done | bytes 131104 | tf_op jit(solution)/shard_map/ppermute | solution.py:84
  94.9 1.1 broadcast_in_dim.19
  96.0 10.9 %all-to-all-start.1 = ((f32[8,2,64,256]{3,2,1,0:T(8,128)}), f32[8,2,64,256]{3,2,1,0:T(8,128)S(1)}, u32[]{:S(2)}, u32[]{:S(2)}) async-start(f32[8,2,64,256]{3,2,1,0:T(8,128)} %broadcast_in_dim.19), calls=%async_computation.1 | async-start | bytes 2097152 | tf_op jit(solution)/shard_map/all_to_all | solution.py:86
  106.9 0.0 copy-done.3
  106.9 0.6 stack.27.table_ref
  107.5 14.4 %all-to-all-done.1 = f32[8,2,64,256]{3,2,1,0:T(8,128)S(1)} async-done(((f32[8,2,64,256]{3,2,1,0:T(8,128)}), f32[8,2,64,256]{3,2,1,0:T(8,128)S(1)}, u32[]{:S(2)}, u32[]{:S(2)}) %all-to-all-start.1) | async-done | bytes 1048608 | tf_op jit(solution)/shard_map/all_to_all | solution.py:86
  121.9 1.1 copy.7
  123.0 17.4 %all-gather.2.cloned.1.call-done = f32[2,2048,256]{2,1,0:T(8,128)} async-done(((f32[2,256,256]{2,1,0:T(8,128)}), f32[2,2048,256]{2,1,0:T(8,128)}) %all-gather.2.cloned.1.call-update) | async-done | bytes 4194320 | tf_op jit(solution)/shard_map/all_gather | solution.py:91
  140.4 16.9 %shard_map.55 = f32[16,256,256]{2,1,0:T(8,128)} custom-call(s32[5,16]{1,0:T(8,128)} %stack.27.table_ref, f32[16,256,256]{2,1,0:T(8,128)} %bitcast.49, f32[16,256,256]{2,1,0:T(8,128)} %bitcast.44, f32[16,256,256]{2,1,0:T(8,128)} %bitcast.45, f32[4,256,256]{2,1,0:T(8,128)} %bitcast.47, f32[4,256,256]{2,1,0:T(8,128)} %bitcast.48, f32[16,256,256]{2,1,0:T(8,128)} %bitcast.46), custom_call_target="tpu_custom_call" | custom-call | tf_op jit(solution)/shard_map/pallas_call | solution.py:56
  (8 shorter events, 0.1 us)
Async XLA Ops:
  6.5 15.9 %copy-start = (f32[256,256]{1,0:T(8,128)S(1)}, f32[256,256]{1,0:T(8,128)}, u32[]{:S(2)}) copy-start(f32[256,256]{1,0:T(8,128)} %param.11) | copy-start | bytes 786436
  9.6 12.1 %copy-start.2 = (s32[2,8]{1,0:T(2,128)S(1)}, s32[2,8]{1,0:T(2,128)}, u32[]{:S(2)}) copy-start(s32[2,8]{1,0:T(2,128)} %param.8) | copy-start | bytes 196
  9.6 12.8 %copy-start.1 = (f32[2,256,256]{2,1,0:T(8,128)S(1)}, f32[2,256,256]{2,1,0:T(8,128)}, u32[]{:S(2)}) copy-start(f32[2,256,256]{2,1,0:T(8,128)} %param.10) | copy-start | bytes 1572868
  9.6 60.5 %all-to-all-start = ((f32[32,64,256]{2,1,0:T(8,128)}), f32[32,64,256]{2,1,0:T(8,128)S(1)}, u32[]{:S(2)}, u32[]{:S(2)}) async-start(f32[32,64,256]{2,1,0:T(8,128)} %bitcast.6), calls=%async_computation | async-start | bytes 4194304 | tf_op jit(solution)/shard_map/all_to_all | solution.py:71
  21.6 118.8 %all-gather.2.cloned.1.call-start = ((), (), s32[]{:S(2)}) async-start(), calls=%async_computation.2 | async-start | bytes 4718592 | tf_op jit(solution)/shard_map/all_gather | solution.py:91
  72.5 34.4 %copy-start.3 = (s32[2,16,1]{1,2,0:T(1,128)S(1)}, s32[2,16,1]{1,2,0:T(1,128)}, u32[]{:S(2)}) copy-start(s32[2,16,1]{1,2,0:T(1,128)} %param.9) | copy-start | bytes 388
  86.3 8.6 %collective-permute-start = (f32[2,64,256]{2,1,0:T(8,128)S(1)}, f32[2,64,256]{2,1,0:T(8,128)S(1)}, u32[]{:S(2)}, u32[]{:S(2)}) collective-permute-start(f32[2,64,256]{2,1,0:T(8,128)S(1)} %pad_maximum_fusion), channel_id=1, source_target_pairs={{0,0},{1,32},{2,64},{3,96},{4,128},{5,160},{6,192},{7,224},{32,1},... | collective-permute-start | bytes 393224 | tf_op jit(solution)/shard_map/ppermute | solution.py:84
  96.0 26.0 %all-to-all-start.1 = ((f32[8,2,64,256]{3,2,1,0:T(8,128)}), f32[8,2,64,256]{3,2,1,0:T(8,128)S(1)}, u32[]{:S(2)}, u32[]{:S(2)}) async-start(f32[8,2,64,256]{3,2,1,0:T(8,128)} %broadcast_in_dim.19), calls=%async_computation.1 | async-start | bytes 2097152 | tf_op jit(solution)/shard_map/all_to_all | solution.py:86
Sparse Core Ops, SparseCore 0:
  86.4 53.9 all-gather.1

commit v9 on v8

--- a/solution.py
+++ b/solution.py
@@ -12,6 +12,7 @@
 
 
 HIGHEST_PRECISION = lax.Precision.HIGHEST
+PRODUCT_PRECISION = lax.Precision.HIGH
 TRANSPOSED_RIGHT = (((1,), (1,)), ((), ()))
 COL_AXES = ("zh", "zl", "x")
 CLASS_AXES = ("zl", "x")
@@ -24,11 +25,11 @@
 def tail_kernel(table_ref, stored_ref, left_one, left_two, right_one, right_two, panel_ref, out_ref):
     slot = pl.program_id(0)
     schur = lax.dot_general(
-        left_one[0], right_one[0], TRANSPOSED_RIGHT, precision=HIGHEST_PRECISION,
+        left_one[0], right_one[0], TRANSPOSED_RIGHT, precision=PRODUCT_PRECISION,
         preferred_element_type=jnp.float32,
     )
     schur += lax.dot_general(
-        left_two[0], right_two[0], TRANSPOSED_RIGHT, precision=HIGHEST_PRECISION,
+        left_two[0], right_two[0], TRANSPOSED_RIGHT, precision=PRODUCT_PRECISION,
         preferred_element_type=jnp.float32,
     )
     kept = stored_ref[0] - jnp.where(table_ref[2, slot] > 0, schur, 0.0)

time: 165 us -> 163 us (0.988)
  Pallas kernels: 16.9 us -> 14.6 us
    pallas_call x1, Pallas kernels: 16.9 us -> 14.6 us  [finish_slots(): pl.pallas_call(tail_kernel, grid_spec=spec, out_shape=jax.ShapeDtypeStruc...]
where the time goes in v9:
time: 163 us; the launch traced here: 162 us
  waiting for transfers between devices  81.7 us (50%)
  starting transfers between devices  28.9 us (18%)
  Pallas kernels  14.6 us (9%)
  blocking collectives  13.8 us (8%)
  between operations  13.5 us (8%)
  local copies, waits for them, and re-layouts  5.86 us (4%)
  matrix products  2.78 us (2%)
    all_to_all x1, waiting for transfers between devices, per_device(): received = lax.all_to_all(pieces, COL_AXES, 0, 0, tiled=True)  47.3 us
    all_gather x1, waiting for transfers between devices, per_device(): both_rows = lax.all_gather(both_rows, ('zh', 'zl'), axis=1, tiled=True)  17.4 us
    pallas_call x1, Pallas kernels, finish_slots(): pl.pallas_call(tail_kernel, grid_spec=spec, out_shape=jax.ShapeDtypeStruc...  14.6 us
    all_to_all x1, waiting for transfers between devices, per_device(): class_pieces = lax.all_to_all(spread, 'row', 0, 0, tiled=True)  14.4 us
    all_gather x1, blocking collectives, per_device(): both_rows = lax.all_gather(both_pieces, 'x', axis=1, tiled=True)  13.8 us
    all_to_all x1, starting transfers between devices, per_device(): received = lax.all_to_all(pieces, COL_AXES, 0, 0, tiled=True)  12 us
    all_to_all x1, starting transfers between devices, per_device(): class_pieces = lax.all_to_all(spread, 'row', 0, 0, tiled=True)  10.9 us
    ppermute x1, starting transfers between devices, per_device(): swapped = lax.ppermute(both_pieces, ('row',) + CLASS_AXES, swap)  5.96 us
  transfers between devices with their start and end apart: 4, of which 4 were waited for; matrix products, arithmetic and copies ran while one was open for 2% of the time, Pallas kernels for 0%

profile of v9, /device:TPU:1, one launch (start us, length us, event | category | flops | bytes accessed | tf_op | source)
XLA Modules:
  0.0 161.9 jit_solution(18312079013836826533)
XLA Ops:
  6.5 0.0 copy-start
  6.5 3.1 %slice.51 = f32[8,1,256,256]{3,2,1,0:T(8,128)} slice(f32[16,1,256,256]{3,2,1,0:T(8,128)} %param.7), slice={[0:8], [0:1], [0:256], [0:256]} | slice | bytes 4194304 | tf_op jit(solution)/shard_map/slice | solution.py:69
  9.6 0.0 copy-start.2
  9.6 0.0 copy-start.1
  9.6 12.0 %all-to-all-start = ((f32[32,64,256]{2,1,0:T(8,128)}), f32[32,64,256]{2,1,0:T(8,128)S(1)}, u32[]{:S(2)}, u32[]{:S(2)}) async-start(f32[32,64,256]{2,1,0:T(8,128)} %bitcast.6), calls=%async_computation | async-start | bytes 4194304 | tf_op jit(solution)/shard_map/all_to_all | solution.py:72
  21.6 0.0 all-gather.2.cloned.1.call-start
  21.7 0.0 copy-done.2
  21.7 0.7 fusion.12
  22.4 0.0 copy-done
  22.4 0.0 copy-done.1
  22.4 0.4 fusion.2
  22.8 47.3 %all-to-all-done = f32[32,64,256]{2,1,0:T(8,128)S(1)} async-done(((f32[32,64,256]{2,1,0:T(8,128)}), f32[32,64,256]{2,1,0:T(8,128)S(1)}, u32[]{:S(2)}, u32[]{:S(2)}) %all-to-all-start) | async-done | bytes 2097184 | tf_op jit(solution)/shard_map/all_to_all | solution.py:72
  70.1 1.0 convolution_select_fusion.1
  71.1 0.4 convolution_subtract_fusion
  71.5 1.0 fusion
  72.5 0.0 copy-start.3
  72.5 13.8 %all_gather.6 = f32[2,256,256]{2,1,0:T(8,128)} all-gather(f32[2,64,256]{2,1,0:T(8,128)S(1)} %pad_maximum_fusion), channel_id=1, replica_groups=mesh['row'=8,'zh'=4,'zl'=2,'x'=4] {'x'}, dimensions={1}, use_global_device_ids=true | all-gather | bytes 655360 | tf_op jit(solution)/shard_map/all_gather | solution.py:91
  86.3 0.0 all-gather.2.cloned.1.call-update
  86.3 6.0 %collective-permute-start = (f32[2,64,256]{2,1,0:T(8,128)S(1)}, f32[2,64,256]{2,1,0:T(8,128)S(1)}, u32[]{:S(2)}, u32[]{:S(2)}) collective-permute-start(f32[2,64,256]{2,1,0:T(8,128)S(1)} %pad_maximum_fusion), channel_id=1, source_target_pairs={{0,0},{1,32},{2,64},{3,96},{4,128},{5,160},{6,192},{7,224},{32,1},... | collective-permute-start | bytes 393224 | tf_op jit(solution)/shard_map/ppermute | solution.py:85
  92.3 2.6 %collective-permute-done = f32[2,64,256]{2,1,0:T(8,128)S(1)} collective-permute-done((f32[2,64,256]{2,1,0:T(8,128)S(1)}, f32[2,64,256]{2,1,0:T(8,128)S(1)}, u32[]{:S(2)}, u32[]{:S(2)}) %collective-permute-start) | collective-permute-done | bytes 131104 | tf_op jit(solution)/shard_map/ppermute | solution.py:85
  94.9 1.1 broadcast_in_dim.19
  96.0 10.9 %all-to-all-start.1 = ((f32[8,2,64,256]{3,2,1,0:T(8,128)}), f32[8,2,64,256]{3,2,1,0:T(8,128)S(1)}, u32[]{:S(2)}, u32[]{:S(2)}) async-start(f32[8,2,64,256]{3,2,1,0:T(8,128)} %broadcast_in_dim.19), calls=%async_computation.1 | async-start | bytes 2097152 | tf_op jit(solution)/shard_map/all_to_all | solution.py:87
  106.9 0.0 copy-done.3
  106.9 0.6 stack.27.table_ref
  107.5 14.4 %all-to-all-done.1 = f32[8,2,64,256]{3,2,1,0:T(8,128)S(1)} async-done(((f32[8,2,64,256]{3,2,1,0:T(8,128)}), f32[8,2,64,256]{3,2,1,0:T(8,128)S(1)}, u32[]{:S(2)}, u32[]{:S(2)}) %all-to-all-start.1) | async-done | bytes 1048608 | tf_op jit(solution)/shard_map/all_to_all | solution.py:87
  121.9 1.1 copy.7
  123.0 17.4 %all-gather.2.cloned.1.call-done = f32[2,2048,256]{2,1,0:T(8,128)} async-done(((f32[2,256,256]{2,1,0:T(8,128)}), f32[2,2048,256]{2,1,0:T(8,128)}) %all-gather.2.cloned.1.call-update) | async-done | bytes 4194320 | tf_op jit(solution)/shard_map/all_gather | solution.py:92
  140.4 14.6 %shard_map.55 = f32[16,256,256]{2,1,0:T(8,128)} custom-call(s32[5,16]{1,0:T(8,128)} %stack.27.table_ref, f32[16,256,256]{2,1,0:T(8,128)} %bitcast.49, f32[16,256,256]{2,1,0:T(8,128)} %bitcast.44, f32[16,256,256]{2,1,0:T(8,128)} %bitcast.45, f32[4,256,256]{2,1,0:T(8,128)} %bitcast.47, f32[4,256,256]{2,1,0:T(8,128)} %bitcast.48, f32[16,256,256]{2,1,0:T(8,128)} %bitcast.46), custom_call_target="tpu_custom_call" | custom-call | tf_op jit(solution)/shard_map/pallas_call | solution.py:57
  (8 shorter events, 0.1 us)
Async XLA Ops:
  6.5 15.9 %copy-start = (f32[256,256]{1,0:T(8,128)S(1)}, f32[256,256]{1,0:T(8,128)}, u32[]{:S(2)}) copy-start(f32[256,256]{1,0:T(8,128)} %param.11) | copy-start | bytes 786436
  9.6 12.1 %copy-start.2 = (s32[2,8]{1,0:T(2,128)S(1)}, s32[2,8]{1,0:T(2,128)}, u32[]{:S(2)}) copy-start(s32[2,8]{1,0:T(2,128)} %param.8) | copy-start | bytes 196
  9.6 12.8 %copy-start.1 = (f32[2,256,256]{2,1,0:T(8,128)S(1)}, f32[2,256,256]{2,1,0:T(8,128)}, u32[]{:S(2)}) copy-start(f32[2,256,256]{2,1,0:T(8,128)} %param.10) | copy-start | bytes 1572868
  9.6 60.5 %all-to-all-start = ((f32[32,64,256]{2,1,0:T(8,128)}), f32[32,64,256]{2,1,0:T(8,128)S(1)}, u32[]{:S(2)}, u32[]{:S(2)}) async-start(f32[32,64,256]{2,1,0:T(8,128)} %bitcast.6), calls=%async_computation | async-start | bytes 4194304 | tf_op jit(solution)/shard_map/all_to_all | solution.py:72
  21.6 118.8 %all-gather.2.cloned.1.call-start = ((), (), s32[]{:S(2)}) async-start(), calls=%async_computation.2 | async-start | bytes 4718592 | tf_op jit(solution)/shard_map/all_gather | solution.py:92
  72.5 34.4 %copy-start.3 = (s32[2,16,1]{1,2,0:T(1,128)S(1)}, s32[2,16,1]{1,2,0:T(1,128)}, u32[]{:S(2)}) copy-start(s32[2,16,1]{1,2,0:T(1,128)} %param.9) | copy-start | bytes 388
  86.3 8.6 %collective-permute-start = (f32[2,64,256]{2,1,0:T(8,128)S(1)}, f32[2,64,256]{2,1,0:T(8,128)S(1)}, u32[]{:S(2)}, u32[]{:S(2)}) collective-permute-start(f32[2,64,256]{2,1,0:T(8,128)S(1)} %pad_maximum_fusion), channel_id=1, source_target_pairs={{0,0},{1,32},{2,64},{3,96},{4,128},{5,160},{6,192},{7,224},{32,1},... | collective-permute-start | bytes 393224 | tf_op jit(solution)/shard_map/ppermute | solution.py:85
  96.0 26.0 %all-to-all-start.1 = ((f32[8,2,64,256]{3,2,1,0:T(8,128)}), f32[8,2,64,256]{3,2,1,0:T(8,128)S(1)}, u32[]{:S(2)}, u32[]{:S(2)}) async-start(f32[8,2,64,256]{3,2,1,0:T(8,128)} %broadcast_in_dim.19), calls=%async_computation.1 | async-start | bytes 2097152 | tf_op jit(solution)/shard_map/all_to_all | solution.py:87
Sparse Core Ops, SparseCore 0:
  86.4 53.9 all-gather.1

commit v10 on v9

--- a/solution.py
+++ b/solution.py
@@ -16,6 +16,7 @@
 TRANSPOSED_RIGHT = (((1,), (1,)), ((), ()))
 COL_AXES = ("zh", "zl", "x")
 CLASS_AXES = ("zl", "x")
+Z_AXES = ("zh", "zl")
 
 
 def apply_inverse(panel_rows_block, inverse):
@@ -50,7 +51,9 @@
             pl.BlockSpec(tile, lambda s, t: (head + t[0, s], 0, 0)),
             pl.BlockSpec(tile, lambda s, t: (t[1, s], 0, 0)),
             pl.BlockSpec(tile, lambda s, t: (classes + t[1, s], 0, 0)),
-            pl.BlockSpec(tile, lambda s, t: (t[4, 0] * head + jnp.minimum(s, head - 1), 0, 0)),
+            pl.BlockSpec(
+                tile, lambda s, t: (t[4, 0] * head + (jnp.minimum(s, head - 1) - t[5, 0] + head) % head, 0, 0)
+            ),
         ],
         out_specs=pl.BlockSpec(tile, lambda s, t: (s, 0, 0)),
     )
@@ -88,22 +91,36 @@
     per_slot = block // chunk
     class_pieces = class_pieces.reshape(PER_CLASS, per_slot, 2, chunk, block)
     both_cols = class_pieces.transpose(2, 0, 1, 3, 4).reshape(2, PER_CLASS, block, block)
-    both_rows = lax.all_gather(both_pieces, "x", axis=1, tiled=True)
-    both_rows = lax.all_gather(both_rows, ("zh", "zl"), axis=1, tiled=True)
-    both_rows = both_rows.reshape(2, slot_count, block, block)
+    own_slot = lax.all_gather(both_pieces, "x", axis=1, tiled=True)
+    ring = lax.axis_size(Z_AXES)
+    ring_place = lax.axis_index(Z_AXES)
+    forward = [(i, (i + 1) % ring) for i in range(ring)]
+    backward = [(i, (i - 1) % ring) for i in range(ring)]
+    by_offset = [own_slot] * ring
+    ahead = own_slot
+    behind = own_slot
+    for step in range(1, ring // 2 + 1):
+        ahead = lax.ppermute(ahead, Z_AXES, forward)
+        by_offset[ring - step] = ahead
+        if step < ring - step:
+            behind = lax.ppermute(behind, Z_AXES, backward)
+            by_offset[step] = behind
+    rows_by_offset = jnp.stack(by_offset, axis=1)
     class_start = column // row_count * PER_CLASS
     row_index = target_slots[0, :, 0]
     col_index = target_slots[1, :, 0]
     present = row_index >= 0
     left_slot = jnp.clip(jnp.where(present, row_index, 0), 0, slot_count - 1)
+    left_slot = (left_slot - ring_place) % ring
     right_slot = jnp.clip(jnp.where(present, col_index - class_start, 0), 0, PER_CLASS - 1)
     head_live = panel_rows >= 0
     keep_head = (column == 0) & head_live[0] | (column == 1) & head_live[1]
     slots = stored.shape[0]
     keep = jnp.zeros((slots,), jnp.bool_).at[:slot_count].set(keep_head)
     panel_column = jnp.full((slots,), column == 1)
-    table = jnp.stack([left_slot, right_slot, present, keep, panel_column]).astype(jnp.int32)
-    rows = both_rows.reshape(2 * slot_count, block, block)
+    place = jnp.full((slots,), ring_place)
+    table = jnp.stack([left_slot, right_slot, present, keep, panel_column, place]).astype(jnp.int32)
+    rows = rows_by_offset.reshape(2 * slot_count, block, block)
     cols = both_cols.reshape(2 * PER_CLASS, block, block)
     factored = finish_slots(table, stored, rows, cols)
     return factored[:, None]

time: 163 us -> 168 us (1.031)
  local copies, waits for them, and re-layouts: 5.86 us -> 20.2 us
  between operations: 13.5 us -> 0.17 us
  starting transfers between devices: 28.9 us -> 39.5 us
  waiting for transfers between devices: 81.7 us -> 75.2 us
    ppermute x0 -> x7, waiting for transfers between devices: none -> 27.9 us  [the longest x4 27.9 us: per_device(): ahead = lax.ppermute(ahead, Z_AXES, forward)]
    all_gather x1 -> x0, waiting for transfers between devices: 17.4 us -> none  [per_device(): both_rows = lax.all_gather(both_rows, ('zh', 'zl'), axis=1, tiled=True)]
    all_to_all x1, waiting for transfers between devices: 14.4 us -> 0.01 us  [per_device(): class_pieces = lax.all_to_all(spread, 'row', 0, 0, tiled=True)]
    ppermute x0 -> x7, starting transfers between devices: none -> 10.4 us  [the longest x3 5.94 us: per_device(): behind = lax.ppermute(behind, Z_AXES, backward)]
    unnamed x8 -> x15, local copies, waits for them, and re-layouts: 0.02 us -> 8.93 us
    another operation x2 -> x4, local copies, waits for them, and re-layouts: 0.61 us -> 5.98 us  [the longest x2 5.37 us: per_device(): rows_by_offset = jnp.stack(by_offset, axis=1)]
    ppermute x1, waiting for transfers between devices: 2.63 us -> 0.01 us  [per_device(): swapped = lax.ppermute(both_pieces, ('row',) + CLASS_AXES, swap)]
  transfers between devices with their start and end apart: 4 -> 10, of which waited for: 4 -> 4; matrix products, arithmetic and copies ran while one was open for 2% -> 6% of each run, Pallas kernels for 0% -> 0%
where the time goes in v10:
time: 168 us; the launch traced here: 167 us
  waiting for transfers between devices  75.2 us (45%)
  starting transfers between devices  39.5 us (24%)
  local copies, waits for them, and re-layouts  20.2 us (12%)
  Pallas kernels  14.6 us (9%)
  blocking collectives  13.4 us (8%)
  matrix products  2.9 us (2%)
    all_to_all x1, waiting for transfers between devices, per_device(): received = lax.all_to_all(pieces, COL_AXES, 0, 0, tiled=True)  47.3 us
    ppermute x4, waiting for transfers between devices, per_device(): ahead = lax.ppermute(ahead, Z_AXES, forward)  27.9 us
    pallas_call x1, Pallas kernels, finish_slots(): pl.pallas_call(tail_kernel, grid_spec=spec, out_shape=jax.ShapeDtypeStruc...  14.6 us
    all_gather x1, blocking collectives, per_device(): own_slot = lax.all_gather(both_pieces, 'x', axis=1, tiled=True)  13.4 us
    all_to_all x1, starting transfers between devices, per_device(): received = lax.all_to_all(pieces, COL_AXES, 0, 0, tiled=True)  12 us
    all_to_all x1, starting transfers between devices, per_device(): class_pieces = lax.all_to_all(spread, 'row', 0, 0, tiled=True)  11.2 us
    unnamed x15, local copies, waits for them, and re-layouts  8.93 us
    ppermute x3, starting transfers between devices, per_device(): behind = lax.ppermute(behind, Z_AXES, backward)  5.94 us
  transfers between devices with their start and end apart: 10, of which 4 were waited for; matrix products, arithmetic and copies ran while one was open for 6% of the time, Pallas kernels for 0%

profile of v10, /device:TPU:1, one launch (start us, length us, event | category | flops | bytes accessed | tf_op | source)
XLA Modules:
  0.0 166.7 jit_solution(16995136361468764919)
XLA Ops:
  0.0 0.0 copy-start
  0.0 0.0 copy-start.3
  0.0 0.0 copy-start.1
  0.0 3.1 %slice.51 = f32[8,1,256,256]{3,2,1,0:T(8,128)} slice(f32[16,1,256,256]{3,2,1,0:T(8,128)} %param.7), slice={[0:8], [0:1], [0:256], [0:256]} | slice | bytes 4194304 | tf_op jit(solution)/shard_map/slice | solution.py:72
  3.1 0.0 copy-start.2
  3.1 12.0 %all-to-all-start = ((f32[32,64,256]{2,1,0:T(8,128)}), f32[32,64,256]{2,1,0:T(8,128)S(1)}, u32[]{:S(2)}, u32[]{:S(2)}) async-start(f32[32,64,256]{2,1,0:T(8,128)} %bitcast.6), calls=%async_computation | async-start | bytes 4194304 | tf_op jit(solution)/shard_map/all_to_all | solution.py:75
  15.2 0.0 copy-done.3
  15.2 0.7 fusion.14
  15.9 0.0 copy-done
  15.9 0.0 copy-done.1
  15.9 0.4 fusion.2
  16.3 47.3 %all-to-all-done = f32[32,64,256]{2,1,0:T(8,128)S(1)} async-done(((f32[32,64,256]{2,1,0:T(8,128)}), f32[32,64,256]{2,1,0:T(8,128)S(1)}, u32[]{:S(2)}, u32[]{:S(2)}) %all-to-all-start) | async-done | bytes 2097184 | tf_op jit(solution)/shard_map/all_to_all | solution.py:75
  63.6 1.1 convolution_select_fusion.1
  64.7 0.4 convolution_subtract_fusion
  65.0 1.1 fusion
  66.1 13.4 %all_gather.3 = f32[2,256,256]{2,1,0:T(8,128)S(1)} all-gather(f32[2,64,256]{2,1,0:T(8,128)S(1)} %pad_maximum_fusion), channel_id=1, replica_groups=mesh['row'=8,'zh'=4,'zl'=2,'x'=4] {'x'}, dimensions={1}, use_global_device_ids=true | all-gather | bytes 655360 | tf_op jit(solution)/shard_map/all_gather | solution.py:94
  79.5 0.0 collective-permute-start.3
  79.5 2.7 %collective-permute-start = (f32[2,256,256]{2,1,0:T(8,128)S(1)}, f32[2,256,256]{2,1,0:T(8,128)S(1)}, u32[]{:S(2)}, u32[]{:S(2)}) collective-permute-start(f32[2,256,256]{2,1,0:T(8,128)S(1)} %all_gather.3), channel_id=1, source_target_pairs={{0,28},{4,0},{8,4},{12,8},{16,12},{20,16},{24,20},{28,24},{1,29},{... | collective-permute-start | bytes 1572872 | tf_op jit(solution)/shard_map/ppermute | solution.py:106
  82.2 9.6 %collective-permute-done.3 = f32[2,256,256]{2,1,0:T(8,128)S(1)} collective-permute-done((f32[2,256,256]{2,1,0:T(8,128)S(1)}, f32[2,256,256]{2,1,0:T(8,128)S(1)}, u32[]{:S(2)}, u32[]{:S(2)}) %collective-permute-start.3) | collective-permute-done | bytes 524320 | tf_op jit(solution)/shard_map/ppermute | solution.py:103
  91.8 0.0 collective-permute-start.4
  91.8 0.0 copy-done.2
  91.9 5.9 %collective-permute-start.7 = (f32[2,64,256]{2,1,0:T(8,128)S(1)}, f32[2,64,256]{2,1,0:T(8,128)S(1)}, u32[]{:S(2)}, u32[]{:S(2)}) collective-permute-start(f32[2,64,256]{2,1,0:T(8,128)S(1)} %pad_maximum_fusion), channel_id=1, source_target_pairs={{0,0},{1,32},{2,64},{3,96},{4,128},{5,160},{6,192},{7,224},{32,1},... | collective-permute-start | bytes 393224 | tf_op jit(solution)/shard_map/ppermute | solution.py:88
  97.7 0.0 collective-permute-done
  97.7 3.2 %collective-permute-start.1 = (f32[2,256,256]{2,1,0:T(8,128)S(1)}, f32[2,256,256]{2,1,0:T(8,128)}, u32[]{:S(2)}, u32[]{:S(2)}) collective-permute-start(f32[2,256,256]{2,1,0:T(8,128)S(1)} %collective-permute-done), channel_id=1, source_target_pairs={{0,28},{4,0},{8,4},{12,8},{16,12},{20,16},{24,20},{28,24},{1,29},{... | collective-permute-start | bytes 1572872 | tf_op jit(solution)/shard_map/ppermute | solution.py:106
  100.9 0.0 collective-permute-done.7
  100.9 1.1 broadcast_in_dim.19
  102.0 11.2 %all-to-all-start.1 = ((f32[8,2,64,256]{3,2,1,0:T(8,128)}), f32[8,2,64,256]{3,2,1,0:T(8,128)S(1)}, u32[]{:S(2)}, u32[]{:S(2)}) async-start(f32[8,2,64,256]{3,2,1,0:T(8,128)} %broadcast_in_dim.19), calls=%async_computation.1 | async-start | bytes 2097152 | tf_op jit(solution)/shard_map/all_to_all | solution.py:90
  113.2 0.0 collective-permute-done.4
  113.2 3.4 %collective-permute-start.5 = (f32[2,256,256]{2,1,0:T(8,128)S(1)}, f32[2,256,256]{2,1,0:T(8,128)}, u32[]{:S(2)}, u32[]{:S(2)}) collective-permute-start(f32[2,256,256]{2,1,0:T(8,128)S(1)} %collective-permute-done.4), channel_id=1, source_target_pairs={{0,4},{4,8},{8,12},{12,16},{16,20},{20,24},{24,28},{28,0},{1,5},{5... | collective-permute-start | bytes 1572872 | tf_op jit(solution)/shard_map/ppermute | solution.py:103
  116.6 0.6 stack.54.table_ref
  117.3 0.0 collective-permute-done.1
  117.3 0.1 collective-permute-start.2
  117.3 0.8 bitcast_dynamic-update-slice_fusion.7
  118.2 10.8 %collective-permute-done.5 = f32[2,256,256]{2,1,0:T(8,128)} collective-permute-done((f32[2,256,256]{2,1,0:T(8,128)S(1)}, f32[2,256,256]{2,1,0:T(8,128)}, u32[]{:S(2)}, u32[]{:S(2)}) %collective-permute-start.5) | collective-permute-done | bytes 524320 | tf_op jit(solution)/shard_map/ppermute | solution.py:103
  129.0 1.1 collective-permute-start.6
  130.1 0.8 bitcast_dynamic-update-slice_fusion.6
  130.9 1.9 %bitcast_dynamic-update-slice_fusion.5 = f32[2,8,256,256]{3,2,0,1:T(8,128)} fusion(f32[2,8,256,256]{3,2,0,1:T(8,128)} %bitcast_dynamic-update-slice_fusion.6, f32[2,256,256]{2,1,0:T(8,128)} %collective-permute-done.1), kind=kLoop, calls=%fused_computation.9 | loop fusion | bytes 1048576
  132.7 0.0 all-to-all-done.1
  132.8 1.1 copy.9
  133.8 0.0 collective-permute-done.2
  133.8 1.9 %bitcast_dynamic-update-slice_fusion.4 = f32[2,8,256,256]{3,2,0,1:T(8,128)} fusion(f32[2,8,256,256]{3,2,0,1:T(8,128)} %bitcast_dynamic-update-slice_fusion.5, f32[2,256,256]{2,1,0:T(8,128)} %collective-permute-done.2), kind=kLoop, calls=%fused_computation.8 | loop fusion | bytes 1048576
  135.7 7.5 %collective-permute-done.6 = f32[2,256,256]{2,1,0:T(8,128)S(1)} collective-permute-done((f32[2,256,256]{2,1,0:T(8,128)}, f32[2,256,256]{2,1,0:T(8,128)S(1)}, u32[]{:S(2)}, u32[]{:S(2)}) %collective-permute-start.6) | collective-permute-done | bytes 524320 | tf_op jit(solution)/shard_map/ppermute | solution.py:103
  143.2 0.8 bitcast_dynamic-update-slice_fusion.3
  144.0 1.9 %bitcast_dynamic-update-slice_fusion.2 = f32[2,8,256,256]{3,2,0,1:T(8,128)} fusion(f32[2,8,256,256]{3,2,0,1:T(8,128)} %bitcast_dynamic-update-slice_fusion.3, f32[2,256,256]{2,1,0:T(8,128)} %collective-permute-done.5), kind=kLoop, calls=%fused_computation.6 | loop fusion | bytes 1048576
  145.9 0.8 bitcast_dynamic-update-slice_fusion.1
  146.7 0.8 bitcast_dynamic-update-slice_fusion
  147.5 4.5 %copy.8 = f32[2,8,256,256]{3,2,1,0:T(8,128)} copy(f32[2,8,256,256]{3,2,0,1:T(8,128)} %bitcast_dynamic-update-slice_fusion) | data formatting | bytes 8388608 | tf_op jit(solution)/shard_map/stack | solution.py:108
  152.1 14.6 %shard_map.55 = f32[16,256,256]{2,1,0:T(8,128)} custom-call(s32[6,16]{1,0:T(8,128)} %stack.54.table_ref, f32[16,256,256]{2,1,0:T(8,128)} %bitcast.65, f32[16,256,256]{2,1,0:T(8,128)} %bitcast.60, f32[16,256,256]{2,1,0:T(8,128)} %bitcast.61, f32[4,256,256]{2,1,0:T(8,128)} %bitcast.63, f32[4,256,256]{2,1,0:T(8,128)} %bitcast.64, f32[16,256,256]{2,1,0:T(8,128)} %bitcast.62), custom_call_target="tpu_custom_call" | custom-call | tf_op jit(solution)/shard_map/pallas_call | solution.py:60
  (9 shorter events, 0.1 us)
Async XLA Ops:
  0.0 15.9 %copy-start = (f32[256,256]{1,0:T(8,128)S(1)}, f32[256,256]{1,0:T(8,128)}, u32[]{:S(2)}) copy-start(f32[256,256]{1,0:T(8,128)} %param.11) | copy-start | bytes 786436
  0.0 15.2 %copy-start.3 = (s32[2,8]{1,0:T(2,128)S(1)}, s32[2,8]{1,0:T(2,128)}, u32[]{:S(2)}) copy-start(s32[2,8]{1,0:T(2,128)} %param.8) | copy-start | bytes 196
  0.0 15.9 %copy-start.1 = (f32[2,256,256]{2,1,0:T(8,128)S(1)}, f32[2,256,256]{2,1,0:T(8,128)}, u32[]{:S(2)}) copy-start(f32[2,256,256]{2,1,0:T(8,128)} %param.10) | copy-start | bytes 1572868
  3.1 88.7 %copy-start.2 = (s32[2,16,1]{1,2,0:T(1,128)S(1)}, s32[2,16,1]{1,2,0:T(1,128)}, u32[]{:S(2)}) copy-start(s32[2,16,1]{1,2,0:T(1,128)} %param.9) | copy-start | bytes 388
  3.1 60.5 %all-to-all-start = ((f32[32,64,256]{2,1,0:T(8,128)}), f32[32,64,256]{2,1,0:T(8,128)S(1)}, u32[]{:S(2)}, u32[]{:S(2)}) async-start(f32[32,64,256]{2,1,0:T(8,128)} %bitcast.6), calls=%async_computation | async-start | bytes 4194304 | tf_op jit(solution)/shard_map/all_to_all | solution.py:75
  79.5 12.3 %collective-permute-start.3 = (f32[2,256,256]{2,1,0:T(8,128)S(1)}, f32[2,256,256]{2,1,0:T(8,128)S(1)}, u32[]{:S(2)}, u32[]{:S(2)}) collective-permute-start(f32[2,256,256]{2,1,0:T(8,128)S(1)} %all_gather.3), channel_id=1, source_target_pairs={{0,4},{4,8},{8,12},{12,16},{16,20},{20,24},{24,28},{28,0},{1,5},{5... | collective-permute-start | bytes 1572872 | tf_op jit(solution)/shard_map/ppermute | solution.py:103
  79.5 18.2 %collective-permute-start = (f32[2,256,256]{2,1,0:T(8,128)S(1)}, f32[2,256,256]{2,1,0:T(8,128)S(1)}, u32[]{:S(2)}, u32[]{:S(2)}) collective-permute-start(f32[2,256,256]{2,1,0:T(8,128)S(1)} %all_gather.3), channel_id=1, source_target_pairs={{0,28},{4,0},{8,4},{12,8},{16,12},{20,16},{24,20},{28,24},{1,29},{... | collective-permute-start | bytes 1572872 | tf_op jit(solution)/shard_map/ppermute | solution.py:106
  91.8 21.5 %collective-permute-start.4 = (f32[2,256,256]{2,1,0:T(8,128)S(1)}, f32[2,256,256]{2,1,0:T(8,128)S(1)}, u32[]{:S(2)}, u32[]{:S(2)}) collective-permute-start(f32[2,256,256]{2,1,0:T(8,128)S(1)} %collective-permute-done.3), channel_id=1, source_target_pairs={{0,4},{4,8},{8,12},{12,16},{16,20},{20,24},{24,28},{28,0},{1,5},{5... | collective-permute-start | bytes 1572872 | tf_op jit(solution)/shard_map/ppermute | solution.py:103
  91.9 9.1 %collective-permute-start.7 = (f32[2,64,256]{2,1,0:T(8,128)S(1)}, f32[2,64,256]{2,1,0:T(8,128)S(1)}, u32[]{:S(2)}, u32[]{:S(2)}) collective-permute-start(f32[2,64,256]{2,1,0:T(8,128)S(1)} %pad_maximum_fusion), channel_id=1, source_target_pairs={{0,0},{1,32},{2,64},{3,96},{4,128},{5,160},{6,192},{7,224},{32,1},... | collective-permute-start | bytes 393224 | tf_op jit(solution)/shard_map/ppermute | solution.py:88
  97.7 19.5 %collective-permute-start.1 = (f32[2,256,256]{2,1,0:T(8,128)S(1)}, f32[2,256,256]{2,1,0:T(8,128)}, u32[]{:S(2)}, u32[]{:S(2)}) collective-permute-start(f32[2,256,256]{2,1,0:T(8,128)S(1)} %collective-permute-done), channel_id=1, source_target_pairs={{0,28},{4,0},{8,4},{12,8},{16,12},{20,16},{24,20},{28,24},{1,29},{... | collective-permute-start | bytes 1572872 | tf_op jit(solution)/shard_map/ppermute | solution.py:106
  102.0 30.7 %all-to-all-start.1 = ((f32[8,2,64,256]{3,2,1,0:T(8,128)}), f32[8,2,64,256]{3,2,1,0:T(8,128)S(1)}, u32[]{:S(2)}, u32[]{:S(2)}) async-start(f32[8,2,64,256]{3,2,1,0:T(8,128)} %broadcast_in_dim.19), calls=%async_computation.1 | async-start | bytes 2097152 | tf_op jit(solution)/shard_map/all_to_all | solution.py:90
  113.2 15.7 %collective-permute-start.5 = (f32[2,256,256]{2,1,0:T(8,128)S(1)}, f32[2,256,256]{2,1,0:T(8,128)}, u32[]{:S(2)}, u32[]{:S(2)}) collective-permute-start(f32[2,256,256]{2,1,0:T(8,128)S(1)} %collective-permute-done.4), channel_id=1, source_target_pairs={{0,4},{4,8},{8,12},{12,16},{16,20},{20,24},{24,28},{28,0},{1,5},{5... | collective-permute-start | bytes 1572872 | tf_op jit(solution)/shard_map/ppermute | solution.py:103
  117.3 16.6 %collective-permute-start.2 = (f32[2,256,256]{2,1,0:T(8,128)}, f32[2,256,256]{2,1,0:T(8,128)}, u32[]{:S(2)}, u32[]{:S(2)}) collective-permute-start(f32[2,256,256]{2,1,0:T(8,128)} %collective-permute-done.1), channel_id=1, source_target_pairs={{0,28},{4,0},{8,4},{12,8},{16,12},{20,16},{24,20},{28,24},{1,29},{... | collective-permute-start | bytes 1572872 | tf_op jit(solution)/shard_map/ppermute | solution.py:106
  129.0 14.2 %collective-permute-start.6 = (f32[2,256,256]{2,1,0:T(8,128)}, f32[2,256,256]{2,1,0:T(8,128)S(1)}, u32[]{:S(2)}, u32[]{:S(2)}) collective-permute-start(f32[2,256,256]{2,1,0:T(8,128)} %collective-permute-done.5), channel_id=1, source_target_pairs={{0,4},{4,8},{8,12},{12,16},{16,20},{20,24},{24,28},{28,0},{1,5},{5... | collective-permute-start | bytes 1572872 | tf_op jit(solution)/shard_map/ppermute | solution.py:103

commit v11 on v9

--- a/solution.py
+++ b/solution.py
@@ -13,7 +13,7 @@
 
 HIGHEST_PRECISION = lax.Precision.HIGHEST
 PRODUCT_PRECISION = lax.Precision.HIGH
-TRANSPOSED_RIGHT = (((1,), (1,)), ((), ()))
+PLAIN_PRODUCT = (((1,), (0,)), ((), ()))
 COL_AXES = ("zh", "zl", "x")
 CLASS_AXES = ("zl", "x")
 
@@ -25,11 +25,11 @@
 def tail_kernel(table_ref, stored_ref, left_one, left_two, right_one, right_two, panel_ref, out_ref):
     slot = pl.program_id(0)
     schur = lax.dot_general(
-        left_one[0], right_one[0], TRANSPOSED_RIGHT, precision=PRODUCT_PRECISION,
+        left_one[0], right_one[0], PLAIN_PRODUCT, precision=PRODUCT_PRECISION,
         preferred_element_type=jnp.float32,
     )
     schur += lax.dot_general(
-        left_two[0], right_two[0], TRANSPOSED_RIGHT, precision=PRODUCT_PRECISION,
+        left_two[0], right_two[0], PLAIN_PRODUCT, precision=PRODUCT_PRECISION,
         preferred_element_type=jnp.float32,
     )
     kept = stored_ref[0] - jnp.where(table_ref[2, slot] > 0, schur, 0.0)
@@ -104,7 +104,7 @@
     panel_column = jnp.full((slots,), column == 1)
     table = jnp.stack([left_slot, right_slot, present, keep, panel_column]).astype(jnp.int32)
     rows = both_rows.reshape(2 * slot_count, block, block)
-    cols = both_cols.reshape(2 * PER_CLASS, block, block)
+    cols = jnp.swapaxes(both_cols.reshape(2 * PER_CLASS, block, block), 1, 2)
     factored = finish_slots(table, stored, rows, cols)
     return factored[:, None]
 

time: 163 us -> 163 us (level)
  transfers between devices with their start and end apart: 4 -> 4, of which waited for: 4 -> 4; matrix products, arithmetic and copies ran while one was open for 2% -> 3% of each run, Pallas kernels for 0% -> 0%
where the time goes in v11:
time: 163 us; the launch traced here: 162 us
  waiting for transfers between devices  81.4 us (50%)
  starting transfers between devices  28.9 us (18%)
  Pallas kernels  14.4 us (9%)
  blocking collectives  13.8 us (8%)
  between operations  13.5 us (8%)
  local copies, waits for them, and re-layouts  6.19 us (4%)
  matrix products  2.78 us (2%)
    all_to_all x1, waiting for transfers between devices, per_device(): received = lax.all_to_all(pieces, COL_AXES, 0, 0, tiled=True)  47.3 us
    all_gather x1, waiting for transfers between devices, per_device(): both_rows = lax.all_gather(both_rows, ('zh', 'zl'), axis=1, tiled=True)  17 us
    pallas_call x1, Pallas kernels, finish_slots(): pl.pallas_call(tail_kernel, grid_spec=spec, out_shape=jax.ShapeDtypeStruc...  14.4 us
    all_to_all x1, waiting for transfers between devices, per_device(): class_pieces = lax.all_to_all(spread, 'row', 0, 0, tiled=True)  14.4 us
    all_gather x1, blocking collectives, per_device(): both_rows = lax.all_gather(both_pieces, 'x', axis=1, tiled=True)  13.8 us
    all_to_all x1, starting transfers between devices, per_device(): received = lax.all_to_all(pieces, COL_AXES, 0, 0, tiled=True)  12 us
    all_to_all x1, starting transfers between devices, per_device(): class_pieces = lax.all_to_all(spread, 'row', 0, 0, tiled=True)  10.9 us
    ppermute x1, starting transfers between devices, per_device(): swapped = lax.ppermute(both_pieces, ('row',) + CLASS_AXES, swap)  5.96 us
  transfers between devices with their start and end apart: 4, of which 4 were waited for; matrix products, arithmetic and copies ran while one was open for 3% of the time, Pallas kernels for 0%

profile of v11, /device:TPU:1, one launch (start us, length us, event | category | flops | bytes accessed | tf_op | source)
XLA Modules:
  0.0 161.7 jit_solution(5316455459522342900)
XLA Ops:
  6.5 0.0 copy-start
  6.5 3.1 %slice.51 = f32[8,1,256,256]{3,2,1,0:T(8,128)} slice(f32[16,1,256,256]{3,2,1,0:T(8,128)} %param.7), slice={[0:8], [0:1], [0:256], [0:256]} | slice | bytes 4194304 | tf_op jit(solution)/shard_map/slice | solution.py:69
  9.6 0.0 copy-start.2
  9.6 0.0 copy-start.1
  9.6 12.0 %all-to-all-start = ((f32[32,64,256]{2,1,0:T(8,128)}), f32[32,64,256]{2,1,0:T(8,128)S(1)}, u32[]{:S(2)}, u32[]{:S(2)}) async-start(f32[32,64,256]{2,1,0:T(8,128)} %bitcast.6), calls=%async_computation | async-start | bytes 4194304 | tf_op jit(solution)/shard_map/all_to_all | solution.py:72
  21.6 0.0 all-gather.2.cloned.1.call-start
  21.7 0.0 copy-done.2
  21.7 0.7 fusion.12
  22.4 0.0 copy-done
  22.4 0.0 copy-done.1
  22.4 0.4 fusion.2
  22.8 47.3 %all-to-all-done = f32[32,64,256]{2,1,0:T(8,128)S(1)} async-done(((f32[32,64,256]{2,1,0:T(8,128)}), f32[32,64,256]{2,1,0:T(8,128)S(1)}, u32[]{:S(2)}, u32[]{:S(2)}) %all-to-all-start) | async-done | bytes 2097184 | tf_op jit(solution)/shard_map/all_to_all | solution.py:72
  70.1 1.0 convolution_select_fusion.1
  71.1 0.4 convolution_subtract_fusion
  71.5 1.0 fusion
  72.5 0.0 copy-start.3
  72.5 13.8 %all_gather.6 = f32[2,256,256]{2,1,0:T(8,128)} all-gather(f32[2,64,256]{2,1,0:T(8,128)S(1)} %pad_maximum_fusion), channel_id=1, replica_groups=mesh['row'=8,'zh'=4,'zl'=2,'x'=4] {'x'}, dimensions={1}, use_global_device_ids=true | all-gather | bytes 655360 | tf_op jit(solution)/shard_map/all_gather | solution.py:91
  86.3 0.0 all-gather.2.cloned.1.call-update
  86.3 6.0 %collective-permute-start = (f32[2,64,256]{2,1,0:T(8,128)S(1)}, f32[2,64,256]{2,1,0:T(8,128)S(1)}, u32[]{:S(2)}, u32[]{:S(2)}) collective-permute-start(f32[2,64,256]{2,1,0:T(8,128)S(1)} %pad_maximum_fusion), channel_id=1, source_target_pairs={{0,0},{1,32},{2,64},{3,96},{4,128},{5,160},{6,192},{7,224},{32,1},... | collective-permute-start | bytes 393224 | tf_op jit(solution)/shard_map/ppermute | solution.py:85
  92.3 2.6 %collective-permute-done = f32[2,64,256]{2,1,0:T(8,128)S(1)} collective-permute-done((f32[2,64,256]{2,1,0:T(8,128)S(1)}, f32[2,64,256]{2,1,0:T(8,128)S(1)}, u32[]{:S(2)}, u32[]{:S(2)}) %collective-permute-start) | collective-permute-done | bytes 131104 | tf_op jit(solution)/shard_map/ppermute | solution.py:85
  94.9 1.1 broadcast_in_dim.19
  96.0 10.9 %all-to-all-start.1 = ((f32[8,2,64,256]{3,2,1,0:T(8,128)}), f32[8,2,64,256]{3,2,1,0:T(8,128)S(1)}, u32[]{:S(2)}, u32[]{:S(2)}) async-start(f32[8,2,64,256]{3,2,1,0:T(8,128)} %broadcast_in_dim.19), calls=%async_computation.1 | async-start | bytes 2097152 | tf_op jit(solution)/shard_map/all_to_all | solution.py:87
  106.9 0.0 copy-done.3
  106.9 0.6 stack.27.table_ref
  107.5 14.4 %all-to-all-done.1 = f32[8,2,64,256]{3,2,1,0:T(8,128)S(1)} async-done(((f32[8,2,64,256]{3,2,1,0:T(8,128)}), f32[8,2,64,256]{3,2,1,0:T(8,128)S(1)}, u32[]{:S(2)}, u32[]{:S(2)}) %all-to-all-start.1) | async-done | bytes 1048608 | tf_op jit(solution)/shard_map/all_to_all | solution.py:87
  121.9 0.1 copy.7
  122.0 1.3 copy.8
  123.4 17.0 %all-gather.2.cloned.1.call-done = f32[2,2048,256]{2,1,0:T(8,128)} async-done(((f32[2,256,256]{2,1,0:T(8,128)}), f32[2,2048,256]{2,1,0:T(8,128)}) %all-gather.2.cloned.1.call-update) | async-done | bytes 4194320 | tf_op jit(solution)/shard_map/all_gather | solution.py:92
  140.4 14.4 %shard_map.55 = f32[16,256,256]{2,1,0:T(8,128)} custom-call(s32[5,16]{1,0:T(8,128)} %stack.27.table_ref, f32[16,256,256]{2,1,0:T(8,128)} %bitcast.50, f32[16,256,256]{2,1,0:T(8,128)} %bitcast.45, f32[16,256,256]{2,1,0:T(8,128)} %bitcast.46, f32[4,256,256]{2,1,0:T(8,128)} %bitcast.48, f32[4,256,256]{2,1,0:T(8,128)} %bitcast.49, f32[16,256,256]{2,1,0:T(8,128)} %bitcast.47), custom_call_target="tpu_custom_call" | custom-call | tf_op jit(solution)/shard_map/pallas_call | solution.py:57
  (8 shorter events, 0.1 us)
Async XLA Ops:
  6.5 15.9 %copy-start = (f32[256,256]{1,0:T(8,128)S(1)}, f32[256,256]{1,0:T(8,128)}, u32[]{:S(2)}) copy-start(f32[256,256]{1,0:T(8,128)} %param.11) | copy-start | bytes 786436
  9.6 12.1 %copy-start.2 = (s32[2,8]{1,0:T(2,128)S(1)}, s32[2,8]{1,0:T(2,128)}, u32[]{:S(2)}) copy-start(s32[2,8]{1,0:T(2,128)} %param.8) | copy-start | bytes 196
  9.6 12.8 %copy-start.1 = (f32[2,256,256]{2,1,0:T(8,128)S(1)}, f32[2,256,256]{2,1,0:T(8,128)}, u32[]{:S(2)}) copy-start(f32[2,256,256]{2,1,0:T(8,128)} %param.10) | copy-start | bytes 1572868
  9.6 60.5 %all-to-all-start = ((f32[32,64,256]{2,1,0:T(8,128)}), f32[32,64,256]{2,1,0:T(8,128)S(1)}, u32[]{:S(2)}, u32[]{:S(2)}) async-start(f32[32,64,256]{2,1,0:T(8,128)} %bitcast.6), calls=%async_computation | async-start | bytes 4194304 | tf_op jit(solution)/shard_map/all_to_all | solution.py:72
  21.6 118.8 %all-gather.2.cloned.1.call-start = ((), (), s32[]{:S(2)}) async-start(), calls=%async_computation.2 | async-start | bytes 4718592 | tf_op jit(solution)/shard_map/all_gather | solution.py:92
  72.5 34.4 %copy-start.3 = (s32[2,16,1]{1,2,0:T(1,128)S(1)}, s32[2,16,1]{1,2,0:T(1,128)}, u32[]{:S(2)}) copy-start(s32[2,16,1]{1,2,0:T(1,128)} %param.9) | copy-start | bytes 388
  86.3 8.6 %collective-permute-start = (f32[2,64,256]{2,1,0:T(8,128)S(1)}, f32[2,64,256]{2,1,0:T(8,128)S(1)}, u32[]{:S(2)}, u32[]{:S(2)}) collective-permute-start(f32[2,64,256]{2,1,0:T(8,128)S(1)} %pad_maximum_fusion), channel_id=1, source_target_pairs={{0,0},{1,32},{2,64},{3,96},{4,128},{5,160},{6,192},{7,224},{32,1},... | collective-permute-start | bytes 393224 | tf_op jit(solution)/shard_map/ppermute | solution.py:85
  96.0 26.0 %all-to-all-start.1 = ((f32[8,2,64,256]{3,2,1,0:T(8,128)}), f32[8,2,64,256]{3,2,1,0:T(8,128)S(1)}, u32[]{:S(2)}, u32[]{:S(2)}) async-start(f32[8,2,64,256]{3,2,1,0:T(8,128)} %broadcast_in_dim.19), calls=%async_computation.1 | async-start | bytes 2097152 | tf_op jit(solution)/shard_map/all_to_all | solution.py:87
Sparse Core Ops, SparseCore 0:
  86.4 53.9 all-gather.1

commit v12 on v11

--- a/solution.py
+++ b/solution.py
@@ -9,6 +9,7 @@
 
 PER_CLASS = 2
 X_SIZE = 4
+SLOTS_PER_STEP = 2
 
 
 HIGHEST_PRECISION = lax.Precision.HIGHEST
@@ -22,18 +23,21 @@
     return jnp.einsum("ab,cb->ac", panel_rows_block, inverse, precision=HIGHEST_PRECISION)
 
 
-def tail_kernel(table_ref, stored_ref, left_one, left_two, right_one, right_two, panel_ref, out_ref):
-    slot = pl.program_id(0)
-    schur = lax.dot_general(
-        left_one[0], right_one[0], PLAIN_PRODUCT, precision=PRODUCT_PRECISION,
-        preferred_element_type=jnp.float32,
-    )
-    schur += lax.dot_general(
-        left_two[0], right_two[0], PLAIN_PRODUCT, precision=PRODUCT_PRECISION,
-        preferred_element_type=jnp.float32,
-    )
-    kept = stored_ref[0] - jnp.where(table_ref[2, slot] > 0, schur, 0.0)
-    out_ref[0] = jnp.where(table_ref[3, slot] > 0, panel_ref[0], kept)
+def tail_kernel(table_ref, stored_ref, *refs):
+    lefts, rights, panels, out_ref = refs[:4], refs[4:8], refs[8:10], refs[10]
+    step = pl.program_id(0)
+    for j in range(SLOTS_PER_STEP):
+        slot = step * SLOTS_PER_STEP + j
+        schur = lax.dot_general(
+            lefts[2 * j][0], rights[2 * j][0], PLAIN_PRODUCT, precision=PRODUCT_PRECISION,
+            preferred_element_type=jnp.float32,
+        )
+        schur += lax.dot_general(
+            lefts[2 * j + 1][0], rights[2 * j + 1][0], PLAIN_PRODUCT, precision=PRODUCT_PRECISION,
+            preferred_element_type=jnp.float32,
+        )
+        kept = stored_ref[j] - jnp.where(table_ref[2, slot] > 0, schur, 0.0)
+        out_ref[j] = jnp.where(table_ref[3, slot] > 0, panels[j][0], kept)
 
 
 def finish_slots(table, stored, rows, cols):
@@ -41,22 +45,34 @@
     head = rows.shape[0] // 2
     classes = cols.shape[0] // 2
     tile = (1, block, block)
+    pair = (SLOTS_PER_STEP, block, block)
+    left_specs = []
+    right_specs = []
+    panel_specs = []
+    for j in range(SLOTS_PER_STEP):
+        for f in range(2):
+            left_specs.append(
+                pl.BlockSpec(tile, lambda s, t, j=j, f=f: (f * head + t[0, s * SLOTS_PER_STEP + j], 0, 0))
+            )
+            right_specs.append(
+                pl.BlockSpec(tile, lambda s, t, j=j, f=f: (f * classes + t[1, s * SLOTS_PER_STEP + j], 0, 0))
+            )
+        panel_specs.append(
+            pl.BlockSpec(
+                tile,
+                lambda s, t, j=j: (t[4, 0] * head + jnp.minimum(s * SLOTS_PER_STEP + j, head - 1), 0, 0),
+            )
+        )
     spec = pltpu.PrefetchScalarGridSpec(
         num_scalar_prefetch=1,
-        grid=(slots,),
-        in_specs=[
-            pl.BlockSpec(tile, lambda s, t: (s, 0, 0)),
-            pl.BlockSpec(tile, lambda s, t: (t[0, s], 0, 0)),
-            pl.BlockSpec(tile, lambda s, t: (head + t[0, s], 0, 0)),
-            pl.BlockSpec(tile, lambda s, t: (t[1, s], 0, 0)),
-            pl.BlockSpec(tile, lambda s, t: (classes + t[1, s], 0, 0)),
-            pl.BlockSpec(tile, lambda s, t: (t[4, 0] * head + jnp.minimum(s, head - 1), 0, 0)),
-        ],
-        out_specs=pl.BlockSpec(tile, lambda s, t: (s, 0, 0)),
+        grid=(slots // SLOTS_PER_STEP,),
+        in_specs=[pl.BlockSpec(pair, lambda s, t: (s, 0, 0))] + left_specs + right_specs + panel_specs,
+        out_specs=pl.BlockSpec(pair, lambda s, t: (s, 0, 0)),
     )
+    operands = [rows] * (2 * SLOTS_PER_STEP) + [cols] * (2 * SLOTS_PER_STEP) + [rows] * SLOTS_PER_STEP
     return pl.pallas_call(
         tail_kernel, grid_spec=spec, out_shape=jax.ShapeDtypeStruct(stored.shape, stored.dtype)
-    )(table, stored, rows, rows, cols, cols, rows)
+    )(table, stored, *operands)
 
 
 def per_device(blocks, panel_rows, target_slots, diag_inverse, cross_block):

time: 163 us -> 160 us (0.982)
  Pallas kernels: 14.4 us -> 11.2 us
    pallas_call x1, Pallas kernels: 14.4 us -> 11.2 us  [finish_slots(): pl.pallas_call(tail_kernel, grid_spec=spec, out_shape=jax.ShapeDtypeStruc...]
where the time goes in v12:
time: 160 us; the launch traced here: 158 us
  waiting for transfers between devices  81.4 us (51%)
  starting transfers between devices  28.9 us (18%)
  blocking collectives  13.8 us (9%)
  between operations  13.5 us (8%)
  Pallas kernels  11.2 us (7%)
  local copies, waits for them, and re-layouts  6.19 us (4%)
  matrix products  2.78 us (2%)
    all_to_all x1, waiting for transfers between devices, per_device(): received = lax.all_to_all(pieces, COL_AXES, 0, 0, tiled=True)  47.3 us
    all_gather x1, waiting for transfers between devices, per_device(): both_rows = lax.all_gather(both_rows, ('zh', 'zl'), axis=1, tiled=True)  17 us
    all_to_all x1, waiting for transfers between devices, per_device(): class_pieces = lax.all_to_all(spread, 'row', 0, 0, tiled=True)  14.4 us
    all_gather x1, blocking collectives, per_device(): both_rows = lax.all_gather(both_pieces, 'x', axis=1, tiled=True)  13.8 us
    all_to_all x1, starting transfers between devices, per_device(): received = lax.all_to_all(pieces, COL_AXES, 0, 0, tiled=True)  12 us
    pallas_call x1, Pallas kernels, finish_slots(): pl.pallas_call(tail_kernel, grid_spec=spec, out_shape=jax.ShapeDtypeStruc...  11.2 us
    all_to_all x1, starting transfers between devices, per_device(): class_pieces = lax.all_to_all(spread, 'row', 0, 0, tiled=True)  10.9 us
    ppermute x1, starting transfers between devices, per_device(): swapped = lax.ppermute(both_pieces, ('row',) + CLASS_AXES, swap)  5.96 us
  transfers between devices with their start and end apart: 4, of which 4 were waited for; matrix products, arithmetic and copies ran while one was open for 3% of the time, Pallas kernels for 0%

profile of v12, /device:TPU:1, one launch (start us, length us, event | category | flops | bytes accessed | tf_op | source)
XLA Modules:
  0.0 158.4 jit_solution(5341939220314552435)
XLA Ops:
  6.5 0.0 copy-start
  6.5 3.1 %slice.51 = f32[8,1,256,256]{3,2,1,0:T(8,128)} slice(f32[16,1,256,256]{3,2,1,0:T(8,128)} %param.7), slice={[0:8], [0:1], [0:256], [0:256]} | slice | bytes 4194304 | tf_op jit(solution)/shard_map/slice | solution.py:85
  9.6 0.0 copy-start.2
  9.6 0.0 copy-start.1
  9.6 12.0 %all-to-all-start = ((f32[32,64,256]{2,1,0:T(8,128)}), f32[32,64,256]{2,1,0:T(8,128)S(1)}, u32[]{:S(2)}, u32[]{:S(2)}) async-start(f32[32,64,256]{2,1,0:T(8,128)} %bitcast.6), calls=%async_computation | async-start | bytes 4194304 | tf_op jit(solution)/shard_map/all_to_all | solution.py:88
  21.6 0.0 all-gather.2.cloned.1.call-start
  21.7 0.0 copy-done.2
  21.7 0.7 fusion.12
  22.4 0.0 copy-done
  22.4 0.0 copy-done.1
  22.4 0.4 fusion.2
  22.8 47.3 %all-to-all-done = f32[32,64,256]{2,1,0:T(8,128)S(1)} async-done(((f32[32,64,256]{2,1,0:T(8,128)}), f32[32,64,256]{2,1,0:T(8,128)S(1)}, u32[]{:S(2)}, u32[]{:S(2)}) %all-to-all-start) | async-done | bytes 2097184 | tf_op jit(solution)/shard_map/all_to_all | solution.py:88
  70.1 1.0 convolution_select_fusion.1
  71.1 0.4 convolution_subtract_fusion
  71.5 1.0 fusion
  72.5 0.0 copy-start.3
  72.5 13.8 %all_gather.6 = f32[2,256,256]{2,1,0:T(8,128)} all-gather(f32[2,64,256]{2,1,0:T(8,128)S(1)} %pad_maximum_fusion), channel_id=1, replica_groups=mesh['row'=8,'zh'=4,'zl'=2,'x'=4] {'x'}, dimensions={1}, use_global_device_ids=true | all-gather | bytes 655360 | tf_op jit(solution)/shard_map/all_gather | solution.py:107
  86.3 0.0 all-gather.2.cloned.1.call-update
  86.3 6.0 %collective-permute-start = (f32[2,64,256]{2,1,0:T(8,128)S(1)}, f32[2,64,256]{2,1,0:T(8,128)S(1)}, u32[]{:S(2)}, u32[]{:S(2)}) collective-permute-start(f32[2,64,256]{2,1,0:T(8,128)S(1)} %pad_maximum_fusion), channel_id=1, source_target_pairs={{0,0},{1,32},{2,64},{3,96},{4,128},{5,160},{6,192},{7,224},{32,1},... | collective-permute-start | bytes 393224 | tf_op jit(solution)/shard_map/ppermute | solution.py:101
  92.3 2.6 %collective-permute-done = f32[2,64,256]{2,1,0:T(8,128)S(1)} collective-permute-done((f32[2,64,256]{2,1,0:T(8,128)S(1)}, f32[2,64,256]{2,1,0:T(8,128)S(1)}, u32[]{:S(2)}, u32[]{:S(2)}) %collective-permute-start) | collective-permute-done | bytes 131104 | tf_op jit(solution)/shard_map/ppermute | solution.py:101
  94.9 1.1 broadcast_in_dim.19
  96.0 10.9 %all-to-all-start.1 = ((f32[8,2,64,256]{3,2,1,0:T(8,128)}), f32[8,2,64,256]{3,2,1,0:T(8,128)S(1)}, u32[]{:S(2)}, u32[]{:S(2)}) async-start(f32[8,2,64,256]{3,2,1,0:T(8,128)} %broadcast_in_dim.19), calls=%async_computation.1 | async-start | bytes 2097152 | tf_op jit(solution)/shard_map/all_to_all | solution.py:103
  106.9 0.0 copy-done.3
  106.9 0.6 stack.27.table_ref
  107.5 14.4 %all-to-all-done.1 = f32[8,2,64,256]{3,2,1,0:T(8,128)S(1)} async-done(((f32[8,2,64,256]{3,2,1,0:T(8,128)}), f32[8,2,64,256]{3,2,1,0:T(8,128)S(1)}, u32[]{:S(2)}, u32[]{:S(2)}) %all-to-all-start.1) | async-done | bytes 1048608 | tf_op jit(solution)/shard_map/all_to_all | solution.py:103
  121.9 0.1 copy.7
  122.0 1.3 copy.8
  123.4 17.0 %all-gather.2.cloned.1.call-done = f32[2,2048,256]{2,1,0:T(8,128)} async-done(((f32[2,256,256]{2,1,0:T(8,128)}), f32[2,2048,256]{2,1,0:T(8,128)}) %all-gather.2.cloned.1.call-update) | async-done | bytes 4194320 | tf_op jit(solution)/shard_map/all_gather | solution.py:108
  140.4 11.2 %shard_map.55 = f32[16,256,256]{2,1,0:T(8,128)} custom-call(s32[5,16]{1,0:T(8,128)} %stack.27.table_ref, f32[16,256,256]{2,1,0:T(8,128)} %bitcast.55, f32[16,256,256]{2,1,0:T(8,128)} %bitcast.45, f32[16,256,256]{2,1,0:T(8,128)} %bitcast.46, f32[16,256,256]{2,1,0:T(8,128)} %bitcast.47, f32[16,256,256]{2,1,0:T(8,128)} %bitcast.48, f32[4,256,256]{2,1,0:T(8,128)} %bitcast.51, ...), custom_call_target="tpu_custom_call" | custom-call | tf_op jit(solution)/shard_map/pallas_call | solution.py:73
  (8 shorter events, 0.1 us)
Async XLA Ops:
  6.5 15.9 %copy-start = (f32[256,256]{1,0:T(8,128)S(1)}, f32[256,256]{1,0:T(8,128)}, u32[]{:S(2)}) copy-start(f32[256,256]{1,0:T(8,128)} %param.11) | copy-start | bytes 786436
  9.6 12.1 %copy-start.2 = (s32[2,8]{1,0:T(2,128)S(1)}, s32[2,8]{1,0:T(2,128)}, u32[]{:S(2)}) copy-start(s32[2,8]{1,0:T(2,128)} %param.8) | copy-start | bytes 196
  9.6 12.8 %copy-start.1 = (f32[2,256,256]{2,1,0:T(8,128)S(1)}, f32[2,256,256]{2,1,0:T(8,128)}, u32[]{:S(2)}) copy-start(f32[2,256,256]{2,1,0:T(8,128)} %param.10) | copy-start | bytes 1572868
  9.6 60.5 %all-to-all-start = ((f32[32,64,256]{2,1,0:T(8,128)}), f32[32,64,256]{2,1,0:T(8,128)S(1)}, u32[]{:S(2)}, u32[]{:S(2)}) async-start(f32[32,64,256]{2,1,0:T(8,128)} %bitcast.6), calls=%async_computation | async-start | bytes 4194304 | tf_op jit(solution)/shard_map/all_to_all | solution.py:88
  21.6 118.8 %all-gather.2.cloned.1.call-start = ((), (), s32[]{:S(2)}) async-start(), calls=%async_computation.2 | async-start | bytes 4718592 | tf_op jit(solution)/shard_map/all_gather | solution.py:108
  72.5 34.4 %copy-start.3 = (s32[2,16,1]{1,2,0:T(1,128)S(1)}, s32[2,16,1]{1,2,0:T(1,128)}, u32[]{:S(2)}) copy-start(s32[2,16,1]{1,2,0:T(1,128)} %param.9) | copy-start | bytes 388
  86.3 8.6 %collective-permute-start = (f32[2,64,256]{2,1,0:T(8,128)S(1)}, f32[2,64,256]{2,1,0:T(8,128)S(1)}, u32[]{:S(2)}, u32[]{:S(2)}) collective-permute-start(f32[2,64,256]{2,1,0:T(8,128)S(1)} %pad_maximum_fusion), channel_id=1, source_target_pairs={{0,0},{1,32},{2,64},{3,96},{4,128},{5,160},{6,192},{7,224},{32,1},... | collective-permute-start | bytes 393224 | tf_op jit(solution)/shard_map/ppermute | solution.py:101
  96.0 26.0 %all-to-all-start.1 = ((f32[8,2,64,256]{3,2,1,0:T(8,128)}), f32[8,2,64,256]{3,2,1,0:T(8,128)S(1)}, u32[]{:S(2)}, u32[]{:S(2)}) async-start(f32[8,2,64,256]{3,2,1,0:T(8,128)} %broadcast_in_dim.19), calls=%async_computation.1 | async-start | bytes 2097152 | tf_op jit(solution)/shard_map/all_to_all | solution.py:103
Sparse Core Ops, SparseCore 0:
  86.4 53.9 all-gather.1

commit v13 on v12

--- a/solution.py
+++ b/solution.py
@@ -9,7 +9,7 @@
 
 PER_CLASS = 2
 X_SIZE = 4
-SLOTS_PER_STEP = 2
+SLOTS_PER_STEP = 4
 
 
 HIGHEST_PRECISION = lax.Precision.HIGHEST
@@ -24,7 +24,9 @@
 
 
 def tail_kernel(table_ref, stored_ref, *refs):
-    lefts, rights, panels, out_ref = refs[:4], refs[4:8], refs[8:10], refs[10]
+    pairs = 2 * SLOTS_PER_STEP
+    lefts, rights = refs[:pairs], refs[pairs:2 * pairs]
+    panels, out_ref = refs[2 * pairs:2 * pairs + SLOTS_PER_STEP], refs[-1]
     step = pl.program_id(0)
     for j in range(SLOTS_PER_STEP):
         slot = step * SLOTS_PER_STEP + j

time: 160 us -> 160 us (level)
  no operation moved by 1% of the time
where the time goes in v13:
time: 160 us; the launch traced here: 159 us
  waiting for transfers between devices  81.4 us (51%)
  starting transfers between devices  28.9 us (18%)
  blocking collectives  13.8 us (9%)
  between operations  13.6 us (8%)
  Pallas kernels  11.3 us (7%)
  local copies, waits for them, and re-layouts  6.19 us (4%)
  matrix products  2.78 us (2%)
    all_to_all x1, waiting for transfers between devices, per_device(): received = lax.all_to_all(pieces, COL_AXES, 0, 0, tiled=True)  47.3 us
    all_gather x1, waiting for transfers between devices, per_device(): both_rows = lax.all_gather(both_rows, ('zh', 'zl'), axis=1, tiled=True)  17 us
    all_to_all x1, waiting for transfers between devices, per_device(): class_pieces = lax.all_to_all(spread, 'row', 0, 0, tiled=True)  14.4 us
    all_gather x1, blocking collectives, per_device(): both_rows = lax.all_gather(both_pieces, 'x', axis=1, tiled=True)  13.8 us
    all_to_all x1, starting transfers between devices, per_device(): received = lax.all_to_all(pieces, COL_AXES, 0, 0, tiled=True)  12 us
    pallas_call x1, Pallas kernels, finish_slots(): pl.pallas_call(tail_kernel, grid_spec=spec, out_shape=jax.ShapeDtypeStruc...  11.3 us
    all_to_all x1, starting transfers between devices, per_device(): class_pieces = lax.all_to_all(spread, 'row', 0, 0, tiled=True)  10.9 us
    ppermute x1, starting transfers between devices, per_device(): swapped = lax.ppermute(both_pieces, ('row',) + CLASS_AXES, swap)  5.96 us
  transfers between devices with their start and end apart: 4, of which 4 were waited for; matrix products, arithmetic and copies ran while one was open for 3% of the time, Pallas kernels for 0%

profile of v13, /device:TPU:1, one launch (start us, length us, event | category | flops | bytes accessed | tf_op | source)
XLA Modules:
  0.0 158.5 jit_solution(15679274849868052391)
XLA Ops:
  6.5 0.0 copy-start
  6.5 3.1 %slice.51 = f32[8,1,256,256]{3,2,1,0:T(8,128)} slice(f32[16,1,256,256]{3,2,1,0:T(8,128)} %param.7), slice={[0:8], [0:1], [0:256], [0:256]} | slice | bytes 4194304 | tf_op jit(solution)/shard_map/slice | solution.py:87
  9.6 0.0 copy-start.2
  9.6 0.0 copy-start.1
  9.6 12.0 %all-to-all-start = ((f32[32,64,256]{2,1,0:T(8,128)}), f32[32,64,256]{2,1,0:T(8,128)S(1)}, u32[]{:S(2)}, u32[]{:S(2)}) async-start(f32[32,64,256]{2,1,0:T(8,128)} %bitcast.6), calls=%async_computation | async-start | bytes 4194304 | tf_op jit(solution)/shard_map/all_to_all | solution.py:90
  21.6 0.0 all-gather.2.cloned.1.call-start
  21.7 0.0 copy-done.2
  21.7 0.7 fusion.12
  22.4 0.0 copy-done
  22.4 0.0 copy-done.1
  22.4 0.4 fusion.2
  22.8 47.3 %all-to-all-done = f32[32,64,256]{2,1,0:T(8,128)S(1)} async-done(((f32[32,64,256]{2,1,0:T(8,128)}), f32[32,64,256]{2,1,0:T(8,128)S(1)}, u32[]{:S(2)}, u32[]{:S(2)}) %all-to-all-start) | async-done | bytes 2097184 | tf_op jit(solution)/shard_map/all_to_all | solution.py:90
  70.1 1.0 convolution_select_fusion.1
  71.1 0.4 convolution_subtract_fusion
  71.5 1.0 fusion
  72.5 0.0 copy-start.3
  72.5 13.8 %all_gather.6 = f32[2,256,256]{2,1,0:T(8,128)} all-gather(f32[2,64,256]{2,1,0:T(8,128)S(1)} %pad_maximum_fusion), channel_id=1, replica_groups=mesh['row'=8,'zh'=4,'zl'=2,'x'=4] {'x'}, dimensions={1}, use_global_device_ids=true | all-gather | bytes 655360 | tf_op jit(solution)/shard_map/all_gather | solution.py:109
  86.3 0.0 all-gather.2.cloned.1.call-update
  86.3 6.0 %collective-permute-start = (f32[2,64,256]{2,1,0:T(8,128)S(1)}, f32[2,64,256]{2,1,0:T(8,128)S(1)}, u32[]{:S(2)}, u32[]{:S(2)}) collective-permute-start(f32[2,64,256]{2,1,0:T(8,128)S(1)} %pad_maximum_fusion), channel_id=1, source_target_pairs={{0,0},{1,32},{2,64},{3,96},{4,128},{5,160},{6,192},{7,224},{32,1},... | collective-permute-start | bytes 393224 | tf_op jit(solution)/shard_map/ppermute | solution.py:103
  92.3 2.6 %collective-permute-done = f32[2,64,256]{2,1,0:T(8,128)S(1)} collective-permute-done((f32[2,64,256]{2,1,0:T(8,128)S(1)}, f32[2,64,256]{2,1,0:T(8,128)S(1)}, u32[]{:S(2)}, u32[]{:S(2)}) %collective-permute-start) | collective-permute-done | bytes 131104 | tf_op jit(solution)/shard_map/ppermute | solution.py:103
  94.9 1.1 broadcast_in_dim.19
  96.0 10.9 %all-to-all-start.1 = ((f32[8,2,64,256]{3,2,1,0:T(8,128)}), f32[8,2,64,256]{3,2,1,0:T(8,128)S(1)}, u32[]{:S(2)}, u32[]{:S(2)}) async-start(f32[8,2,64,256]{3,2,1,0:T(8,128)} %broadcast_in_dim.19), calls=%async_computation.1 | async-start | bytes 2097152 | tf_op jit(solution)/shard_map/all_to_all | solution.py:105
  106.9 0.0 copy-done.3
  106.9 0.6 stack.27.table_ref
  107.5 14.4 %all-to-all-done.1 = f32[8,2,64,256]{3,2,1,0:T(8,128)S(1)} async-done(((f32[8,2,64,256]{3,2,1,0:T(8,128)}), f32[8,2,64,256]{3,2,1,0:T(8,128)S(1)}, u32[]{:S(2)}, u32[]{:S(2)}) %all-to-all-start.1) | async-done | bytes 1048608 | tf_op jit(solution)/shard_map/all_to_all | solution.py:105
  121.9 0.1 copy.7
  122.0 1.3 copy.8
  123.4 17.0 %all-gather.2.cloned.1.call-done = f32[2,2048,256]{2,1,0:T(8,128)} async-done(((f32[2,256,256]{2,1,0:T(8,128)}), f32[2,2048,256]{2,1,0:T(8,128)}) %all-gather.2.cloned.1.call-update) | async-done | bytes 4194320 | tf_op jit(solution)/shard_map/all_gather | solution.py:110
  140.4 11.3 %shard_map.55 = f32[16,256,256]{2,1,0:T(8,128)} custom-call(s32[5,16]{1,0:T(8,128)} %stack.27.table_ref, f32[16,256,256]{2,1,0:T(8,128)} %bitcast.65, f32[16,256,256]{2,1,0:T(8,128)} %bitcast.45, f32[16,256,256]{2,1,0:T(8,128)} %bitcast.46, f32[16,256,256]{2,1,0:T(8,128)} %bitcast.47, f32[16,256,256]{2,1,0:T(8,128)} %bitcast.48, f32[16,256,256]{2,1,0:T(8,128)} %bitcast.49, ...), custom_call_target="tpu_custom_call" | custom-call | tf_op jit(solution)/shard_map/pallas_call | solution.py:75
  (8 shorter events, 0.1 us)
Async XLA Ops:
  6.5 15.9 %copy-start = (f32[256,256]{1,0:T(8,128)S(1)}, f32[256,256]{1,0:T(8,128)}, u32[]{:S(2)}) copy-start(f32[256,256]{1,0:T(8,128)} %param.11) | copy-start | bytes 786436
  9.6 12.1 %copy-start.2 = (s32[2,8]{1,0:T(2,128)S(1)}, s32[2,8]{1,0:T(2,128)}, u32[]{:S(2)}) copy-start(s32[2,8]{1,0:T(2,128)} %param.8) | copy-start | bytes 196
  9.6 12.8 %copy-start.1 = (f32[2,256,256]{2,1,0:T(8,128)S(1)}, f32[2,256,256]{2,1,0:T(8,128)}, u32[]{:S(2)}) copy-start(f32[2,256,256]{2,1,0:T(8,128)} %param.10) | copy-start | bytes 1572868
  9.6 60.5 %all-to-all-start = ((f32[32,64,256]{2,1,0:T(8,128)}), f32[32,64,256]{2,1,0:T(8,128)S(1)}, u32[]{:S(2)}, u32[]{:S(2)}) async-start(f32[32,64,256]{2,1,0:T(8,128)} %bitcast.6), calls=%async_computation | async-start | bytes 4194304 | tf_op jit(solution)/shard_map/all_to_all | solution.py:90
  21.6 118.8 %all-gather.2.cloned.1.call-start = ((), (), s32[]{:S(2)}) async-start(), calls=%async_computation.2 | async-start | bytes 4718592 | tf_op jit(solution)/shard_map/all_gather | solution.py:110
  72.5 34.4 %copy-start.3 = (s32[2,16,1]{1,2,0:T(1,128)S(1)}, s32[2,16,1]{1,2,0:T(1,128)}, u32[]{:S(2)}) copy-start(s32[2,16,1]{1,2,0:T(1,128)} %param.9) | copy-start | bytes 388
  86.3 8.6 %collective-permute-start = (f32[2,64,256]{2,1,0:T(8,128)S(1)}, f32[2,64,256]{2,1,0:T(8,128)S(1)}, u32[]{:S(2)}, u32[]{:S(2)}) collective-permute-start(f32[2,64,256]{2,1,0:T(8,128)S(1)} %pad_maximum_fusion), channel_id=1, source_target_pairs={{0,0},{1,32},{2,64},{3,96},{4,128},{5,160},{6,192},{7,224},{32,1},... | collective-permute-start | bytes 393224 | tf_op jit(solution)/shard_map/ppermute | solution.py:103
  96.0 26.0 %all-to-all-start.1 = ((f32[8,2,64,256]{3,2,1,0:T(8,128)}), f32[8,2,64,256]{3,2,1,0:T(8,128)S(1)}, u32[]{:S(2)}, u32[]{:S(2)}) async-start(f32[8,2,64,256]{3,2,1,0:T(8,128)} %broadcast_in_dim.19), calls=%async_computation.1 | async-start | bytes 2097152 | tf_op jit(solution)/shard_map/all_to_all | solution.py:105
Sparse Core Ops, SparseCore 0:
  86.4 53.9 all-gather.1

commit v14 on v12

--- a/solution.py
+++ b/solution.py
@@ -104,7 +104,21 @@
     per_slot = block // chunk
     class_pieces = class_pieces.reshape(PER_CLASS, per_slot, 2, chunk, block)
     both_cols = class_pieces.transpose(2, 0, 1, 3, 4).reshape(2, PER_CLASS, block, block)
-    both_rows = lax.all_gather(both_pieces, "x", axis=1, tiled=True)
+    x_ring = lax.axis_size("x")
+    x_place = lax.axis_index("x")
+    forward = [(i, (i + 1) % x_ring) for i in range(x_ring)]
+    backward = [(i, (i - 1) % x_ring) for i in range(x_ring)]
+    by_offset = [both_pieces] * x_ring
+    ahead = both_pieces
+    behind = both_pieces
+    for step in range(1, x_ring // 2 + 1):
+        ahead = lax.ppermute(ahead, "x", forward)
+        by_offset[x_ring - step] = ahead
+        if step < x_ring - step:
+            behind = lax.ppermute(behind, "x", backward)
+            by_offset[step] = behind
+    both_rows = jnp.roll(jnp.stack(by_offset, axis=1), x_place, axis=1)
+    both_rows = both_rows.reshape(2, x_ring * chunk, block)
     both_rows = lax.all_gather(both_rows, ("zh", "zl"), axis=1, tiled=True)
     both_rows = both_rows.reshape(2, slot_count, block, block)
     class_start = column // row_count * PER_CLASS

time: 160 us -> 159 us (level)
  blocking collectives: 13.8 us -> 0 us
  waiting for transfers between devices: 81.4 us -> 89.6 us
  starting transfers between devices: 28.9 us -> 32.8 us
    all_gather x1 -> x0, blocking collectives: 13.8 us -> none  [per_device(): both_rows = lax.all_gather(both_pieces, 'x', axis=1, tiled=True)]
    ppermute x0 -> x3, waiting for transfers between devices: none -> 7.27 us  [the longest x2 6.67 us: per_device(): ahead = lax.ppermute(ahead, 'x', forward)]
    ppermute x0 -> x3, starting transfers between devices: none -> 4.58 us  [the longest x1 2.46 us: per_device(): behind = lax.ppermute(behind, 'x', backward)]
    ppermute x1, starting transfers between devices: 5.96 us -> 3.55 us  [per_device(): swapped = lax.ppermute(both_pieces, ('row',) + CLASS_AXES, swap)]
    all_to_all x1, starting transfers between devices: 10.9 us -> 12.6 us  [per_device(): class_pieces = lax.all_to_all(spread, 'row', 0, 0, tiled=True)]
  transfers between devices with their start and end apart: 4 -> 7, of which waited for: 4 -> 7; matrix products, arithmetic and copies ran while one was open for 3% -> 3% of each run, Pallas kernels for 0% -> 0%
where the time goes in v14:
time: 159 us; the launch traced here: 158 us
  waiting for transfers between devices  89.6 us (56%)
  starting transfers between devices  32.8 us (21%)
  between operations  13.6 us (9%)
  Pallas kernels  11.2 us (7%)
  local copies, waits for them, and re-layouts  7.18 us (5%)
  matrix products  2.76 us (2%)
    all_to_all x1, waiting for transfers between devices, per_device(): received = lax.all_to_all(pieces, COL_AXES, 0, 0, tiled=True)  47.3 us
    all_gather x1, waiting for transfers between devices, per_device(): both_rows = lax.all_gather(both_rows, ('zh', 'zl'), axis=1, tiled=True)  17.9 us
    all_to_all x1, waiting for transfers between devices, per_device(): class_pieces = lax.all_to_all(spread, 'row', 0, 0, tiled=True)  14.4 us
    all_to_all x1, starting transfers between devices, per_device(): class_pieces = lax.all_to_all(spread, 'row', 0, 0, tiled=True)  12.6 us
    all_to_all x1, starting transfers between devices, per_device(): received = lax.all_to_all(pieces, COL_AXES, 0, 0, tiled=True)  12 us
    pallas_call x1, Pallas kernels, finish_slots(): pl.pallas_call(tail_kernel, grid_spec=spec, out_shape=jax.ShapeDtypeStruc...  11.2 us
    ppermute x2, waiting for transfers between devices, per_device(): ahead = lax.ppermute(ahead, 'x', forward)  6.67 us
    ppermute x1, starting transfers between devices, per_device(): swapped = lax.ppermute(both_pieces, ('row',) + CLASS_AXES, swap)  3.55 us
  transfers between devices with their start and end apart: 7, of which 7 were waited for; matrix products, arithmetic and copies ran while one was open for 3% of the time, Pallas kernels for 0%

profile of v14, /device:TPU:1, one launch (start us, length us, event | category | flops | bytes accessed | tf_op | source)
XLA Modules:
  0.0 157.9 jit_solution(2789686140029651050)
XLA Ops:
  6.5 0.0 copy-start
  6.5 3.1 %slice.51 = f32[8,1,256,256]{3,2,1,0:T(8,128)} slice(f32[16,1,256,256]{3,2,1,0:T(8,128)} %param.7), slice={[0:8], [0:1], [0:256], [0:256]} | slice | bytes 4194304 | tf_op jit(solution)/shard_map/slice | solution.py:85
  9.6 0.0 copy-start.2
  9.6 0.0 copy-start.1
  9.6 12.0 %all-to-all-start = ((f32[32,64,256]{2,1,0:T(8,128)}), f32[32,64,256]{2,1,0:T(8,128)S(1)}, u32[]{:S(2)}, u32[]{:S(2)}) async-start(f32[32,64,256]{2,1,0:T(8,128)} %bitcast.6), calls=%async_computation | async-start | bytes 4194304 | tf_op jit(solution)/shard_map/all_to_all | solution.py:88
  21.6 0.0 all-gather.2.cloned.1.call-start
  21.7 0.0 copy-done.2
  21.7 0.7 fusion.12
  22.4 0.0 copy-done
  22.4 0.0 copy-done.1
  22.4 0.4 fusion.2
  22.8 47.3 %all-to-all-done = f32[32,64,256]{2,1,0:T(8,128)S(1)} async-done(((f32[32,64,256]{2,1,0:T(8,128)}), f32[32,64,256]{2,1,0:T(8,128)S(1)}, u32[]{:S(2)}, u32[]{:S(2)}) %all-to-all-start) | async-done | bytes 2097184 | tf_op jit(solution)/shard_map/all_to_all | solution.py:88
  70.1 0.9 convolution_select_fusion.1
  71.0 0.4 convolution_subtract_fusion
  71.4 1.1 fusion
  72.5 2.1 %collective-permute-start.1 = (f32[2,64,256]{2,1,0:T(8,128)S(1)}, f32[2,64,256]{2,1,0:T(8,128)S(1)}, u32[]{:S(2)}, u32[]{:S(2)}) collective-permute-start(f32[2,64,256]{2,1,0:T(8,128)S(1)} %pad_maximum_fusion), channel_id=1, source_target_pairs={{0,1},{1,2},{2,3},{3,0},{4,5},{5,6},{6,7},{7,4},{8,9},{9,10},{10,1... | collective-permute-start | bytes 393224 | tf_op jit(solution)/shard_map/ppermute | solution.py:115
  74.6 2.5 %collective-permute-start = (f32[2,64,256]{2,1,0:T(8,128)S(1)}, f32[2,64,256]{2,1,0:T(8,128)S(1)}, u32[]{:S(2)}, u32[]{:S(2)}) collective-permute-start(f32[2,64,256]{2,1,0:T(8,128)S(1)} %pad_maximum_fusion), channel_id=1, source_target_pairs={{0,3},{1,0},{2,1},{3,2},{4,7},{5,4},{6,5},{7,6},{8,11},{9,8},{10,9... | collective-permute-start | bytes 393224 | tf_op jit(solution)/shard_map/ppermute | solution.py:118
  77.1 2.3 %collective-permute-done.1 = f32[2,64,256]{2,1,0:T(8,128)S(1)} collective-permute-done((f32[2,64,256]{2,1,0:T(8,128)S(1)}, f32[2,64,256]{2,1,0:T(8,128)S(1)}, u32[]{:S(2)}, u32[]{:S(2)}) %collective-permute-start.1) | collective-permute-done | bytes 131104 | tf_op jit(solution)/shard_map/ppermute | solution.py:115
  79.3 0.0 collective-permute-start.2
  79.3 0.6 collective-permute-done
  79.9 4.4 %collective-permute-done.2 = f32[2,64,256]{2,1,0:T(8,128)S(1)} collective-permute-done((f32[2,64,256]{2,1,0:T(8,128)S(1)}, f32[2,64,256]{2,1,0:T(8,128)S(1)}, u32[]{:S(2)}, u32[]{:S(2)}) %collective-permute-start.2) | collective-permute-done | bytes 131104 | tf_op jit(solution)/shard_map/ppermute | solution.py:115
  84.5 0.9 copy.7
  85.4 0.0 copy-start.3
  85.4 0.0 all-gather.2.cloned.1.call-update
  85.4 3.5 %collective-permute-start.3 = (f32[2,64,256]{2,1,0:T(8,128)S(1)}, f32[2,64,256]{2,1,0:T(8,128)S(1)}, u32[]{:S(2)}, u32[]{:S(2)}) collective-permute-start(f32[2,64,256]{2,1,0:T(8,128)S(1)} %pad_maximum_fusion), channel_id=1, source_target_pairs={{0,0},{1,32},{2,64},{3,96},{4,128},{5,160},{6,192},{7,224},{32,1},... | collective-permute-start | bytes 393224 | tf_op jit(solution)/shard_map/ppermute | solution.py:101
  89.0 2.7 %collective-permute-done.3 = f32[2,64,256]{2,1,0:T(8,128)S(1)} collective-permute-done((f32[2,64,256]{2,1,0:T(8,128)S(1)}, f32[2,64,256]{2,1,0:T(8,128)S(1)}, u32[]{:S(2)}, u32[]{:S(2)}) %collective-permute-start.3) | collective-permute-done | bytes 131104 | tf_op jit(solution)/shard_map/ppermute | solution.py:101
  91.7 1.1 broadcast_in_dim.19
  92.8 12.6 %all-to-all-start.1 = ((f32[8,2,64,256]{3,2,1,0:T(8,128)}), f32[8,2,64,256]{3,2,1,0:T(8,128)S(1)}, u32[]{:S(2)}, u32[]{:S(2)}) async-start(f32[8,2,64,256]{3,2,1,0:T(8,128)} %broadcast_in_dim.19), calls=%async_computation.1 | async-start | bytes 2097152 | tf_op jit(solution)/shard_map/all_to_all | solution.py:103
  105.4 0.0 copy-done.3
  105.5 0.6 stack.40.table_ref
  106.1 14.4 %all-to-all-done.1 = f32[8,2,64,256]{3,2,1,0:T(8,128)S(1)} async-done(((f32[8,2,64,256]{3,2,1,0:T(8,128)}), f32[8,2,64,256]{3,2,1,0:T(8,128)S(1)}, u32[]{:S(2)}, u32[]{:S(2)}) %all-to-all-start.1) | async-done | bytes 1048608 | tf_op jit(solution)/shard_map/all_to_all | solution.py:103
  120.5 0.1 copy.8
  120.6 1.3 copy.9
  121.9 17.9 %all-gather.2.cloned.1.call-done = f32[2,2048,256]{2,1,0:T(8,128)} async-done(((f32[2,256,256]{2,1,0:T(8,128)}), f32[2,2048,256]{2,1,0:T(8,128)}) %all-gather.2.cloned.1.call-update) | async-done | bytes 4194320 | tf_op jit(solution)/shard_map/all_gather | solution.py:122
  139.8 11.2 %shard_map.55 = f32[16,256,256]{2,1,0:T(8,128)} custom-call(s32[5,16]{1,0:T(8,128)} %stack.40.table_ref, f32[16,256,256]{2,1,0:T(8,128)} %bitcast.68, f32[16,256,256]{2,1,0:T(8,128)} %bitcast.58, f32[16,256,256]{2,1,0:T(8,128)} %bitcast.59, f32[16,256,256]{2,1,0:T(8,128)} %bitcast.60, f32[16,256,256]{2,1,0:T(8,128)} %bitcast.61, f32[4,256,256]{2,1,0:T(8,128)} %bitcast.64, ...), custom_call_target="tpu_custom_call" | custom-call | tf_op jit(solution)/shard_map/pallas_call | solution.py:73
  (17 shorter events, 0.2 us)
Async XLA Ops:
  6.5 15.9 %copy-start = (f32[256,256]{1,0:T(8,128)S(1)}, f32[256,256]{1,0:T(8,128)}, u32[]{:S(2)}) copy-start(f32[256,256]{1,0:T(8,128)} %param.11) | copy-start | bytes 786436
  9.6 12.1 %copy-start.2 = (s32[2,8]{1,0:T(2,128)S(1)}, s32[2,8]{1,0:T(2,128)}, u32[]{:S(2)}) copy-start(s32[2,8]{1,0:T(2,128)} %param.8) | copy-start | bytes 196
  9.6 12.8 %copy-start.1 = (f32[2,256,256]{2,1,0:T(8,128)S(1)}, f32[2,256,256]{2,1,0:T(8,128)}, u32[]{:S(2)}) copy-start(f32[2,256,256]{2,1,0:T(8,128)} %param.10) | copy-start | bytes 1572868
  9.6 60.5 %all-to-all-start = ((f32[32,64,256]{2,1,0:T(8,128)}), f32[32,64,256]{2,1,0:T(8,128)S(1)}, u32[]{:S(2)}, u32[]{:S(2)}) async-start(f32[32,64,256]{2,1,0:T(8,128)} %bitcast.6), calls=%async_computation | async-start | bytes 4194304 | tf_op jit(solution)/shard_map/all_to_all | solution.py:88
  21.6 118.2 %all-gather.2.cloned.1.call-start = ((), (), s32[]{:S(2)}) async-start(), calls=%async_computation.2 | async-start | bytes 4718592 | tf_op jit(solution)/shard_map/all_gather | solution.py:122
  72.5 6.8 %collective-permute-start.1 = (f32[2,64,256]{2,1,0:T(8,128)S(1)}, f32[2,64,256]{2,1,0:T(8,128)S(1)}, u32[]{:S(2)}, u32[]{:S(2)}) collective-permute-start(f32[2,64,256]{2,1,0:T(8,128)S(1)} %pad_maximum_fusion), channel_id=1, source_target_pairs={{0,1},{1,2},{2,3},{3,0},{4,5},{5,6},{6,7},{7,4},{8,9},{9,10},{10,1... | collective-permute-start | bytes 393224 | tf_op jit(solution)/shard_map/ppermute | solution.py:115
  74.6 5.3 %collective-permute-start = (f32[2,64,256]{2,1,0:T(8,128)S(1)}, f32[2,64,256]{2,1,0:T(8,128)S(1)}, u32[]{:S(2)}, u32[]{:S(2)}) collective-permute-start(f32[2,64,256]{2,1,0:T(8,128)S(1)} %pad_maximum_fusion), channel_id=1, source_target_pairs={{0,3},{1,0},{2,1},{3,2},{4,7},{5,4},{6,5},{7,6},{8,11},{9,8},{10,9... | collective-permute-start | bytes 393224 | tf_op jit(solution)/shard_map/ppermute | solution.py:118
  79.3 5.0 %collective-permute-start.2 = (f32[2,64,256]{2,1,0:T(8,128)S(1)}, f32[2,64,256]{2,1,0:T(8,128)S(1)}, u32[]{:S(2)}, u32[]{:S(2)}) collective-permute-start(f32[2,64,256]{2,1,0:T(8,128)S(1)} %collective-permute-done.1), channel_id=1, source_target_pairs={{0,1},{1,2},{2,3},{3,0},{4,5},{5,6},{6,7},{7,4},{8,9},{9,10},{10,1... | collective-permute-start | bytes 393224 | tf_op jit(solution)/shard_map/ppermute | solution.py:115
  85.4 20.0 %copy-start.3 = (s32[2,16,1]{1,2,0:T(1,128)S(1)}, s32[2,16,1]{1,2,0:T(1,128)}, u32[]{:S(2)}) copy-start(s32[2,16,1]{1,2,0:T(1,128)} %param.9) | copy-start | bytes 388
  85.4 6.3 %collective-permute-start.3 = (f32[2,64,256]{2,1,0:T(8,128)S(1)}, f32[2,64,256]{2,1,0:T(8,128)S(1)}, u32[]{:S(2)}, u32[]{:S(2)}) collective-permute-start(f32[2,64,256]{2,1,0:T(8,128)S(1)} %pad_maximum_fusion), channel_id=1, source_target_pairs={{0,0},{1,32},{2,64},{3,96},{4,128},{5,160},{6,192},{7,224},{32,1},... | collective-permute-start | bytes 393224 | tf_op jit(solution)/shard_map/ppermute | solution.py:101
  92.8 27.7 %all-to-all-start.1 = ((f32[8,2,64,256]{3,2,1,0:T(8,128)}), f32[8,2,64,256]{3,2,1,0:T(8,128)S(1)}, u32[]{:S(2)}, u32[]{:S(2)}) async-start(f32[8,2,64,256]{3,2,1,0:T(8,128)} %broadcast_in_dim.19), calls=%async_computation.1 | async-start | bytes 2097152 | tf_op jit(solution)/shard_map/all_to_all | solution.py:103
Sparse Core Ops, SparseCore 0:
  85.5 54.2 all-gather.1

commit v15 on v14

--- a/solution.py
+++ b/solution.py
@@ -23,56 +23,43 @@
     return jnp.einsum("ab,cb->ac", panel_rows_block, inverse, precision=HIGHEST_PRECISION)
 
 
-def tail_kernel(table_ref, stored_ref, *refs):
-    lefts, rights, panels, out_ref = refs[:4], refs[4:8], refs[8:10], refs[10]
+def tail_kernel(table_ref, stored_ref, rows_ref, cols_ref, out_ref):
+    head = rows_ref.shape[0] // 2
+    classes = cols_ref.shape[0] // 2
     step = pl.program_id(0)
     for j in range(SLOTS_PER_STEP):
         slot = step * SLOTS_PER_STEP + j
+        left = table_ref[0, slot]
+        right = table_ref[1, slot]
         schur = lax.dot_general(
-            lefts[2 * j][0], rights[2 * j][0], PLAIN_PRODUCT, precision=PRODUCT_PRECISION,
+            rows_ref[left], cols_ref[right], PLAIN_PRODUCT, precision=PRODUCT_PRECISION,
             preferred_element_type=jnp.float32,
         )
         schur += lax.dot_general(
-            lefts[2 * j + 1][0], rights[2 * j + 1][0], PLAIN_PRODUCT, precision=PRODUCT_PRECISION,
-            preferred_element_type=jnp.float32,
+            rows_ref[head + left], cols_ref[classes + right], PLAIN_PRODUCT,
+            precision=PRODUCT_PRECISION, preferred_element_type=jnp.float32,
         )
         kept = stored_ref[j] - jnp.where(table_ref[2, slot] > 0, schur, 0.0)
-        out_ref[j] = jnp.where(table_ref[3, slot] > 0, panels[j][0], kept)
+        panel = rows_ref[table_ref[4, 0] * head + jnp.minimum(slot, head - 1)]
+        out_ref[j] = jnp.where(table_ref[3, slot] > 0, panel, kept)
 
 
 def finish_slots(table, stored, rows, cols):
     slots, block, _ = stored.shape
-    head = rows.shape[0] // 2
-    classes = cols.shape[0] // 2
-    tile = (1, block, block)
     pair = (SLOTS_PER_STEP, block, block)
-    left_specs = []
-    right_specs = []
-    panel_specs = []
-    for j in range(SLOTS_PER_STEP):
-        for f in range(2):
-            left_specs.append(
-                pl.BlockSpec(tile, lambda s, t, j=j, f=f: (f * head + t[0, s * SLOTS_PER_STEP + j], 0, 0))
-            )
-            right_specs.append(
-                pl.BlockSpec(tile, lambda s, t, j=j, f=f: (f * classes + t[1, s * SLOTS_PER_STEP + j], 0, 0))
-            )
-        panel_specs.append(
-            pl.BlockSpec(
-                tile,
-                lambda s, t, j=j: (t[4, 0] * head + jnp.minimum(s * SLOTS_PER_STEP + j, head - 1), 0, 0),
-            )
-        )
     spec = pltpu.PrefetchScalarGridSpec(
         num_scalar_prefetch=1,
         grid=(slots // SLOTS_PER_STEP,),
-        in_specs=[pl.BlockSpec(pair, lambda s, t: (s, 0, 0))] + left_specs + right_specs + panel_specs,
+        in_specs=[
+            pl.BlockSpec(pair, lambda s, t: (s, 0, 0)),
+            pl.BlockSpec(rows.shape, lambda s, t: (0, 0, 0)),
+            pl.BlockSpec(cols.shape, lambda s, t: (0, 0, 0)),
+        ],
         out_specs=pl.BlockSpec(pair, lambda s, t: (s, 0, 0)),
     )
-    operands = [rows] * (2 * SLOTS_PER_STEP) + [cols] * (2 * SLOTS_PER_STEP) + [rows] * SLOTS_PER_STEP
     return pl.pallas_call(
         tail_kernel, grid_spec=spec, out_shape=jax.ShapeDtypeStruct(stored.shape, stored.dtype)
-    )(table, stored, *operands)
+    )(table, stored, rows, cols)
 
 
 def per_device(blocks, panel_rows, target_slots, diag_inverse, cross_block):

time: 159 us -> 158 us (level)
  no operation moved by 1% of the time
where the time goes in v15:
time: 158 us
  waiting for transfers between devices  89.6 us (57%)
  starting transfers between devices  32.8 us (21%)
  between operations  13.6 us (9%)
  Pallas kernels  11.2 us (7%)
  local copies, waits for them, and re-layouts  7.18 us (5%)
  matrix products  2.76 us (2%)
    all_to_all x1, waiting for transfers between devices, per_device(): received = lax.all_to_all(pieces, COL_AXES, 0, 0, tiled=True)  47.3 us
    all_gather x1, waiting for transfers between devices, per_device(): both_rows = lax.all_gather(both_rows, ('zh', 'zl'), axis=1, tiled=True)  17.9 us
    all_to_all x1, waiting for transfers between devices, per_device(): class_pieces = lax.all_to_all(spread, 'row', 0, 0, tiled=True)  14.4 us
    all_to_all x1, starting transfers between devices, per_device(): class_pieces = lax.all_to_all(spread, 'row', 0, 0, tiled=True)  12.6 us
    all_to_all x1, starting transfers between devices, per_device(): received = lax.all_to_all(pieces, COL_AXES, 0, 0, tiled=True)  12 us
    pallas_call x1, Pallas kernels, finish_slots(): pl.pallas_call(tail_kernel, grid_spec=spec, out_shape=jax.ShapeDtypeStruc...  11.2 us
    ppermute x2, waiting for transfers between devices, per_device(): ahead = lax.ppermute(ahead, 'x', forward)  6.67 us
    ppermute x1, starting transfers between devices, per_device(): swapped = lax.ppermute(both_pieces, ('row',) + CLASS_AXES, swap)  3.55 us
  transfers between devices with their start and end apart: 7, of which 7 were waited for; matrix products, arithmetic and copies ran while one was open for 3% of the time, Pallas kernels for 0%

profile of v15, /device:TPU:1, one launch (start us, length us, event | category | flops | bytes accessed | tf_op | source)
XLA Modules:
  0.0 157.9 jit_solution(12666799590131183316)
XLA Ops:
  6.5 0.0 copy-start
  6.5 3.1 %slice.51 = f32[8,1,256,256]{3,2,1,0:T(8,128)} slice(f32[16,1,256,256]{3,2,1,0:T(8,128)} %param.7), slice={[0:8], [0:1], [0:256], [0:256]} | slice | bytes 4194304 | tf_op jit(solution)/shard_map/slice | solution.py:72
  9.6 0.0 copy-start.2
  9.6 0.0 copy-start.1
  9.6 12.0 %all-to-all-start = ((f32[32,64,256]{2,1,0:T(8,128)}), f32[32,64,256]{2,1,0:T(8,128)S(1)}, u32[]{:S(2)}, u32[]{:S(2)}) async-start(f32[32,64,256]{2,1,0:T(8,128)} %bitcast.6), calls=%async_computation | async-start | bytes 4194304 | tf_op jit(solution)/shard_map/all_to_all | solution.py:75
  21.6 0.0 all-gather.2.cloned.1.call-start
  21.7 0.0 copy-done.2
  21.7 0.7 fusion.12
  22.4 0.0 copy-done
  22.4 0.0 copy-done.1
  22.4 0.4 fusion.2
  22.8 47.3 %all-to-all-done = f32[32,64,256]{2,1,0:T(8,128)S(1)} async-done(((f32[32,64,256]{2,1,0:T(8,128)}), f32[32,64,256]{2,1,0:T(8,128)S(1)}, u32[]{:S(2)}, u32[]{:S(2)}) %all-to-all-start) | async-done | bytes 2097184 | tf_op jit(solution)/shard_map/all_to_all | solution.py:75
  70.1 0.9 convolution_select_fusion.1
  71.0 0.4 convolution_subtract_fusion
  71.4 1.1 fusion
  72.5 2.1 %collective-permute-start.1 = (f32[2,64,256]{2,1,0:T(8,128)S(1)}, f32[2,64,256]{2,1,0:T(8,128)S(1)}, u32[]{:S(2)}, u32[]{:S(2)}) collective-permute-start(f32[2,64,256]{2,1,0:T(8,128)S(1)} %pad_maximum_fusion), channel_id=1, source_target_pairs={{0,1},{1,2},{2,3},{3,0},{4,5},{5,6},{6,7},{7,4},{8,9},{9,10},{10,1... | collective-permute-start | bytes 393224 | tf_op jit(solution)/shard_map/ppermute | solution.py:102
  74.6 2.5 %collective-permute-start = (f32[2,64,256]{2,1,0:T(8,128)S(1)}, f32[2,64,256]{2,1,0:T(8,128)S(1)}, u32[]{:S(2)}, u32[]{:S(2)}) collective-permute-start(f32[2,64,256]{2,1,0:T(8,128)S(1)} %pad_maximum_fusion), channel_id=1, source_target_pairs={{0,3},{1,0},{2,1},{3,2},{4,7},{5,4},{6,5},{7,6},{8,11},{9,8},{10,9... | collective-permute-start | bytes 393224 | tf_op jit(solution)/shard_map/ppermute | solution.py:105
  77.1 2.3 %collective-permute-done.1 = f32[2,64,256]{2,1,0:T(8,128)S(1)} collective-permute-done((f32[2,64,256]{2,1,0:T(8,128)S(1)}, f32[2,64,256]{2,1,0:T(8,128)S(1)}, u32[]{:S(2)}, u32[]{:S(2)}) %collective-permute-start.1) | collective-permute-done | bytes 131104 | tf_op jit(solution)/shard_map/ppermute | solution.py:102
  79.3 0.0 collective-permute-start.2
  79.3 0.6 collective-permute-done
  79.9 4.4 %collective-permute-done.2 = f32[2,64,256]{2,1,0:T(8,128)S(1)} collective-permute-done((f32[2,64,256]{2,1,0:T(8,128)S(1)}, f32[2,64,256]{2,1,0:T(8,128)S(1)}, u32[]{:S(2)}, u32[]{:S(2)}) %collective-permute-start.2) | collective-permute-done | bytes 131104 | tf_op jit(solution)/shard_map/ppermute | solution.py:102
  84.5 0.9 copy.7
  85.4 0.0 copy-start.3
  85.4 0.0 all-gather.2.cloned.1.call-update
  85.4 3.5 %collective-permute-start.3 = (f32[2,64,256]{2,1,0:T(8,128)S(1)}, f32[2,64,256]{2,1,0:T(8,128)S(1)}, u32[]{:S(2)}, u32[]{:S(2)}) collective-permute-start(f32[2,64,256]{2,1,0:T(8,128)S(1)} %pad_maximum_fusion), channel_id=1, source_target_pairs={{0,0},{1,32},{2,64},{3,96},{4,128},{5,160},{6,192},{7,224},{32,1},... | collective-permute-start | bytes 393224 | tf_op jit(solution)/shard_map/ppermute | solution.py:88
  89.0 2.7 %collective-permute-done.3 = f32[2,64,256]{2,1,0:T(8,128)S(1)} collective-permute-done((f32[2,64,256]{2,1,0:T(8,128)S(1)}, f32[2,64,256]{2,1,0:T(8,128)S(1)}, u32[]{:S(2)}, u32[]{:S(2)}) %collective-permute-start.3) | collective-permute-done | bytes 131104 | tf_op jit(solution)/shard_map/ppermute | solution.py:88
  91.7 1.1 broadcast_in_dim.19
  92.8 12.6 %all-to-all-start.1 = ((f32[8,2,64,256]{3,2,1,0:T(8,128)}), f32[8,2,64,256]{3,2,1,0:T(8,128)S(1)}, u32[]{:S(2)}, u32[]{:S(2)}) async-start(f32[8,2,64,256]{3,2,1,0:T(8,128)} %broadcast_in_dim.19), calls=%async_computation.1 | async-start | bytes 2097152 | tf_op jit(solution)/shard_map/all_to_all | solution.py:90
  105.4 0.0 copy-done.3
  105.5 0.6 stack.40.table_ref
  106.1 14.4 %all-to-all-done.1 = f32[8,2,64,256]{3,2,1,0:T(8,128)S(1)} async-done(((f32[8,2,64,256]{3,2,1,0:T(8,128)}), f32[8,2,64,256]{3,2,1,0:T(8,128)S(1)}, u32[]{:S(2)}, u32[]{:S(2)}) %all-to-all-start.1) | async-done | bytes 1048608 | tf_op jit(solution)/shard_map/all_to_all | solution.py:90
  120.5 0.1 copy.8
  120.6 1.3 copy.9
  121.9 17.9 %all-gather.2.cloned.1.call-done = f32[2,2048,256]{2,1,0:T(8,128)} async-done(((f32[2,256,256]{2,1,0:T(8,128)}), f32[2,2048,256]{2,1,0:T(8,128)}) %all-gather.2.cloned.1.call-update) | async-done | bytes 4194320 | tf_op jit(solution)/shard_map/all_gather | solution.py:109
  139.8 11.2 %shard_map.55 = f32[16,256,256]{2,1,0:T(8,128)} custom-call(s32[5,16]{1,0:T(8,128)} %stack.40.table_ref, f32[16,256,256]{2,1,0:T(8,128)} %bitcast.58, f32[16,256,256]{2,1,0:T(8,128)} %bitcast.60, f32[4,256,256]{2,1,0:T(8,128)} %bitcast.59), custom_call_target="tpu_custom_call" | custom-call | tf_op jit(solution)/shard_map/pallas_call | solution.py:60
  (17 shorter events, 0.2 us)
Async XLA Ops:
  6.5 15.9 %copy-start = (f32[256,256]{1,0:T(8,128)S(1)}, f32[256,256]{1,0:T(8,128)}, u32[]{:S(2)}) copy-start(f32[256,256]{1,0:T(8,128)} %param.11) | copy-start | bytes 786436
  9.6 12.1 %copy-start.2 = (s32[2,8]{1,0:T(2,128)S(1)}, s32[2,8]{1,0:T(2,128)}, u32[]{:S(2)}) copy-start(s32[2,8]{1,0:T(2,128)} %param.8) | copy-start | bytes 196
  9.6 12.8 %copy-start.1 = (f32[2,256,256]{2,1,0:T(8,128)S(1)}, f32[2,256,256]{2,1,0:T(8,128)}, u32[]{:S(2)}) copy-start(f32[2,256,256]{2,1,0:T(8,128)} %param.10) | copy-start | bytes 1572868
  9.6 60.5 %all-to-all-start = ((f32[32,64,256]{2,1,0:T(8,128)}), f32[32,64,256]{2,1,0:T(8,128)S(1)}, u32[]{:S(2)}, u32[]{:S(2)}) async-start(f32[32,64,256]{2,1,0:T(8,128)} %bitcast.6), calls=%async_computation | async-start | bytes 4194304 | tf_op jit(solution)/shard_map/all_to_all | solution.py:75
  21.6 118.2 %all-gather.2.cloned.1.call-start = ((), (), s32[]{:S(2)}) async-start(), calls=%async_computation.2 | async-start | bytes 4718592 | tf_op jit(solution)/shard_map/all_gather | solution.py:109
  72.5 6.8 %collective-permute-start.1 = (f32[2,64,256]{2,1,0:T(8,128)S(1)}, f32[2,64,256]{2,1,0:T(8,128)S(1)}, u32[]{:S(2)}, u32[]{:S(2)}) collective-permute-start(f32[2,64,256]{2,1,0:T(8,128)S(1)} %pad_maximum_fusion), channel_id=1, source_target_pairs={{0,1},{1,2},{2,3},{3,0},{4,5},{5,6},{6,7},{7,4},{8,9},{9,10},{10,1... | collective-permute-start | bytes 393224 | tf_op jit(solution)/shard_map/ppermute | solution.py:102
  74.6 5.3 %collective-permute-start = (f32[2,64,256]{2,1,0:T(8,128)S(1)}, f32[2,64,256]{2,1,0:T(8,128)S(1)}, u32[]{:S(2)}, u32[]{:S(2)}) collective-permute-start(f32[2,64,256]{2,1,0:T(8,128)S(1)} %pad_maximum_fusion), channel_id=1, source_target_pairs={{0,3},{1,0},{2,1},{3,2},{4,7},{5,4},{6,5},{7,6},{8,11},{9,8},{10,9... | collective-permute-start | bytes 393224 | tf_op jit(solution)/shard_map/ppermute | solution.py:105
  79.3 5.0 %collective-permute-start.2 = (f32[2,64,256]{2,1,0:T(8,128)S(1)}, f32[2,64,256]{2,1,0:T(8,128)S(1)}, u32[]{:S(2)}, u32[]{:S(2)}) collective-permute-start(f32[2,64,256]{2,1,0:T(8,128)S(1)} %collective-permute-done.1), channel_id=1, source_target_pairs={{0,1},{1,2},{2,3},{3,0},{4,5},{5,6},{6,7},{7,4},{8,9},{9,10},{10,1... | collective-permute-start | bytes 393224 | tf_op jit(solution)/shard_map/ppermute | solution.py:102
  85.4 20.0 %copy-start.3 = (s32[2,16,1]{1,2,0:T(1,128)S(1)}, s32[2,16,1]{1,2,0:T(1,128)}, u32[]{:S(2)}) copy-start(s32[2,16,1]{1,2,0:T(1,128)} %param.9) | copy-start | bytes 388
  85.4 6.3 %collective-permute-start.3 = (f32[2,64,256]{2,1,0:T(8,128)S(1)}, f32[2,64,256]{2,1,0:T(8,128)S(1)}, u32[]{:S(2)}, u32[]{:S(2)}) collective-permute-start(f32[2,64,256]{2,1,0:T(8,128)S(1)} %pad_maximum_fusion), channel_id=1, source_target_pairs={{0,0},{1,32},{2,64},{3,96},{4,128},{5,160},{6,192},{7,224},{32,1},... | collective-permute-start | bytes 393224 | tf_op jit(solution)/shard_map/ppermute | solution.py:88
  92.8 27.7 %all-to-all-start.1 = ((f32[8,2,64,256]{3,2,1,0:T(8,128)}), f32[8,2,64,256]{3,2,1,0:T(8,128)S(1)}, u32[]{:S(2)}, u32[]{:S(2)}) async-start(f32[8,2,64,256]{3,2,1,0:T(8,128)} %broadcast_in_dim.19), calls=%async_computation.1 | async-start | bytes 2097152 | tf_op jit(solution)/shard_map/all_to_all | solution.py:90
Sparse Core Ops, SparseCore 0:
  85.5 54.2 all-gather.1

commit v16 on v15

--- a/solution.py
+++ b/solution.py
@@ -23,22 +23,39 @@
     return jnp.einsum("ab,cb->ac", panel_rows_block, inverse, precision=HIGHEST_PRECISION)
 
 
-def tail_kernel(table_ref, stored_ref, rows_ref, cols_ref, out_ref):
+def split_halves(source, high, low):
+    for index in range(source.shape[0]):
+        value = source[index]
+        top = value.astype(jnp.bfloat16)
+        high[index] = top
+        low[index] = (value - top.astype(jnp.float32)).astype(jnp.bfloat16)
+
+
+def three_pass(high_rows, low_rows, high_cols, low_cols, left, right):
+    def dot(x, y):
+        return lax.dot_general(x, y, PLAIN_PRODUCT, preferred_element_type=jnp.float32)
+
+    top = high_rows[left]
+    return dot(top, high_cols[right]) + dot(top, low_cols[right]) + dot(low_rows[left], high_cols[right])
+
+
+def tail_kernel(table_ref, stored_ref, rows_ref, cols_ref, out_ref, *halves):
+    high_rows, low_rows, high_cols, low_cols = halves
     head = rows_ref.shape[0] // 2
     classes = cols_ref.shape[0] // 2
     step = pl.program_id(0)
+
+    @pl.when(step == 0)
+    def _():
+        split_halves(rows_ref, high_rows, low_rows)
+        split_halves(cols_ref, high_cols, low_cols)
+
     for j in range(SLOTS_PER_STEP):
         slot = step * SLOTS_PER_STEP + j
         left = table_ref[0, slot]
         right = table_ref[1, slot]
-        schur = lax.dot_general(
-            rows_ref[left], cols_ref[right], PLAIN_PRODUCT, precision=PRODUCT_PRECISION,
-            preferred_element_type=jnp.float32,
-        )
-        schur += lax.dot_general(
-            rows_ref[head + left], cols_ref[classes + right], PLAIN_PRODUCT,
-            precision=PRODUCT_PRECISION, preferred_element_type=jnp.float32,
-        )
+        schur = three_pass(*halves, left, right)
+        schur += three_pass(*halves, head + left, classes + right)
         kept = stored_ref[j] - jnp.where(table_ref[2, slot] > 0, schur, 0.0)
         panel = rows_ref[table_ref[4, 0] * head + jnp.minimum(slot, head - 1)]
         out_ref[j] = jnp.where(table_ref[3, slot] > 0, panel, kept)
@@ -56,6 +73,12 @@
             pl.BlockSpec(cols.shape, lambda s, t: (0, 0, 0)),
         ],
         out_specs=pl.BlockSpec(pair, lambda s, t: (s, 0, 0)),
+        scratch_shapes=[
+            pltpu.VMEM(rows.shape, jnp.bfloat16),
+            pltpu.VMEM(rows.shape, jnp.bfloat16),
+            pltpu.VMEM(cols.shape, jnp.bfloat16),
+            pltpu.VMEM(cols.shape, jnp.bfloat16),
+        ],
     )
     return pl.pallas_call(
         tail_kernel, grid_spec=spec, out_shape=jax.ShapeDtypeStruct(stored.shape, stored.dtype)

time: 158 us -> 159 us (level)
  no operation moved by 1% of the time
where the time goes in v16:
time: 159 us; the launch traced here: 158 us
  waiting for transfers between devices  89.6 us (56%)
  starting transfers between devices  32.8 us (21%)
  between operations  13.6 us (9%)
  Pallas kernels  11.8 us (7%)
  local copies, waits for them, and re-layouts  7.18 us (5%)
  matrix products  2.76 us (2%)
    all_to_all x1, waiting for transfers between devices, per_device(): received = lax.all_to_all(pieces, COL_AXES, 0, 0, tiled=True)  47.3 us
    all_gather x1, waiting for transfers between devices, per_device(): both_rows = lax.all_gather(both_rows, ('zh', 'zl'), axis=1, tiled=True)  17.9 us
    all_to_all x1, waiting for transfers between devices, per_device(): class_pieces = lax.all_to_all(spread, 'row', 0, 0, tiled=True)  14.4 us
    all_to_all x1, starting transfers between devices, per_device(): class_pieces = lax.all_to_all(spread, 'row', 0, 0, tiled=True)  12.6 us
    all_to_all x1, starting transfers between devices, per_device(): received = lax.all_to_all(pieces, COL_AXES, 0, 0, tiled=True)  12 us
    pallas_call x1, Pallas kernels, finish_slots(): pl.pallas_call(tail_kernel, grid_spec=spec, out_shape=jax.ShapeDtypeStruc...  11.8 us
    ppermute x2, waiting for transfers between devices, per_device(): ahead = lax.ppermute(ahead, 'x', forward)  6.67 us
    ppermute x1, starting transfers between devices, per_device(): swapped = lax.ppermute(both_pieces, ('row',) + CLASS_AXES, swap)  3.55 us
  transfers between devices with their start and end apart: 7, of which 7 were waited for; matrix products, arithmetic and copies ran while one was open for 3% of the time, Pallas kernels for 0%

profile of v16, /device:TPU:1, one launch (start us, length us, event | category | flops | bytes accessed | tf_op | source)
XLA Modules:
  0.0 158.4 jit_solution(3186669591442536235)
XLA Ops:
  6.5 0.0 copy-start
  6.5 3.1 %slice.51 = f32[8,1,256,256]{3,2,1,0:T(8,128)} slice(f32[16,1,256,256]{3,2,1,0:T(8,128)} %param.7), slice={[0:8], [0:1], [0:256], [0:256]} | slice | bytes 4194304 | tf_op jit(solution)/shard_map/slice | solution.py:95
  9.6 0.0 copy-start.2
  9.6 0.0 copy-start.1
  9.6 12.0 %all-to-all-start = ((f32[32,64,256]{2,1,0:T(8,128)}), f32[32,64,256]{2,1,0:T(8,128)S(1)}, u32[]{:S(2)}, u32[]{:S(2)}) async-start(f32[32,64,256]{2,1,0:T(8,128)} %bitcast.6), calls=%async_computation | async-start | bytes 4194304 | tf_op jit(solution)/shard_map/all_to_all | solution.py:98
  21.6 0.0 all-gather.2.cloned.1.call-start
  21.7 0.0 copy-done.2
  21.7 0.7 fusion.12
  22.4 0.0 copy-done
  22.4 0.0 copy-done.1
  22.4 0.4 fusion.2
  22.8 47.3 %all-to-all-done = f32[32,64,256]{2,1,0:T(8,128)S(1)} async-done(((f32[32,64,256]{2,1,0:T(8,128)}), f32[32,64,256]{2,1,0:T(8,128)S(1)}, u32[]{:S(2)}, u32[]{:S(2)}) %all-to-all-start) | async-done | bytes 2097184 | tf_op jit(solution)/shard_map/all_to_all | solution.py:98
  70.1 0.9 convolution_select_fusion.1
  71.0 0.4 convolution_subtract_fusion
  71.4 1.1 fusion
  72.5 2.1 %collective-permute-start.1 = (f32[2,64,256]{2,1,0:T(8,128)S(1)}, f32[2,64,256]{2,1,0:T(8,128)S(1)}, u32[]{:S(2)}, u32[]{:S(2)}) collective-permute-start(f32[2,64,256]{2,1,0:T(8,128)S(1)} %pad_maximum_fusion), channel_id=1, source_target_pairs={{0,1},{1,2},{2,3},{3,0},{4,5},{5,6},{6,7},{7,4},{8,9},{9,10},{10,1... | collective-permute-start | bytes 393224 | tf_op jit(solution)/shard_map/ppermute | solution.py:125
  74.6 2.5 %collective-permute-start = (f32[2,64,256]{2,1,0:T(8,128)S(1)}, f32[2,64,256]{2,1,0:T(8,128)S(1)}, u32[]{:S(2)}, u32[]{:S(2)}) collective-permute-start(f32[2,64,256]{2,1,0:T(8,128)S(1)} %pad_maximum_fusion), channel_id=1, source_target_pairs={{0,3},{1,0},{2,1},{3,2},{4,7},{5,4},{6,5},{7,6},{8,11},{9,8},{10,9... | collective-permute-start | bytes 393224 | tf_op jit(solution)/shard_map/ppermute | solution.py:128
  77.1 2.3 %collective-permute-done.1 = f32[2,64,256]{2,1,0:T(8,128)S(1)} collective-permute-done((f32[2,64,256]{2,1,0:T(8,128)S(1)}, f32[2,64,256]{2,1,0:T(8,128)S(1)}, u32[]{:S(2)}, u32[]{:S(2)}) %collective-permute-start.1) | collective-permute-done | bytes 131104 | tf_op jit(solution)/shard_map/ppermute | solution.py:125
  79.3 0.0 collective-permute-start.2
  79.3 0.6 collective-permute-done
  79.9 4.4 %collective-permute-done.2 = f32[2,64,256]{2,1,0:T(8,128)S(1)} collective-permute-done((f32[2,64,256]{2,1,0:T(8,128)S(1)}, f32[2,64,256]{2,1,0:T(8,128)S(1)}, u32[]{:S(2)}, u32[]{:S(2)}) %collective-permute-start.2) | collective-permute-done | bytes 131104 | tf_op jit(solution)/shard_map/ppermute | solution.py:125
  84.5 0.9 copy.7
  85.4 0.0 copy-start.3
  85.4 0.0 all-gather.2.cloned.1.call-update
  85.4 3.5 %collective-permute-start.3 = (f32[2,64,256]{2,1,0:T(8,128)S(1)}, f32[2,64,256]{2,1,0:T(8,128)S(1)}, u32[]{:S(2)}, u32[]{:S(2)}) collective-permute-start(f32[2,64,256]{2,1,0:T(8,128)S(1)} %pad_maximum_fusion), channel_id=1, source_target_pairs={{0,0},{1,32},{2,64},{3,96},{4,128},{5,160},{6,192},{7,224},{32,1},... | collective-permute-start | bytes 393224 | tf_op jit(solution)/shard_map/ppermute | solution.py:111
  89.0 2.7 %collective-permute-done.3 = f32[2,64,256]{2,1,0:T(8,128)S(1)} collective-permute-done((f32[2,64,256]{2,1,0:T(8,128)S(1)}, f32[2,64,256]{2,1,0:T(8,128)S(1)}, u32[]{:S(2)}, u32[]{:S(2)}) %collective-permute-start.3) | collective-permute-done | bytes 131104 | tf_op jit(solution)/shard_map/ppermute | solution.py:111
  91.7 1.1 broadcast_in_dim.19
  92.8 12.6 %all-to-all-start.1 = ((f32[8,2,64,256]{3,2,1,0:T(8,128)}), f32[8,2,64,256]{3,2,1,0:T(8,128)S(1)}, u32[]{:S(2)}, u32[]{:S(2)}) async-start(f32[8,2,64,256]{3,2,1,0:T(8,128)} %broadcast_in_dim.19), calls=%async_computation.1 | async-start | bytes 2097152 | tf_op jit(solution)/shard_map/all_to_all | solution.py:113
  105.4 0.0 copy-done.3
  105.5 0.6 stack.40.table_ref
  106.1 14.4 %all-to-all-done.1 = f32[8,2,64,256]{3,2,1,0:T(8,128)S(1)} async-done(((f32[8,2,64,256]{3,2,1,0:T(8,128)}), f32[8,2,64,256]{3,2,1,0:T(8,128)S(1)}, u32[]{:S(2)}, u32[]{:S(2)}) %all-to-all-start.1) | async-done | bytes 1048608 | tf_op jit(solution)/shard_map/all_to_all | solution.py:113
  120.5 0.1 copy.8
  120.6 1.3 copy.9
  121.9 17.9 %all-gather.2.cloned.1.call-done = f32[2,2048,256]{2,1,0:T(8,128)} async-done(((f32[2,256,256]{2,1,0:T(8,128)}), f32[2,2048,256]{2,1,0:T(8,128)}) %all-gather.2.cloned.1.call-update) | async-done | bytes 4194320 | tf_op jit(solution)/shard_map/all_gather | solution.py:132
  139.8 11.8 %shard_map.55 = f32[16,256,256]{2,1,0:T(8,128)} custom-call(s32[5,16]{1,0:T(8,128)} %stack.40.table_ref, f32[16,256,256]{2,1,0:T(8,128)} %bitcast.58, f32[16,256,256]{2,1,0:T(8,128)} %bitcast.60, f32[4,256,256]{2,1,0:T(8,128)} %bitcast.59), custom_call_target="tpu_custom_call" | custom-call | tf_op jit(solution)/shard_map/pallas_call | solution.py:83
  (17 shorter events, 0.2 us)
Async XLA Ops:
  6.5 15.9 %copy-start = (f32[256,256]{1,0:T(8,128)S(1)}, f32[256,256]{1,0:T(8,128)}, u32[]{:S(2)}) copy-start(f32[256,256]{1,0:T(8,128)} %param.11) | copy-start | bytes 786436
  9.6 12.1 %copy-start.2 = (s32[2,8]{1,0:T(2,128)S(1)}, s32[2,8]{1,0:T(2,128)}, u32[]{:S(2)}) copy-start(s32[2,8]{1,0:T(2,128)} %param.8) | copy-start | bytes 196
  9.6 12.8 %copy-start.1 = (f32[2,256,256]{2,1,0:T(8,128)S(1)}, f32[2,256,256]{2,1,0:T(8,128)}, u32[]{:S(2)}) copy-start(f32[2,256,256]{2,1,0:T(8,128)} %param.10) | copy-start | bytes 1572868
  9.6 60.5 %all-to-all-start = ((f32[32,64,256]{2,1,0:T(8,128)}), f32[32,64,256]{2,1,0:T(8,128)S(1)}, u32[]{:S(2)}, u32[]{:S(2)}) async-start(f32[32,64,256]{2,1,0:T(8,128)} %bitcast.6), calls=%async_computation | async-start | bytes 4194304 | tf_op jit(solution)/shard_map/all_to_all | solution.py:98
  21.6 118.2 %all-gather.2.cloned.1.call-start = ((), (), s32[]{:S(2)}) async-start(), calls=%async_computation.2 | async-start | bytes 4718592 | tf_op jit(solution)/shard_map/all_gather | solution.py:132
  72.5 6.8 %collective-permute-start.1 = (f32[2,64,256]{2,1,0:T(8,128)S(1)}, f32[2,64,256]{2,1,0:T(8,128)S(1)}, u32[]{:S(2)}, u32[]{:S(2)}) collective-permute-start(f32[2,64,256]{2,1,0:T(8,128)S(1)} %pad_maximum_fusion), channel_id=1, source_target_pairs={{0,1},{1,2},{2,3},{3,0},{4,5},{5,6},{6,7},{7,4},{8,9},{9,10},{10,1... | collective-permute-start | bytes 393224 | tf_op jit(solution)/shard_map/ppermute | solution.py:125
  74.6 5.3 %collective-permute-start = (f32[2,64,256]{2,1,0:T(8,128)S(1)}, f32[2,64,256]{2,1,0:T(8,128)S(1)}, u32[]{:S(2)}, u32[]{:S(2)}) collective-permute-start(f32[2,64,256]{2,1,0:T(8,128)S(1)} %pad_maximum_fusion), channel_id=1, source_target_pairs={{0,3},{1,0},{2,1},{3,2},{4,7},{5,4},{6,5},{7,6},{8,11},{9,8},{10,9... | collective-permute-start | bytes 393224 | tf_op jit(solution)/shard_map/ppermute | solution.py:128
  79.3 5.0 %collective-permute-start.2 = (f32[2,64,256]{2,1,0:T(8,128)S(1)}, f32[2,64,256]{2,1,0:T(8,128)S(1)}, u32[]{:S(2)}, u32[]{:S(2)}) collective-permute-start(f32[2,64,256]{2,1,0:T(8,128)S(1)} %collective-permute-done.1), channel_id=1, source_target_pairs={{0,1},{1,2},{2,3},{3,0},{4,5},{5,6},{6,7},{7,4},{8,9},{9,10},{10,1... | collective-permute-start | bytes 393224 | tf_op jit(solution)/shard_map/ppermute | solution.py:125
  85.4 20.0 %copy-start.3 = (s32[2,16,1]{1,2,0:T(1,128)S(1)}, s32[2,16,1]{1,2,0:T(1,128)}, u32[]{:S(2)}) copy-start(s32[2,16,1]{1,2,0:T(1,128)} %param.9) | copy-start | bytes 388
  85.4 6.3 %collective-permute-start.3 = (f32[2,64,256]{2,1,0:T(8,128)S(1)}, f32[2,64,256]{2,1,0:T(8,128)S(1)}, u32[]{:S(2)}, u32[]{:S(2)}) collective-permute-start(f32[2,64,256]{2,1,0:T(8,128)S(1)} %pad_maximum_fusion), channel_id=1, source_target_pairs={{0,0},{1,32},{2,64},{3,96},{4,128},{5,160},{6,192},{7,224},{32,1},... | collective-permute-start | bytes 393224 | tf_op jit(solution)/shard_map/ppermute | solution.py:111
  92.8 27.7 %all-to-all-start.1 = ((f32[8,2,64,256]{3,2,1,0:T(8,128)}), f32[8,2,64,256]{3,2,1,0:T(8,128)S(1)}, u32[]{:S(2)}, u32[]{:S(2)}) async-start(f32[8,2,64,256]{3,2,1,0:T(8,128)} %broadcast_in_dim.19), calls=%async_computation.1 | async-start | bytes 2097152 | tf_op jit(solution)/shard_map/all_to_all | solution.py:113
Sparse Core Ops, SparseCore 0:
  85.5 54.2 all-gather.1

commit v17 on v15

--- a/solution.py
+++ b/solution.py
@@ -93,17 +93,10 @@
     both_cols = class_pieces.transpose(2, 0, 1, 3, 4).reshape(2, PER_CLASS, block, block)
     x_ring = lax.axis_size("x")
     x_place = lax.axis_index("x")
-    forward = [(i, (i + 1) % x_ring) for i in range(x_ring)]
-    backward = [(i, (i - 1) % x_ring) for i in range(x_ring)]
     by_offset = [both_pieces] * x_ring
-    ahead = both_pieces
-    behind = both_pieces
-    for step in range(1, x_ring // 2 + 1):
-        ahead = lax.ppermute(ahead, "x", forward)
-        by_offset[x_ring - step] = ahead
-        if step < x_ring - step:
-            behind = lax.ppermute(behind, "x", backward)
-            by_offset[step] = behind
+    for shift in range(1, x_ring):
+        pairs = [(i, (i + shift) % x_ring) for i in range(x_ring)]
+        by_offset[x_ring - shift] = lax.ppermute(both_pieces, "x", pairs)
     both_rows = jnp.roll(jnp.stack(by_offset, axis=1), x_place, axis=1)
     both_rows = both_rows.reshape(2, x_ring * chunk, block)
     both_rows = lax.all_gather(both_rows, ("zh", "zl"), axis=1, tiled=True)

time: 158 us -> 156 us (0.987)
  waiting for transfers between devices: 89.6 us -> 83.8 us
  starting transfers between devices: 32.8 us -> 35.8 us
    all_gather x1, waiting for transfers between devices: 17.9 us -> 13.3 us  [per_device(): both_rows = lax.all_gather(both_rows, ('zh', 'zl'), axis=1, tiled=True)]
    all_to_all x1, starting transfers between devices: 12.6 us -> 14.6 us  [per_device(): class_pieces = lax.all_to_all(spread, 'row', 0, 0, tiled=True)]
    ppermute x3, waiting for transfers between devices: 7.27 us -> 5.45 us  [per_device(): by_offset[x_ring - shift] = lax.ppermute(both_pieces, 'x', pairs)]
    ppermute x3, starting transfers between devices: 4.58 us -> 6.25 us  [per_device(): by_offset[x_ring - shift] = lax.ppermute(both_pieces, 'x', pairs)]
  transfers between devices with their start and end apart: 7 -> 7, of which waited for: 7 -> 6; matrix products, arithmetic and copies ran while one was open for 3% -> 3% of each run, Pallas kernels for 0% -> 0%
where the time goes in v17:
time: 156 us; the launch traced here: 155 us
  waiting for transfers between devices  83.8 us (54%)
  starting transfers between devices  35.8 us (23%)
  between operations  13.6 us (9%)
  Pallas kernels  11.2 us (7%)
  local copies, waits for them, and re-layouts  7.18 us (5%)
  matrix products  2.76 us (2%)
    all_to_all x1, waiting for transfers between devices, per_device(): received = lax.all_to_all(pieces, COL_AXES, 0, 0, tiled=True)  47.3 us
    all_to_all x1, starting transfers between devices, per_device(): class_pieces = lax.all_to_all(spread, 'row', 0, 0, tiled=True)  14.6 us
    all_to_all x1, waiting for transfers between devices, per_device(): class_pieces = lax.all_to_all(spread, 'row', 0, 0, tiled=True)  14.4 us
    all_gather x1, waiting for transfers between devices, per_device(): both_rows = lax.all_gather(both_rows, ('zh', 'zl'), axis=1, tiled=True)  13.3 us
    all_to_all x1, starting transfers between devices, per_device(): received = lax.all_to_all(pieces, COL_AXES, 0, 0, tiled=True)  12 us
    pallas_call x1, Pallas kernels, finish_slots(): pl.pallas_call(tail_kernel, grid_spec=spec, out_shape=jax.ShapeDtypeStruc...  11.2 us
    ppermute x3, starting transfers between devices, per_device(): by_offset[x_ring - shift] = lax.ppermute(both_pieces, 'x', pairs)  6.25 us
    ppermute x3, waiting for transfers between devices, per_device(): by_offset[x_ring - shift] = lax.ppermute(both_pieces, 'x', pairs)  5.45 us
  transfers between devices with their start and end apart: 7, of which 6 were waited for; matrix products, arithmetic and copies ran while one was open for 3% of the time, Pallas kernels for 0%

profile of v17, /device:TPU:1, one launch (start us, length us, event | category | flops | bytes accessed | tf_op | source)
XLA Modules:
  0.0 155.1 jit_solution(10763681169600672399)
XLA Ops:
  6.5 0.0 copy-start
  6.5 3.1 %slice.51 = f32[8,1,256,256]{3,2,1,0:T(8,128)} slice(f32[16,1,256,256]{3,2,1,0:T(8,128)} %param.7), slice={[0:8], [0:1], [0:256], [0:256]} | slice | bytes 4194304 | tf_op jit(solution)/shard_map/slice | solution.py:72
  9.6 0.0 copy-start.2
  9.6 0.0 copy-start.1
  9.6 12.0 %all-to-all-start = ((f32[32,64,256]{2,1,0:T(8,128)}), f32[32,64,256]{2,1,0:T(8,128)S(1)}, u32[]{:S(2)}, u32[]{:S(2)}) async-start(f32[32,64,256]{2,1,0:T(8,128)} %bitcast.6), calls=%async_computation | async-start | bytes 4194304 | tf_op jit(solution)/shard_map/all_to_all | solution.py:75
  21.6 0.0 all-gather.2.cloned.1.call-start
  21.7 0.0 copy-done.2
  21.7 0.7 fusion.12
  22.4 0.0 copy-done
  22.4 0.0 copy-done.1
  22.4 0.4 fusion.2
  22.8 47.3 %all-to-all-done = f32[32,64,256]{2,1,0:T(8,128)S(1)} async-done(((f32[32,64,256]{2,1,0:T(8,128)}), f32[32,64,256]{2,1,0:T(8,128)S(1)}, u32[]{:S(2)}, u32[]{:S(2)}) %all-to-all-start) | async-done | bytes 2097184 | tf_op jit(solution)/shard_map/all_to_all | solution.py:75
  70.1 0.9 convolution_select_fusion.1
  71.0 0.4 convolution_subtract_fusion
  71.4 1.1 fusion
  72.5 4.5 %collective-permute-start = (f32[2,64,256]{2,1,0:T(8,128)S(1)}, f32[2,64,256]{2,1,0:T(8,128)S(1)}, u32[]{:S(2)}, u32[]{:S(2)}) collective-permute-start(f32[2,64,256]{2,1,0:T(8,128)S(1)} %pad_maximum_fusion), channel_id=1, source_target_pairs={{0,3},{1,0},{2,1},{3,2},{4,7},{5,4},{6,5},{7,6},{8,11},{9,8},{10,9... | collective-permute-start | bytes 393224 | tf_op jit(solution)/shard_map/ppermute | solution.py:99
  77.0 0.0 collective-permute-start.2
  77.0 1.8 %collective-permute-start.1 = (f32[2,64,256]{2,1,0:T(8,128)S(1)}, f32[2,64,256]{2,1,0:T(8,128)S(1)}, u32[]{:S(2)}, u32[]{:S(2)}) collective-permute-start(f32[2,64,256]{2,1,0:T(8,128)S(1)} %pad_maximum_fusion), channel_id=1, source_target_pairs={{0,2},{1,3},{2,0},{3,1},{4,6},{5,7},{6,4},{7,5},{8,10},{9,11},{10,... | collective-permute-start | bytes 393224 | tf_op jit(solution)/shard_map/ppermute | solution.py:99
  78.7 0.5 collective-permute-done
  79.2 5.0 %collective-permute-done.1 = f32[2,64,256]{2,1,0:T(8,128)S(1)} collective-permute-done((f32[2,64,256]{2,1,0:T(8,128)S(1)}, f32[2,64,256]{2,1,0:T(8,128)S(1)}, u32[]{:S(2)}, u32[]{:S(2)}) %collective-permute-start.1) | collective-permute-done | bytes 131104 | tf_op jit(solution)/shard_map/ppermute | solution.py:99
  84.2 0.0 collective-permute-done.2
  84.4 0.9 copy.7
  85.2 0.0 copy-start.3
  85.3 0.0 all-gather.2.cloned.1.call-update
  85.3 3.0 %collective-permute-start.3 = (f32[2,64,256]{2,1,0:T(8,128)S(1)}, f32[2,64,256]{2,1,0:T(8,128)S(1)}, u32[]{:S(2)}, u32[]{:S(2)}) collective-permute-start(f32[2,64,256]{2,1,0:T(8,128)S(1)} %pad_maximum_fusion), channel_id=1, source_target_pairs={{0,0},{1,32},{2,64},{3,96},{4,128},{5,160},{6,192},{7,224},{32,1},... | collective-permute-start | bytes 393224 | tf_op jit(solution)/shard_map/ppermute | solution.py:88
  88.3 3.3 %collective-permute-done.3 = f32[2,64,256]{2,1,0:T(8,128)S(1)} collective-permute-done((f32[2,64,256]{2,1,0:T(8,128)S(1)}, f32[2,64,256]{2,1,0:T(8,128)S(1)}, u32[]{:S(2)}, u32[]{:S(2)}) %collective-permute-start.3) | collective-permute-done | bytes 131104 | tf_op jit(solution)/shard_map/ppermute | solution.py:88
  91.6 1.1 broadcast_in_dim.19
  92.6 14.6 %all-to-all-start.1 = ((f32[8,2,64,256]{3,2,1,0:T(8,128)}), f32[8,2,64,256]{3,2,1,0:T(8,128)S(1)}, u32[]{:S(2)}, u32[]{:S(2)}) async-start(f32[8,2,64,256]{3,2,1,0:T(8,128)} %broadcast_in_dim.19), calls=%async_computation.1 | async-start | bytes 2097152 | tf_op jit(solution)/shard_map/all_to_all | solution.py:90
  107.2 0.0 copy-done.3
  107.3 0.6 stack.40.table_ref
  107.9 14.4 %all-to-all-done.1 = f32[8,2,64,256]{3,2,1,0:T(8,128)S(1)} async-done(((f32[8,2,64,256]{3,2,1,0:T(8,128)}), f32[8,2,64,256]{3,2,1,0:T(8,128)S(1)}, u32[]{:S(2)}, u32[]{:S(2)}) %all-to-all-start.1) | async-done | bytes 1048608 | tf_op jit(solution)/shard_map/all_to_all | solution.py:90
  122.3 0.1 copy.8
  122.4 1.3 copy.9
  123.7 13.3 %all-gather.2.cloned.1.call-done = f32[2,2048,256]{2,1,0:T(8,128)} async-done(((f32[2,256,256]{2,1,0:T(8,128)}), f32[2,2048,256]{2,1,0:T(8,128)}) %all-gather.2.cloned.1.call-update) | async-done | bytes 4194320 | tf_op jit(solution)/shard_map/all_gather | solution.py:102
  137.0 11.2 %shard_map.55 = f32[16,256,256]{2,1,0:T(8,128)} custom-call(s32[5,16]{1,0:T(8,128)} %stack.40.table_ref, f32[16,256,256]{2,1,0:T(8,128)} %bitcast.58, f32[16,256,256]{2,1,0:T(8,128)} %bitcast.60, f32[4,256,256]{2,1,0:T(8,128)} %bitcast.59), custom_call_target="tpu_custom_call" | custom-call | tf_op jit(solution)/shard_map/pallas_call | solution.py:60
  (17 shorter events, 0.2 us)
Async XLA Ops:
  6.5 15.9 %copy-start = (f32[256,256]{1,0:T(8,128)S(1)}, f32[256,256]{1,0:T(8,128)}, u32[]{:S(2)}) copy-start(f32[256,256]{1,0:T(8,128)} %param.11) | copy-start | bytes 786436
  9.6 12.1 %copy-start.2 = (s32[2,8]{1,0:T(2,128)S(1)}, s32[2,8]{1,0:T(2,128)}, u32[]{:S(2)}) copy-start(s32[2,8]{1,0:T(2,128)} %param.8) | copy-start | bytes 196
  9.6 12.8 %copy-start.1 = (f32[2,256,256]{2,1,0:T(8,128)S(1)}, f32[2,256,256]{2,1,0:T(8,128)}, u32[]{:S(2)}) copy-start(f32[2,256,256]{2,1,0:T(8,128)} %param.10) | copy-start | bytes 1572868
  9.6 60.5 %all-to-all-start = ((f32[32,64,256]{2,1,0:T(8,128)}), f32[32,64,256]{2,1,0:T(8,128)S(1)}, u32[]{:S(2)}, u32[]{:S(2)}) async-start(f32[32,64,256]{2,1,0:T(8,128)} %bitcast.6), calls=%async_computation | async-start | bytes 4194304 | tf_op jit(solution)/shard_map/all_to_all | solution.py:75
  21.6 115.4 %all-gather.2.cloned.1.call-start = ((), (), s32[]{:S(2)}) async-start(), calls=%async_computation.2 | async-start | bytes 4718592 | tf_op jit(solution)/shard_map/all_gather | solution.py:102
  72.5 6.7 %collective-permute-start = (f32[2,64,256]{2,1,0:T(8,128)S(1)}, f32[2,64,256]{2,1,0:T(8,128)S(1)}, u32[]{:S(2)}, u32[]{:S(2)}) collective-permute-start(f32[2,64,256]{2,1,0:T(8,128)S(1)} %pad_maximum_fusion), channel_id=1, source_target_pairs={{0,3},{1,0},{2,1},{3,2},{4,7},{5,4},{6,5},{7,6},{8,11},{9,8},{10,9... | collective-permute-start | bytes 393224 | tf_op jit(solution)/shard_map/ppermute | solution.py:99
  77.0 7.3 %collective-permute-start.2 = (f32[2,64,256]{2,1,0:T(8,128)S(1)}, f32[2,64,256]{2,1,0:T(8,128)S(1)}, u32[]{:S(2)}, u32[]{:S(2)}) collective-permute-start(f32[2,64,256]{2,1,0:T(8,128)S(1)} %pad_maximum_fusion), channel_id=1, source_target_pairs={{0,1},{1,2},{2,3},{3,0},{4,5},{5,6},{6,7},{7,4},{8,9},{9,10},{10,1... | collective-permute-start | bytes 393224 | tf_op jit(solution)/shard_map/ppermute | solution.py:99
  77.0 7.2 %collective-permute-start.1 = (f32[2,64,256]{2,1,0:T(8,128)S(1)}, f32[2,64,256]{2,1,0:T(8,128)S(1)}, u32[]{:S(2)}, u32[]{:S(2)}) collective-permute-start(f32[2,64,256]{2,1,0:T(8,128)S(1)} %pad_maximum_fusion), channel_id=1, source_target_pairs={{0,2},{1,3},{2,0},{3,1},{4,6},{5,7},{6,4},{7,5},{8,10},{9,11},{10,... | collective-permute-start | bytes 393224 | tf_op jit(solution)/shard_map/ppermute | solution.py:99
  85.2 22.0 %copy-start.3 = (s32[2,16,1]{1,2,0:T(1,128)S(1)}, s32[2,16,1]{1,2,0:T(1,128)}, u32[]{:S(2)}) copy-start(s32[2,16,1]{1,2,0:T(1,128)} %param.9) | copy-start | bytes 388
  85.3 6.3 %collective-permute-start.3 = (f32[2,64,256]{2,1,0:T(8,128)S(1)}, f32[2,64,256]{2,1,0:T(8,128)S(1)}, u32[]{:S(2)}, u32[]{:S(2)}) collective-permute-start(f32[2,64,256]{2,1,0:T(8,128)S(1)} %pad_maximum_fusion), channel_id=1, source_target_pairs={{0,0},{1,32},{2,64},{3,96},{4,128},{5,160},{6,192},{7,224},{32,1},... | collective-permute-start | bytes 393224 | tf_op jit(solution)/shard_map/ppermute | solution.py:88
  92.6 29.7 %all-to-all-start.1 = ((f32[8,2,64,256]{3,2,1,0:T(8,128)}), f32[8,2,64,256]{3,2,1,0:T(8,128)S(1)}, u32[]{:S(2)}, u32[]{:S(2)}) async-start(f32[8,2,64,256]{3,2,1,0:T(8,128)} %broadcast_in_dim.19), calls=%async_computation.1 | async-start | bytes 2097152 | tf_op jit(solution)/shard_map/all_to_all | solution.py:90
Sparse Core Ops, SparseCore 0:
  85.4 51.5 all-gather.1

commit v18 on v17

--- a/solution.py
+++ b/solution.py
@@ -20,7 +20,7 @@
 
 
 def apply_inverse(panel_rows_block, inverse):
-    return jnp.einsum("ab,cb->ac", panel_rows_block, inverse, precision=HIGHEST_PRECISION)
+    return jnp.einsum("ab,cb->ac", panel_rows_block, inverse, precision=PRODUCT_PRECISION)
 
 
 def tail_kernel(table_ref, stored_ref, rows_ref, cols_ref, out_ref):

time: 156 us -> 155 us (level)
  no operation moved by 1% of the time
where the time goes in v18:
time: 155 us
  waiting for transfers between devices  83.8 us (54%)
  starting transfers between devices  35.8 us (23%)
  between operations  13.6 us (9%)
  Pallas kernels  11.2 us (7%)
  local copies, waits for them, and re-layouts  7.18 us (5%)
  matrix products  2.47 us (2%)
    all_to_all x1, waiting for transfers between devices, per_device(): received = lax.all_to_all(pieces, COL_AXES, 0, 0, tiled=True)  47.3 us
    all_to_all x1, starting transfers between devices, per_device(): class_pieces = lax.all_to_all(spread, 'row', 0, 0, tiled=True)  14.5 us
    all_to_all x1, waiting for transfers between devices, per_device(): class_pieces = lax.all_to_all(spread, 'row', 0, 0, tiled=True)  14.4 us
    all_gather x1, waiting for transfers between devices, per_device(): both_rows = lax.all_gather(both_rows, ('zh', 'zl'), axis=1, tiled=True)  13.3 us
    all_to_all x1, starting transfers between devices, per_device(): received = lax.all_to_all(pieces, COL_AXES, 0, 0, tiled=True)  12 us
    pallas_call x1, Pallas kernels, finish_slots(): pl.pallas_call(tail_kernel, grid_spec=spec, out_shape=jax.ShapeDtypeStruc...  11.2 us
    ppermute x3, starting transfers between devices, per_device(): by_offset[x_ring - shift] = lax.ppermute(both_pieces, 'x', pairs)  6.25 us
    ppermute x3, waiting for transfers between devices, per_device(): by_offset[x_ring - shift] = lax.ppermute(both_pieces, 'x', pairs)  5.45 us
  transfers between devices with their start and end apart: 7, of which 6 were waited for; matrix products, arithmetic and copies ran while one was open for 3% of the time, Pallas kernels for 0%

profile of v18, /device:TPU:1, one launch (start us, length us, event | category | flops | bytes accessed | tf_op | source)
XLA Modules:
  0.0 154.8 jit_solution(6323953452161458594)
XLA Ops:
  6.5 0.0 copy-start
  6.5 3.1 %slice.51 = f32[8,1,256,256]{3,2,1,0:T(8,128)} slice(f32[16,1,256,256]{3,2,1,0:T(8,128)} %param.7), slice={[0:8], [0:1], [0:256], [0:256]} | slice | bytes 4194304 | tf_op jit(solution)/shard_map/slice | solution.py:72
  9.6 0.0 copy-start.2
  9.6 0.0 copy-start.1
  9.6 12.0 %all-to-all-start = ((f32[32,64,256]{2,1,0:T(8,128)}), f32[32,64,256]{2,1,0:T(8,128)S(1)}, u32[]{:S(2)}, u32[]{:S(2)}) async-start(f32[32,64,256]{2,1,0:T(8,128)} %bitcast.6), calls=%async_computation | async-start | bytes 4194304 | tf_op jit(solution)/shard_map/all_to_all | solution.py:75
  21.6 0.0 all-gather.2.cloned.1.call-start
  21.7 0.0 copy-done.2
  21.7 0.7 fusion.12
  22.4 0.0 copy-done
  22.4 0.0 copy-done.1
  22.4 0.4 fusion.2
  22.8 47.3 %all-to-all-done = f32[32,64,256]{2,1,0:T(8,128)S(1)} async-done(((f32[32,64,256]{2,1,0:T(8,128)}), f32[32,64,256]{2,1,0:T(8,128)S(1)}, u32[]{:S(2)}, u32[]{:S(2)}) %all-to-all-start) | async-done | bytes 2097184 | tf_op jit(solution)/shard_map/all_to_all | solution.py:75
  70.1 0.8 convolution_select_fusion.1
  70.9 0.3 convolution_subtract_fusion
  71.2 1.0 fusion
  72.2 4.5 %collective-permute-start = (f32[2,64,256]{2,1,0:T(8,128)S(1)}, f32[2,64,256]{2,1,0:T(8,128)S(1)}, u32[]{:S(2)}, u32[]{:S(2)}) collective-permute-start(f32[2,64,256]{2,1,0:T(8,128)S(1)} %pad_maximum_fusion), channel_id=1, source_target_pairs={{0,3},{1,0},{2,1},{3,2},{4,7},{5,4},{6,5},{7,6},{8,11},{9,8},{10,9... | collective-permute-start | bytes 393224 | tf_op jit(solution)/shard_map/ppermute | solution.py:99
  76.7 0.0 collective-permute-start.2
  76.7 1.8 %collective-permute-start.1 = (f32[2,64,256]{2,1,0:T(8,128)S(1)}, f32[2,64,256]{2,1,0:T(8,128)S(1)}, u32[]{:S(2)}, u32[]{:S(2)}) collective-permute-start(f32[2,64,256]{2,1,0:T(8,128)S(1)} %pad_maximum_fusion), channel_id=1, source_target_pairs={{0,2},{1,3},{2,0},{3,1},{4,6},{5,7},{6,4},{7,5},{8,10},{9,11},{10,... | collective-permute-start | bytes 393224 | tf_op jit(solution)/shard_map/ppermute | solution.py:99
  78.5 0.5 collective-permute-done
  79.0 5.0 %collective-permute-done.1 = f32[2,64,256]{2,1,0:T(8,128)S(1)} collective-permute-done((f32[2,64,256]{2,1,0:T(8,128)S(1)}, f32[2,64,256]{2,1,0:T(8,128)S(1)}, u32[]{:S(2)}, u32[]{:S(2)}) %collective-permute-start.1) | collective-permute-done | bytes 131104 | tf_op jit(solution)/shard_map/ppermute | solution.py:99
  84.0 0.0 collective-permute-done.2
  84.1 0.9 copy.7
  85.0 0.0 copy-start.3
  85.0 0.0 all-gather.2.cloned.1.call-update
  85.0 3.0 %collective-permute-start.3 = (f32[2,64,256]{2,1,0:T(8,128)S(1)}, f32[2,64,256]{2,1,0:T(8,128)S(1)}, u32[]{:S(2)}, u32[]{:S(2)}) collective-permute-start(f32[2,64,256]{2,1,0:T(8,128)S(1)} %pad_maximum_fusion), channel_id=1, source_target_pairs={{0,0},{1,32},{2,64},{3,96},{4,128},{5,160},{6,192},{7,224},{32,1},... | collective-permute-start | bytes 393224 | tf_op jit(solution)/shard_map/ppermute | solution.py:88
  88.0 3.3 %collective-permute-done.3 = f32[2,64,256]{2,1,0:T(8,128)S(1)} collective-permute-done((f32[2,64,256]{2,1,0:T(8,128)S(1)}, f32[2,64,256]{2,1,0:T(8,128)S(1)}, u32[]{:S(2)}, u32[]{:S(2)}) %collective-permute-start.3) | collective-permute-done | bytes 131104 | tf_op jit(solution)/shard_map/ppermute | solution.py:88
  91.3 1.1 broadcast_in_dim.19
  92.4 14.5 %all-to-all-start.1 = ((f32[8,2,64,256]{3,2,1,0:T(8,128)}), f32[8,2,64,256]{3,2,1,0:T(8,128)S(1)}, u32[]{:S(2)}, u32[]{:S(2)}) async-start(f32[8,2,64,256]{3,2,1,0:T(8,128)} %broadcast_in_dim.19), calls=%async_computation.1 | async-start | bytes 2097152 | tf_op jit(solution)/shard_map/all_to_all | solution.py:90
  107.0 0.0 copy-done.3
  107.0 0.6 stack.40.table_ref
  107.6 14.4 %all-to-all-done.1 = f32[8,2,64,256]{3,2,1,0:T(8,128)S(1)} async-done(((f32[8,2,64,256]{3,2,1,0:T(8,128)}), f32[8,2,64,256]{3,2,1,0:T(8,128)S(1)}, u32[]{:S(2)}, u32[]{:S(2)}) %all-to-all-start.1) | async-done | bytes 1048608 | tf_op jit(solution)/shard_map/all_to_all | solution.py:90
  122.0 0.1 copy.8
  122.1 1.3 copy.9
  123.4 13.3 %all-gather.2.cloned.1.call-done = f32[2,2048,256]{2,1,0:T(8,128)} async-done(((f32[2,256,256]{2,1,0:T(8,128)}), f32[2,2048,256]{2,1,0:T(8,128)}) %all-gather.2.cloned.1.call-update) | async-done | bytes 4194320 | tf_op jit(solution)/shard_map/all_gather | solution.py:102
  136.7 11.2 %shard_map.55 = f32[16,256,256]{2,1,0:T(8,128)} custom-call(s32[5,16]{1,0:T(8,128)} %stack.40.table_ref, f32[16,256,256]{2,1,0:T(8,128)} %bitcast.58, f32[16,256,256]{2,1,0:T(8,128)} %bitcast.60, f32[4,256,256]{2,1,0:T(8,128)} %bitcast.59), custom_call_target="tpu_custom_call" | custom-call | tf_op jit(solution)/shard_map/pallas_call | solution.py:60
  (17 shorter events, 0.2 us)
Async XLA Ops:
  6.5 15.9 %copy-start = (f32[256,256]{1,0:T(8,128)S(1)}, f32[256,256]{1,0:T(8,128)}, u32[]{:S(2)}) copy-start(f32[256,256]{1,0:T(8,128)} %param.11) | copy-start | bytes 786436
  9.6 12.1 %copy-start.2 = (s32[2,8]{1,0:T(2,128)S(1)}, s32[2,8]{1,0:T(2,128)}, u32[]{:S(2)}) copy-start(s32[2,8]{1,0:T(2,128)} %param.8) | copy-start | bytes 196
  9.6 12.8 %copy-start.1 = (f32[2,256,256]{2,1,0:T(8,128)S(1)}, f32[2,256,256]{2,1,0:T(8,128)}, u32[]{:S(2)}) copy-start(f32[2,256,256]{2,1,0:T(8,128)} %param.10) | copy-start | bytes 1572868
  9.6 60.5 %all-to-all-start = ((f32[32,64,256]{2,1,0:T(8,128)}), f32[32,64,256]{2,1,0:T(8,128)S(1)}, u32[]{:S(2)}, u32[]{:S(2)}) async-start(f32[32,64,256]{2,1,0:T(8,128)} %bitcast.6), calls=%async_computation | async-start | bytes 4194304 | tf_op jit(solution)/shard_map/all_to_all | solution.py:75
  21.6 115.1 %all-gather.2.cloned.1.call-start = ((), (), s32[]{:S(2)}) async-start(), calls=%async_computation.2 | async-start | bytes 4718592 | tf_op jit(solution)/shard_map/all_gather | solution.py:102
  72.2 6.7 %collective-permute-start = (f32[2,64,256]{2,1,0:T(8,128)S(1)}, f32[2,64,256]{2,1,0:T(8,128)S(1)}, u32[]{:S(2)}, u32[]{:S(2)}) collective-permute-start(f32[2,64,256]{2,1,0:T(8,128)S(1)} %pad_maximum_fusion), channel_id=1, source_target_pairs={{0,3},{1,0},{2,1},{3,2},{4,7},{5,4},{6,5},{7,6},{8,11},{9,8},{10,9... | collective-permute-start | bytes 393224 | tf_op jit(solution)/shard_map/ppermute | solution.py:99
  76.7 7.3 %collective-permute-start.2 = (f32[2,64,256]{2,1,0:T(8,128)S(1)}, f32[2,64,256]{2,1,0:T(8,128)S(1)}, u32[]{:S(2)}, u32[]{:S(2)}) collective-permute-start(f32[2,64,256]{2,1,0:T(8,128)S(1)} %pad_maximum_fusion), channel_id=1, source_target_pairs={{0,1},{1,2},{2,3},{3,0},{4,5},{5,6},{6,7},{7,4},{8,9},{9,10},{10,1... | collective-permute-start | bytes 393224 | tf_op jit(solution)/shard_map/ppermute | solution.py:99
  76.7 7.2 %collective-permute-start.1 = (f32[2,64,256]{2,1,0:T(8,128)S(1)}, f32[2,64,256]{2,1,0:T(8,128)S(1)}, u32[]{:S(2)}, u32[]{:S(2)}) collective-permute-start(f32[2,64,256]{2,1,0:T(8,128)S(1)} %pad_maximum_fusion), channel_id=1, source_target_pairs={{0,2},{1,3},{2,0},{3,1},{4,6},{5,7},{6,4},{7,5},{8,10},{9,11},{10,... | collective-permute-start | bytes 393224 | tf_op jit(solution)/shard_map/ppermute | solution.py:99
  85.0 22.0 %copy-start.3 = (s32[2,16,1]{1,2,0:T(1,128)S(1)}, s32[2,16,1]{1,2,0:T(1,128)}, u32[]{:S(2)}) copy-start(s32[2,16,1]{1,2,0:T(1,128)} %param.9) | copy-start | bytes 388
  85.0 6.3 %collective-permute-start.3 = (f32[2,64,256]{2,1,0:T(8,128)S(1)}, f32[2,64,256]{2,1,0:T(8,128)S(1)}, u32[]{:S(2)}, u32[]{:S(2)}) collective-permute-start(f32[2,64,256]{2,1,0:T(8,128)S(1)} %pad_maximum_fusion), channel_id=1, source_target_pairs={{0,0},{1,32},{2,64},{3,96},{4,128},{5,160},{6,192},{7,224},{32,1},... | collective-permute-start | bytes 393224 | tf_op jit(solution)/shard_map/ppermute | solution.py:88
  92.4 29.6 %all-to-all-start.1 = ((f32[8,2,64,256]{3,2,1,0:T(8,128)}), f32[8,2,64,256]{3,2,1,0:T(8,128)S(1)}, u32[]{:S(2)}, u32[]{:S(2)}) async-start(f32[8,2,64,256]{3,2,1,0:T(8,128)} %broadcast_in_dim.19), calls=%async_computation.1 | async-start | bytes 2097152 | tf_op jit(solution)/shard_map/all_to_all | solution.py:90
Sparse Core Ops, SparseCore 0:
  85.1 51.5 all-gather.1
